TPU v7x, 32 devices: a whole 2x2x4 slice. The times are simulated.
32 devices in a mesh: seq: 4 (over y, x), exp: 8 (over z, core).
Axes of the slice: x: 2, y: 2, z: 4, core: 2. Of those that a mesh axis runs over, the one named last changes fastest.
Arguments:
- token_ids: int32 [4, 32], replicated, may hold values from 0 to 51199
- cache_lengths: int32 [32], replicated, may hold values from 1 to 1024, as said below
- empty_blocks: int32 [32, 64], replicated, may hold values 0 or 1
- expert_ids: int32 [4, 32, 6], replicated, may hold values from 0 to 63, all different within a row
- embed_table: bfloat16 [51200, 2048], P(('seq', 'exp')), may hold values from -3 to 3
- attn_gain: float32 [2048], replicated, may hold values from 0.5 to 1.5
- w_query: bfloat16 [2048, 2048], P(None, 'seq'), may hold values from -0.125 to 0.125
- w_key: bfloat16 [2048, 2048], P(None, 'seq'), may hold values from -0.125 to 0.125
- w_value: bfloat16 [2048, 2048], P(None, 'seq'), may hold values from -0.125 to 0.125
- w_out: bfloat16 [2048, 2048], P('seq'), may hold values from -0.125 to 0.125
- k_cache: bfloat16 [32, 1024, 2048], P('exp', 'seq'), may hold values from -200 to 200
- v_cache: bfloat16 [32, 1024, 2048], P('exp', 'seq'), may hold values from -6 to 6
- moe_gain: float32 [2048], replicated, may hold values from 0.5 to 1.5
- w_router: bfloat16 [2048, 64], replicated, may hold values from -0.125 to 0.125
- gate_pieces: bfloat16 [256, 2048, 352], P(('seq', 'exp')), may hold values from -0.125 to 0.125
- up_pieces: bfloat16 [256, 2048, 352], P(('seq', 'exp')), may hold values from -0.125 to 0.125
- down_pieces: bfloat16 [256, 352, 2048], P(('seq', 'exp')), may hold values from -0.15625 to 0.15625
- shared_gate: bfloat16 [2048, 2816], P(None, 'exp'), may hold values from -0.125 to 0.125
- shared_up: bfloat16 [2048, 2816], P(None, 'exp'), may hold values from -0.125 to 0.125
- shared_down: bfloat16 [2816, 2048], P('exp'), may hold values from -0.109375 to 0.109375
- final_gain: float32 [2048], replicated, may hold values from 0.5 to 1.5
- w_head: bfloat16 [2048, 51200], P(None, ('seq', 'exp')), may hold values from -0.125 to 0.125
Outputs:
- hidden_norms: float32 [4, 32], replicated
- greatest_logits: float32 [4, 32], replicated
Inputs may be any that keep to these rules, and one draw needn't show every extreme that they name: `cache_lengths`: one of the 32 requests has exactly 1024 cached positions in every draw.
All inputs are finite; a program needn't handle non-finite values.
Results may differ from a plain program's by a relative error of at most 0.0055.
Values may be sent and summed in bfloat16 or wider, within the bound.
No kernel may reach another device: no remote copies, remote signals or barrier semaphores. Data moves between devices by JAX's collectives and lax.ppermute only.
A program may use at most 128 MiB of HBM per device.

v0:
```python
import math

import jax
import jax.numpy as jnp
from jax import lax
from jax.sharding import PartitionSpec as P

HDIM = 128
PIECES = 4
BLK = 16


epsilon = 1e-06
negative = -1e30


def rms_scale(values, scales):
    return values * lax.rsqrt(jnp.mean(values * values, axis=-1, keepdims=True) + epsilon) * scales


def rotate(values, places):
    half_width = values.shape[-1] // 2
    frequency = 10000.0 ** (-2.0 * jnp.arange(half_width, dtype=jnp.float32) / values.shape[-1])
    angles = places.astype(jnp.float32)[..., None, None] * frequency
    cosine_table = jnp.cos(angles)
    sine_table = jnp.sin(angles)
    lower = values[..., :half_width]
    upper = values[..., half_width:]
    return jnp.concatenate(
        [lower * cosine_table - upper * sine_table, upper * cosine_table + lower * sine_table],
        axis=-1,
    )


def joined(earlier, later):
    top_score = jnp.maximum(earlier[0], later[0])
    left_factor = jnp.exp(earlier[0] - top_score)
    right_factor = jnp.exp(later[0] - top_score)
    return (
        top_score,
        earlier[1] * left_factor + later[1] * right_factor,
        earlier[2] * left_factor[..., None] + later[2] * right_factor[..., None],
    )


def on_device(
    token_ids,
    cache_lengths,
    empty_blocks,
    expert_ids,
    embed_table,
    attn_gain,
    w_query,
    w_key,
    w_value,
    w_out,
    k_cache,
    v_cache,
    moe_gain,
    w_router,
    gate_pieces,
    up_pieces,
    down_pieces,
    shared_gate,
    shared_up,
    shared_down,
    final_gain,
    w_head,
):
    steps, requests = token_ids.shape
    tokens = steps * requests
    width = embed_table.shape[1]
    vocab_local = embed_table.shape[0]
    owner_index = lax.axis_index(("seq", "exp"))
    seq_index = lax.axis_index("seq")
    own_count = requests // lax.axis_size("exp")
    own_start = lax.axis_index("exp") * own_count
    local_ids = token_ids.reshape(tokens) - owner_index * vocab_local
    onehot = (local_ids[:, None] == jnp.arange(vocab_local, dtype=jnp.int32)[None, :]).astype(
        jnp.bfloat16
    )
    looked = jnp.dot(onehot, embed_table, preferred_element_type=jnp.float32).reshape(
        steps, requests, width
    )
    block_part = lax.psum_scatter(
        looked.astype(jnp.bfloat16), "exp", scatter_dimension=1, tiled=True
    )
    own_rows = lax.psum(block_part, "seq").astype(jnp.float32).reshape(steps * own_count, width)
    attn_in = rms_scale(own_rows, attn_gain).astype(jnp.bfloat16)
    own_lengths = lax.dynamic_slice_in_dim(cache_lengths, own_start, own_count, 0)
    places = (own_lengths[None, :] + jnp.arange(steps, dtype=jnp.int32)[:, None]).reshape(
        steps * own_count
    )
    heads_here = w_query.shape[1] // HDIM

    def project(weight):
        return jnp.dot(attn_in, weight, preferred_element_type=jnp.float32).reshape(
            steps * own_count, heads_here, HDIM
        )

    query_part = rotate(project(w_query), places).astype(jnp.bfloat16)
    key_part = rotate(project(w_key), places).astype(jnp.bfloat16)
    value_part = project(w_value).astype(jnp.bfloat16)
    queries, new_keys, new_values = (
        lax.all_gather(query_part, "seq", axis=1, tiled=True),
        lax.all_gather(key_part, "seq", axis=1, tiled=True),
        lax.all_gather(value_part, "seq", axis=1, tiled=True),
    )
    head_count = queries.shape[1]
    queries = queries.reshape(steps, own_count, head_count, HDIM)
    new_keys = new_keys.reshape(steps, own_count, head_count, HDIM)
    new_values = new_values.reshape(steps, own_count, head_count, HDIM)
    span = k_cache.shape[1]
    first_place = seq_index * span
    places_here = first_place + jnp.arange(span, dtype=jnp.int32)
    own_empty = lax.dynamic_slice_in_dim(empty_blocks, own_start, own_count, 0)
    local_blocks = lax.dynamic_slice_in_dim(own_empty, first_place // BLK, span // BLK, 1)
    blocked = jnp.broadcast_to(local_blocks[:, :, None], (own_count, span // BLK, BLK)).reshape(
        own_count, span
    )
    live_mask = ((places_here[None, :] < own_lengths[:, None]) & (blocked == 0))[None, :, None, :]
    cache_keys = k_cache.reshape(own_count, span, head_count, HDIM)
    cache_values = v_cache.reshape(own_count, span, head_count, HDIM)
    score_scale = 1.0 / math.sqrt(HDIM)
    cached = (
        jnp.einsum("trhd,rphd->trhp", queries, cache_keys, preferred_element_type=jnp.float32)
        * score_scale
    )
    local_top = jnp.max(jnp.where(live_mask, cached, negative), axis=3)
    top_score = lax.pmax(local_top, "seq")
    local_weights = jnp.where(live_mask, jnp.exp(cached - top_score[..., None]), 0.0)
    local_mixture = jnp.einsum(
        "trhp,rphd->trhd",
        local_weights.astype(jnp.bfloat16),
        cache_values,
        preferred_element_type=jnp.float32,
    )
    totals, mixture = (
        lax.psum(jnp.sum(local_weights, axis=3).astype(jnp.bfloat16), "seq").astype(jnp.float32),
        lax.psum(local_mixture.astype(jnp.bfloat16), "seq").astype(jnp.float32),
    )
    fresh_scores = (
        jnp.einsum("trhd,urhd->trhu", queries, new_keys, preferred_element_type=jnp.float32)
        * score_scale
    )
    causal = (jnp.arange(steps)[None, :] <= jnp.arange(steps)[:, None])[:, None, None, :]
    fresh_top = jnp.max(jnp.where(causal, fresh_scores, negative), axis=3)
    fresh_weights = jnp.where(causal, jnp.exp(fresh_scores - fresh_top[..., None]), 0.0)
    fresh_mixture = jnp.einsum(
        "trhu,urhd->trhd",
        fresh_weights.astype(jnp.bfloat16),
        new_values,
        preferred_element_type=jnp.float32,
    )
    top_score, totals, mixture = joined(
        (top_score, totals, mixture), (fresh_top, jnp.sum(fresh_weights, axis=3), fresh_mixture)
    )
    heads_out = (mixture / totals[..., None]).astype(jnp.bfloat16)
    own_heads = lax.dynamic_slice_in_dim(heads_out, seq_index * heads_here, heads_here, 2).reshape(
        steps * own_count, heads_here * HDIM
    )
    attn_sum = lax.psum(
        jnp.dot(own_heads, w_out, preferred_element_type=jnp.float32).astype(jnp.bfloat16), "seq"
    ).astype(jnp.float32)
    resid_own = own_rows + attn_sum
    resid_all = (
        lax.all_gather(
            resid_own.reshape(steps, own_count, width).astype(jnp.bfloat16),
            "exp",
            axis=1,
            tiled=True,
        )
        .astype(jnp.float32)
        .reshape(tokens, width)
    )
    moe_in = rms_scale(resid_all, moe_gain).astype(jnp.bfloat16)
    router = jax.nn.sigmoid(jnp.dot(moe_in, w_router, preferred_element_type=jnp.float32))
    expert_count = w_router.shape[1]
    chosen_ids = expert_ids.reshape(tokens, expert_ids.shape[2])
    picked = chosen_ids[:, :, None] == jnp.arange(expert_count, dtype=jnp.int32)[None, None, :]
    chosen = jnp.sum(jnp.where(picked, router[:, None, :], 0.0), axis=2)
    gate_weights = chosen / jnp.sum(chosen, axis=1, keepdims=True)
    rows_here = gate_pieces.shape[0]
    row_expert = (owner_index * rows_here + jnp.arange(rows_here, dtype=jnp.int32)) // PIECES
    token_weight = jnp.sum(
        jnp.where(
            chosen_ids[None, :, :] == row_expert[:, None, None], gate_weights[None, :, :], 0.0
        ),
        axis=2,
    )
    gate_out = jnp.einsum("nd,jdf->jnf", moe_in, gate_pieces, preferred_element_type=jnp.float32)
    up_out = jnp.einsum("nd,jdf->jnf", moe_in, up_pieces, preferred_element_type=jnp.float32)
    expert_hidden = (jax.nn.silu(gate_out) * up_out).astype(jnp.bfloat16)
    expert_out = jnp.einsum(
        "jnf,jfd->jnd", expert_hidden, down_pieces, preferred_element_type=jnp.float32
    )
    routed = jnp.einsum("jn,jnd->nd", token_weight, expert_out)
    share_count = tokens // lax.axis_size("seq")
    share_start = seq_index * share_count
    share_rows = lax.dynamic_slice_in_dim(moe_in, share_start, share_count, 0)
    shared_hidden = (
        jax.nn.silu(jnp.dot(share_rows, shared_gate, preferred_element_type=jnp.float32))
        * jnp.dot(share_rows, shared_up, preferred_element_type=jnp.float32)
    ).astype(jnp.bfloat16)
    shared_out = jnp.dot(shared_hidden, shared_down, preferred_element_type=jnp.float32)
    term_rows = lax.dynamic_update_slice_in_dim(
        routed,
        lax.dynamic_slice_in_dim(routed, share_start, share_count, 0) + shared_out,
        share_start,
        0,
    )
    final_hidden = resid_all + lax.psum(term_rows, ("seq", "exp"))
    hidden_norms = jnp.sqrt(jnp.mean(final_hidden * final_hidden, axis=-1)).reshape(steps, requests)
    head_in = rms_scale(final_hidden, final_gain).astype(jnp.bfloat16)
    local_best = jnp.max(jnp.dot(head_in, w_head, preferred_element_type=jnp.float32), axis=-1)
    greatest_logits = lax.pmax(local_best, ("seq", "exp")).reshape(steps, requests)
    return (hidden_norms, greatest_logits)


def solution(mesh):
    in_specs = (
        P(),
        P(),
        P(),
        P(),
        P(("seq", "exp"), None),
        P(),
        P(None, "seq"),
        P(None, "seq"),
        P(None, "seq"),
        P("seq", None),
        P("exp", "seq", None),
        P("exp", "seq", None),
        P(),
        P(),
        P(("seq", "exp"), None, None),
        P(("seq", "exp"), None, None),
        P(("seq", "exp"), None, None),
        P(None, "exp"),
        P(None, "exp"),
        P("exp", None),
        P(),
        P(None, ("seq", "exp")),
    )
    out_specs = (P(), P())
    return jax.shard_map(
        on_device, mesh=mesh, in_specs=in_specs, out_specs=out_specs, check_vma=False
    )
```

profile of v0, /device:TPU:0, one launch (start us, length us, event | category | flops | bytes accessed | tf_op | source)
XLA Modules:
  0.0 482.6 jit_solution(16864006460640909355)
XLA Ops:
  8.1 4.9 %convolution_convert_fusion = bf16[128,2048]{1,0:T(8,128)(2,1)} fusion(bf16[1600,2048]{1,0:T(8,128)(2,1)} %param.26, s32[128]{0:T(128)S(1)} %sub.51), kind=kOutput, calls=%fused_computation.8 | convolution fusion | flops 839327744 | bytes 7078400 | tf_op jit(solution)/shard_map/dot_general | solution.py:82
  14.3 4.0 copy.184
  18.2 3.9 copy.185
  22.3 4.0 copy.188
  27.7 44.3 %all-reduce.15.cloned.1.call-done = bf16[4,32,2048]{2,1,0:T(8,128)(2,1)} async-done(((bf16[4,32,2048]{2,1,0:T(8,128)(2,1)}), bf16[4,32,2048]{2,1,0:T(8,128)(2,1)}) %all-reduce.15.cloned.1.call-update) | async-done | bytes 524304
  73.7 42.0 %all-reduce.7.cloned.1.call-done = bf16[4,4,2048]{2,1,0:T(4,128)(2,1)} async-done(((bf16[4,4,2048]{2,1,0:T(4,128)(2,1)}), bf16[4,4,2048]{2,1,0:T(4,128)(2,1)}) %all-reduce.7.cloned.1.call-update) | async-done | bytes 65552 | tf_op jit(solution)/shard_map/psum | solution.py:88
  117.6 2.4 fusion.78
  120.8 8.2 %all_gather.12 = bf16[16,16,128]{2,0,1:T(8,128)(2,1)S(1)} all-gather(bf16[16,4,128]{2,0,1:T(8,128)(2,1)S(1)} %pad_maximum_fusion), channel_id=1, replica_groups=mesh['seq'=4,'exp'=8] {'seq'}, dimensions={1}, use_global_device_ids=true | all-gather | bytes 81920 | tf_op jit(solution)/shard_map/all_gather | solution.py:105
  129.1 7.3 %all_gather.13 = bf16[16,16,128]{2,0,1:T(8,128)(2,1)S(1)} all-gather(bf16[16,4,128]{2,0,1:T(8,128)(2,1)S(1)} %pad_maximum_fusion.1), channel_id=1, replica_groups=mesh['seq'=4,'exp'=8] {'seq'}, dimensions={1}, use_global_device_ids=true | all-gather | bytes 81920 | tf_op jit(solution)/shard_map/all_gather | solution.py:106
  137.1 3.5 select_reduce_fusion
  140.6 15.4 %pmax.14 = f32[4,4,16]{0,2,1:T(8,128)S(1)} all-reduce(f32[4,4,16]{0,2,1:T(8,128)S(1)} %get-tuple-element.21), channel_id=1, replica_groups=mesh['seq'=4,'exp'=8] {'seq'}, use_global_device_ids=true, to_apply=%region_4.5 | all-reduce | flops 256 | bytes 2048 | tf_op jit(solution)/shard_map/pmax | solution.py:130
  156.2 3.5 fusion.21
  159.8 14.9 %psum.37 = bf16[4,4,16]{0,2,1:T(8,128)(2,1)S(1)} all-reduce(bf16[4,4,16]{0,2,1:T(8,128)(2,1)S(1)} %fusion.37), channel_id=1, replica_groups=mesh['seq'=4,'exp'=8] {'seq'}, use_global_device_ids=true, to_apply=%region_8.9 | all-reduce | flops 256 | bytes 1024 | tf_op jit(solution)/shard_map/psum | solution.py:139
  177.3 7.4 %all_gather.14 = bf16[16,16,128]{2,0,1:T(8,128)(2,1)S(1)} all-gather(bf16[16,4,128]{2,0,1:T(8,128)(2,1)S(1)} %convolution_convert_fusion.2), channel_id=1, replica_groups=mesh['seq'=4,'exp'=8] {'seq'}, dimensions={1}, use_global_device_ids=true | all-gather | bytes 81920 | tf_op jit(solution)/shard_map/all_gather | solution.py:107
  185.1 16.3 %all-reduce.9.cloned.1.call-done = bf16[4,4,16,128]{3,0,2,1:T(4,128)(2,1)} async-done(((bf16[4,4,16,128]{3,0,2,1:T(4,128)(2,1)}), bf16[4,4,16,128]{3,0,2,1:T(4,128)(2,1)}) %all-reduce.9.cloned.1.call-update) | async-done | bytes 65552 | tf_op jit(solution)/shard_map/psum | solution.py:140
  203.4 42.5 %all-reduce.11.cloned.1.call-done = bf16[16,2048]{1,0:T(8,128)(2,1)} async-done(((bf16[16,2048]{1,0:T(8,128)(2,1)}), bf16[16,2048]{1,0:T(8,128)(2,1)}) %all-reduce.11.cloned.1.call-update) | async-done | bytes 65552 | tf_op jit(solution)/shard_map/psum | solution.py:162
  246.8 14.7 %all_gather.15 = bf16[4,32,2048]{2,0,1:T(4,128)(2,1)S(1)} all-gather(bf16[4,4,2048]{2,0,1:T(4,128)(2,1)S(1)} %copy.178), channel_id=1, replica_groups=mesh['seq'=4,'exp'=8] {'exp'}, dimensions={1}, use_global_device_ids=true | all-gather | bytes 589824 | tf_op jit(solution)/shard_map/all_gather | solution.py:167
  262.6 6.3 %convolution_bitcast_fusion.1 = f32[8,128,352]{1,2,0:T(8,128)S(1)} fusion(bf16[8,2048,352]{1,2,0:T(8,128)(2,1)} %param.36, bf16[128,2048]{1,0:T(8,128)(2,1)S(1)} %fusion.29), kind=kOutput, calls=%fused_computation.13 | convolution fusion | flops 1476395008 | bytes 13500416 | tf_op jit(solution)/shard_map/nd,jdf->jnf/dot_general | solution.py:191
  269.5 18.6 %fusion.11 = bf16[8,128,2048]{2,1,0:T(8,128)(2,1)} fusion(bf16[8,352,2048]{2,1,0:T(8,128)(2,1)} %param.38, bf16[8,2048,352]{1,2,0:T(8,128)(2,1)} %param.37, f32[8,128,352]{1,2,0:T(8,128)S(1)} %convolution_bitcast_fusion.1, bf16[128,2048]{1,0:T(8,128)(2,1)S(1)} %fusion.29), kind=kOutput, calls=%fused_computation.16 | convolution fusion | flops 2954952704 | bytes 29229056 | tf_op jit(solution)/shard_map/jnf,jfd->jnd/dot_general | solution.py:194
  288.1 5.3 %fusion = f32[128,1,2048]{2,1,0:T(1,128)S(1)} fusion(bf16[8,128,1]{0,2,1:T(2,128)(2,1)S(1)} %copy.181, bf16[8,128,2048]{2,1,0:T(8,128)(2,1)} %fusion.11), kind=kOutput, calls=%fused_computation | convolution fusion | flops 4194304 | bytes 5244928 | tf_op jit(solution)/shard_map/jn,jnd->nd/dot_general | solution.py:197
  295.3 3.1 fusion.8
  299.5 130.2 %all-reduce.13.cloned.1.call-done = f32[128,2048]{1,0:T(8,128)} async-done(((f32[128,2048]{1,0:T(8,128)}), f32[128,2048]{1,0:T(8,128)}) %all-reduce.13.cloned.1.call-update) | async-done | bytes 1048592 | tf_op jit(solution)/shard_map/psum | solution.py:212
  431.2 5.0 %convolution_reduce_fusion = f32[128]{0:T(128)S(1)} fusion(bf16[2048,1600]{0,1:T(8,128)(2,1)} %param.43, f32[128,2048]{1,0:T(8,128)S(1)} %get-tuple-element.7, f32[2048]{0:T(1024)S(1)} %copy-done.7, f32[128]{0:T(128)S(1)} %get-tuple-element.19), kind=kOutput, calls=%fused_computation.17 | convolution fusion | flops 839851904 | bytes 7611392 | tf_op jit(solution)/shard_map/dot_general | solution.py:215
  436.3 39.1 %pmax.15 = f32[4,32]{1,0:T(4,128)} all-reduce(f32[4,32]{1,0:T(4,128)S(1)} %reshape.303), channel_id=1, replica_groups=mesh['seq'=4,'exp'=8] {'seq','exp'}, use_global_device_ids=true, to_apply=%region_18.19 | all-reduce | flops 128 | bytes 1024 | tf_op jit(solution)/shard_map/pmax | solution.py:216
  (99 shorter events, 21.0 us)
Async XLA Ops:
  7.2 195.1 %copy-start = (bf16[512,2048]{1,0:T(8,128)(2,1)S(1)}, bf16[512,2048]{1,0:T(8,128)(2,1)}, u32[]{:S(2)}) copy-start(bf16[512,2048]{1,0:T(8,128)(2,1)} %param.31) | copy-start | bytes 6291460
  7.2 64.8 %all-reduce.15.cloned.1.call-start = ((), (), s32[]{:S(2)}) async-start(), calls=%async_computation.4 | async-start | bytes 1048576
  8.1 5.9 %copy-start.11 = (s32[32]{0:T(128)S(1)}, s32[32]{0:T(128)}, u32[]{:S(2)}) copy-start(s32[32]{0:T(128)} %param.23) | copy-start | bytes 388
  13.0 102.6 %all-reduce.7.cloned.1.call-start = ((), (), s32[]{:S(2)}) async-start(), calls=%async_computation | async-start | bytes 131072 | tf_op jit(solution)/shard_map/psum | solution.py:88
  22.3 4.0 copy-start.8
  22.3 4.1 copy-start.12
  22.3 94.3 %copy-start.10 = (f32[2048]{0:T(1024)S(1)}, f32[2048]{0:T(1024)}, u32[]{:S(2)}) copy-start(f32[2048]{0:T(1024)} %param.27) | copy-start | bytes 24580
  73.6 127.8 %all-reduce.9.cloned.1.call-start = ((), (), s32[]{:S(2)}) async-start(), calls=%async_computation.1 | async-start | bytes 131072 | tf_op jit(solution)/shard_map/psum | solution.py:140
  117.6 2.4 copy-start.2
  159.8 86.1 %all-reduce.11.cloned.1.call-start = ((), (), s32[]{:S(2)}) async-start(), calls=%async_computation.2 | async-start | bytes 131072 | tf_op jit(solution)/shard_map/psum | solution.py:162
  175.1 28.3 %copy-start.5 = (bf16[4,4,2048]{2,1,0:T(4,128)(2,1)S(1)}, bf16[4,4,2048]{2,1,0:T(4,128)(2,1)}, u32[]{:S(2)}) copy-start(bf16[4,4,2048]{2,1,0:T(4,128)(2,1)} %all-reduce.7.cloned.1.call-done) | copy-start | bytes 196612
  203.2 59.1 %copy-start.9 = (f32[2048]{0:T(1024)S(1)}, f32[2048]{0:T(1024)}, u32[]{:S(2)}) copy-start(f32[2048]{0:T(1024)} %param.34) | copy-start | bytes 24580
  203.3 226.5 %all-reduce.13.cloned.1.call-start = ((), (), s32[]{:S(2)}) async-start(), calls=%async_computation.3 | async-start | bytes 2097152 | tf_op jit(solution)/shard_map/psum | solution.py:212
  262.6 6.3 %copy-start.6 = (bf16[2048,64]{0,1:T(8,128)(2,1)S(1)}, bf16[2048,64]{0,1:T(8,128)(2,1)}, u32[]{:S(2)}) copy-start(bf16[2048,64]{0,1:T(8,128)(2,1)} %param.35) | copy-start | bytes 786436
  293.4 1.4 copy-start.4
  298.4 1.0 copy-start.3
  298.5 132.7 %copy-start.7 = (f32[2048]{0:T(1024)S(1)}, f32[2048]{0:T(1024)}, u32[]{:S(2)}) copy-start(f32[2048]{0:T(1024)} %param.42) | copy-start | bytes 24580
  431.2 44.9 %copy-start.1 = (bf16[512,2048]{1,0:T(8,128)(2,1)S(1)}, bf16[512,2048]{1,0:T(8,128)(2,1)}, u32[]{:S(2)}) copy-start(bf16[512,2048]{1,0:T(8,128)(2,1)} %param.31) | copy-start | bytes 6291460
Sparse Core Ops, SparseCore 0:
  13.1 58.8 all-reduce.14
  75.1 40.4 all-reduce.6
  159.9 41.4 all-reduce.8
  204.3 41.4 all-reduce.10
  299.6 130.0 all-reduce.12
where the time goes:
time: 484 us; the launch traced here: 483 us
  waiting for transfers between devices  275 us (57%)
  blocking collectives  107 us (22%)
  matrix products  57.7 us (12%)
  local copies, waits for them, and re-layouts  19.1 us (4%)
  between operations  14.8 us (3%)
  other arithmetic  8.37 us (2%)
    psum x1, waiting for transfers between devices, on_device(): final_hidden = resid_all + lax.psum(term_rows, ('seq', 'exp'))  130 us
    unnamed x6, waiting for transfers between devices  44.4 us
    psum x1, waiting for transfers between devices, on_device(): lax.psum(jnp.dot(own_heads, w_out, preferred_element_type=jnp.float32).as...  42.5 us
    psum x1, waiting for transfers between devices, on_device(): lax.psum(block_part, 'seq').astype(jnp.float32)  42 us
    pmax x1, blocking collectives, on_device(): lax.pmax(local_best, ('seq', 'exp')).reshape(steps, requests)  39.1 us
    dot_general x1, matrix products, on_device(): jnp.einsum('jnf,jfd->jnd', expert_hidden, down_pieces, preferred_element_...  18.6 us
    psum x1, waiting for transfers between devices, on_device(): lax.psum(local_mixture.astype(jnp.bfloat16), 'seq').astype(jnp.float32)  16.3 us
    pmax x1, blocking collectives, on_device(): top_score = lax.pmax(local_top, 'seq')  15.4 us
  transfers between devices with their start and end apart: 5, of which 5 were waited for; matrix products, arithmetic and copies ran while one was open for 3% of the time, Pallas kernels for 0%

commit v1 on v0

v1 whole, which is shorter than its diff:
```python
import math

import jax
import jax.numpy as jnp
from jax import lax
from jax.sharding import PartitionSpec as P

HDIM = 128
PIECES = 4
BLK = 16


epsilon = 1e-06
negative = -1e30


def rms_scale(values, scales):
    return values * lax.rsqrt(jnp.mean(values * values, axis=-1, keepdims=True) + epsilon) * scales


def rotate(values, places):
    half_width = values.shape[-1] // 2
    frequency = 10000.0 ** (-2.0 * jnp.arange(half_width, dtype=jnp.float32) / values.shape[-1])
    angles = places.astype(jnp.float32)[..., None, None] * frequency
    cosine_table = jnp.cos(angles)
    sine_table = jnp.sin(angles)
    lower = values[..., :half_width]
    upper = values[..., half_width:]
    return jnp.concatenate(
        [lower * cosine_table - upper * sine_table, upper * cosine_table + lower * sine_table],
        axis=-1,
    )


def gather_all(values):
    inner = lax.all_gather(values, "exp", axis=0, tiled=False)
    return lax.all_gather(inner, "seq", axis=0, tiled=False)


def on_device(
    token_ids,
    cache_lengths,
    empty_blocks,
    expert_ids,
    embed_table,
    attn_gain,
    w_query,
    w_key,
    w_value,
    w_out,
    k_cache,
    v_cache,
    moe_gain,
    w_router,
    gate_pieces,
    up_pieces,
    down_pieces,
    shared_gate,
    shared_up,
    shared_down,
    final_gain,
    w_head,
):
    steps, requests = token_ids.shape
    tokens = steps * requests
    width = embed_table.shape[1]
    vocab_local = embed_table.shape[0]
    n_seq = lax.axis_size("seq")
    n_exp = lax.axis_size("exp")
    n_dev = n_seq * n_exp
    owner_index = lax.axis_index(("seq", "exp"))
    seq_index = lax.axis_index("seq")
    own_count = requests // n_exp
    own_start = lax.axis_index("exp") * own_count
    group = steps * own_count
    share = group // n_seq

    def permuted(values):
        rest = values.shape[2:]
        grouped = jnp.moveaxis(values.reshape((steps, n_exp, own_count) + rest), 1, 0)
        split = grouped.reshape((n_exp, n_seq, share) + rest)
        return jnp.swapaxes(split, 0, 1).reshape((tokens,) + rest)

    def natural(values):
        split = jnp.swapaxes(values.reshape(n_seq, n_exp, share), 0, 1)
        grouped = split.reshape(n_exp, steps, own_count)
        return jnp.moveaxis(grouped, 0, 1).reshape(steps, requests)

    local_ids = token_ids - owner_index * vocab_local
    held = (local_ids >= 0) & (local_ids < vocab_local)
    rows = jnp.take(embed_table, jnp.clip(local_ids, 0, vocab_local - 1), axis=0)
    rows = jnp.where(held[..., None], rows, jnp.zeros((), rows.dtype))
    rows = jnp.moveaxis(rows.reshape(steps, n_exp, own_count, width), 1, 0)
    arrived = lax.all_to_all(rows, "exp", 0, 0, tiled=True)
    row_part = jnp.sum(arrived.astype(jnp.float32), axis=0).astype(jnp.bfloat16)
    row_parts = lax.all_gather(row_part, "seq", axis=0, tiled=False)
    embedded = jnp.sum(row_parts.astype(jnp.float32), axis=0).reshape(group, width)

    attn_in = rms_scale(embedded, attn_gain).astype(jnp.bfloat16)
    own_lengths = lax.dynamic_slice_in_dim(cache_lengths, own_start, own_count, 0)
    places = (own_lengths[None, :] + jnp.arange(steps, dtype=jnp.int32)[:, None]).reshape(group)
    heads_here = w_query.shape[1] // HDIM

    def project(weight):
        return jnp.dot(attn_in, weight, preferred_element_type=jnp.float32).reshape(
            group, heads_here, HDIM
        )

    query_part = rotate(project(w_query), places).astype(jnp.bfloat16)
    key_part = rotate(project(w_key), places).astype(jnp.bfloat16)
    value_part = project(w_value).astype(jnp.bfloat16)
    every = lax.all_gather(
        jnp.stack([query_part, key_part, value_part], axis=0), "seq", axis=0, tiled=False
    )
    head_count = n_seq * heads_here
    every = jnp.moveaxis(every, 0, 2).reshape(3, steps, own_count, head_count, HDIM)
    queries = every[0]

    span = k_cache.shape[1]
    first_place = seq_index * span
    places_here = first_place + jnp.arange(span, dtype=jnp.int32)
    own_empty = lax.dynamic_slice_in_dim(empty_blocks, own_start, own_count, 0)
    local_blocks = lax.dynamic_slice_in_dim(own_empty, first_place // BLK, span // BLK, 1)
    blocked = jnp.broadcast_to(local_blocks[:, :, None], (own_count, span // BLK, BLK)).reshape(
        own_count, span
    )
    live_mask = ((places_here[None, :] < own_lengths[:, None]) & (blocked == 0))[None, :, None, :]
    cache_keys = k_cache.reshape(own_count, span, head_count, HDIM)
    cache_values = v_cache.reshape(own_count, span, head_count, HDIM)
    score_scale = 1.0 / math.sqrt(HDIM)
    cached = (
        jnp.einsum("trhd,rphd->trhp", queries, cache_keys, preferred_element_type=jnp.float32)
        * score_scale
    )
    local_top = jnp.max(jnp.where(live_mask, cached, negative), axis=3)
    local_weights = jnp.where(live_mask, jnp.exp(cached - local_top[..., None]), 0.0)
    local_totals = jnp.sum(local_weights, axis=3)
    local_mixture = jnp.einsum(
        "trhp,rphd->trhd",
        local_weights.astype(jnp.bfloat16),
        cache_values,
        preferred_element_type=jnp.float32,
    )

    def by_owner(values):
        rest = values.shape[3:]
        split = values.reshape((steps, own_count, n_seq, heads_here) + rest)
        return jnp.moveaxis(split, 2, 0).reshape(n_seq, -1)

    mix_len = group * heads_here * HDIM
    stat_len = group * heads_here
    packed = jnp.concatenate(
        [by_owner(local_mixture), by_owner(local_top), by_owner(local_totals)], axis=1
    )
    got = lax.all_to_all(packed, "seq", 0, 0, tiled=True)
    got_mixture = got[:, :mix_len].reshape(n_seq, steps, own_count, heads_here, HDIM)
    got_top = got[:, mix_len : mix_len + stat_len].reshape(n_seq, steps, own_count, heads_here)
    got_totals = got[:, mix_len + stat_len :].reshape(n_seq, steps, own_count, heads_here)

    own_queries = query_part.reshape(steps, own_count, heads_here, HDIM)
    own_keys = key_part.reshape(steps, own_count, heads_here, HDIM)
    own_values = value_part.reshape(steps, own_count, heads_here, HDIM)
    fresh_scores = (
        jnp.einsum("trhd,urhd->trhu", own_queries, own_keys, preferred_element_type=jnp.float32)
        * score_scale
    )
    causal = (jnp.arange(steps)[None, :] <= jnp.arange(steps)[:, None])[:, None, None, :]
    fresh_top = jnp.max(jnp.where(causal, fresh_scores, negative), axis=3)
    fresh_weights = jnp.where(causal, jnp.exp(fresh_scores - fresh_top[..., None]), 0.0)
    fresh_mixture = jnp.einsum(
        "trhu,urhd->trhd",
        fresh_weights.astype(jnp.bfloat16),
        own_values,
        preferred_element_type=jnp.float32,
    )
    top_score = jnp.maximum(jnp.max(got_top, axis=0), fresh_top)
    cache_factor = jnp.exp(got_top - top_score[None])
    fresh_factor = jnp.exp(fresh_top - top_score)
    totals = jnp.sum(got_totals * cache_factor, axis=0) + jnp.sum(fresh_weights, axis=3) * fresh_factor
    mixture = (
        jnp.sum(got_mixture * cache_factor[..., None], axis=0)
        + fresh_mixture * fresh_factor[..., None]
    )
    own_heads = (mixture / totals[..., None]).astype(jnp.bfloat16).reshape(
        group, heads_here * HDIM
    )

    attn_part = jnp.dot(own_heads, w_out, preferred_element_type=jnp.float32)
    attn_sum = jnp.sum(
        lax.all_to_all(attn_part.reshape(n_seq, share, width), "seq", 0, 0, tiled=True), axis=0
    )
    resid_share = lax.dynamic_slice_in_dim(embedded, seq_index * share, share, 0) + attn_sum
    moe_in = gather_all(rms_scale(resid_share, moe_gain).astype(jnp.bfloat16)).reshape(
        tokens, width
    )

    router = jax.nn.sigmoid(jnp.dot(moe_in, w_router, preferred_element_type=jnp.float32))
    expert_count = w_router.shape[1]
    chosen_ids = permuted(expert_ids)
    picked = chosen_ids[:, :, None] == jnp.arange(expert_count, dtype=jnp.int32)[None, None, :]
    chosen = jnp.sum(jnp.where(picked, router[:, None, :], 0.0), axis=2)
    gate_weights = chosen / jnp.sum(chosen, axis=1, keepdims=True)
    rows_here = gate_pieces.shape[0]
    row_expert = (owner_index * rows_here + jnp.arange(rows_here, dtype=jnp.int32)) // PIECES
    token_weight = jnp.sum(
        jnp.where(
            chosen_ids[None, :, :] == row_expert[:, None, None], gate_weights[None, :, :], 0.0
        ),
        axis=2,
    )
    gate_out = jnp.einsum("nd,jdf->jnf", moe_in, gate_pieces, preferred_element_type=jnp.float32)
    up_out = jnp.einsum("nd,jdf->jnf", moe_in, up_pieces, preferred_element_type=jnp.float32)
    expert_hidden = (jax.nn.silu(gate_out) * up_out).astype(jnp.bfloat16)
    expert_out = jnp.einsum(
        "jnf,jfd->jnd", expert_hidden, down_pieces, preferred_element_type=jnp.float32
    )
    routed = jnp.einsum("jn,jnd->nd", token_weight, expert_out)
    share_count = tokens // n_seq
    share_start = seq_index * share_count
    share_rows = lax.dynamic_slice_in_dim(moe_in, share_start, share_count, 0)
    shared_hidden = (
        jax.nn.silu(jnp.dot(share_rows, shared_gate, preferred_element_type=jnp.float32))
        * jnp.dot(share_rows, shared_up, preferred_element_type=jnp.float32)
    ).astype(jnp.bfloat16)
    shared_out = jnp.dot(shared_hidden, shared_down, preferred_element_type=jnp.float32)
    term_rows = lax.dynamic_update_slice_in_dim(
        routed,
        lax.dynamic_slice_in_dim(routed, share_start, share_count, 0) + shared_out,
        share_start,
        0,
    )

    term_sum = jnp.sum(
        lax.all_to_all(term_rows.reshape(n_dev, share, width), ("seq", "exp"), 0, 0, tiled=True),
        axis=0,
    )
    final_share = resid_share + term_sum
    norms_share = jnp.sqrt(jnp.mean(final_share * final_share, axis=-1))
    head_in = gather_all(rms_scale(final_share, final_gain).astype(jnp.bfloat16)).reshape(
        tokens, width
    )
    local_best = jnp.max(jnp.dot(head_in, w_head, preferred_element_type=jnp.float32), axis=-1)
    message = jnp.concatenate([local_best, norms_share], axis=0)
    heard = lax.all_to_all(
        jnp.broadcast_to(message[None, :], (n_dev, message.shape[0])),
        ("seq", "exp"),
        0,
        0,
        tiled=True,
    )
    greatest_logits = natural(jnp.max(heard[:, :tokens], axis=0))
    hidden_norms = natural(heard[:, tokens:].reshape(tokens))
    return (hidden_norms, greatest_logits)


def solution(mesh):
    in_specs = (
        P(),
        P(),
        P(),
        P(),
        P(("seq", "exp"), None),
        P(),
        P(None, "seq"),
        P(None, "seq"),
        P(None, "seq"),
        P("seq", None),
        P("exp", "seq", None),
        P("exp", "seq", None),
        P(),
        P(),
        P(("seq", "exp"), None, None),
        P(("seq", "exp"), None, None),
        P(("seq", "exp"), None, None),
        P(None, "exp"),
        P(None, "exp"),
        P("exp", None),
        P(),
        P(None, ("seq", "exp")),
    )
    out_specs = (P(), P())
    return jax.shard_map(
        on_device, mesh=mesh, in_specs=in_specs, out_specs=out_specs, check_vma=False
    )
```

time: 484 us -> 214 us (0.44)
  waiting for transfers between devices: 275 us -> 11.9 us
  between operations: 14.8 us -> 1.1 us
  starting transfers between devices: 0.21 us -> 13.1 us
  matrix products: 57.7 us -> 52.2 us
  local copies, waits for them, and re-layouts: 19.1 us -> 24.4 us
    psum x4 -> x0, waiting for transfers between devices: 231 us -> none  [the longest x1 130 us: on_device(): final_hidden = resid_all + lax.psum(term_rows, ('seq', 'exp'))]
    pmax x2 -> x0, blocking collectives: 54.5 us -> none  [the longest x1 39.1 us: on_device(): lax.pmax(local_best, ('seq', 'exp')).reshape(steps, requests)]
    unnamed x6 -> x0, waiting for transfers between devices: 44.4 us -> none
    all_to_all x0 -> x2, blocking collectives: none -> 39.7 us  [the longest x1 30.4 us: on_device(): lax.all_to_all(term_rows.reshape(n_dev, share, width), ('seq', 'exp'), 0,...]
    all_gather x4 -> x6, blocking collectives: 37.6 us -> 64.9 us  [the longest x2 27.9 us: gather_all(): inner = lax.all_gather(values, 'exp', axis=0, tiled=False)]
    psum x1 -> x0, blocking collectives: 14.9 us -> none  [on_device(): lax.psum(jnp.sum(local_weights, axis=3).astype(jnp.bfloat16), 'seq')]
    all_to_all x0 -> x3, starting transfers between devices: none -> 13.1 us  [the longest x1 6.33 us: on_device(): arrived = lax.all_to_all(rows, 'exp', 0, 0, tiled=True)]
    all_to_all x0 -> x3, waiting for transfers between devices: none -> 11.9 us  [the longest x1 4.95 us: on_device(): got = lax.all_to_all(packed, 'seq', 0, 0, tiled=True)]
  transfers between devices with their start and end apart: 5 -> 3, of which waited for: 5 -> 3; matrix products, arithmetic and copies ran while one was open for 3% -> 6% of each run, Pallas kernels for 0% -> 0%
where the time goes in v1:
time: 214 us; the launch traced here: 213 us
  blocking collectives  105 us (49%)
  matrix products  52.2 us (24%)
  local copies, waits for them, and re-layouts  24.4 us (11%)
  starting transfers between devices  13.1 us (6%)
  waiting for transfers between devices  11.9 us (6%)
  other arithmetic  5.27 us (2%)
    all_to_all x1, blocking collectives, on_device(): lax.all_to_all(term_rows.reshape(n_dev, share, width), ('seq', 'exp'), 0,...  30.4 us
    all_gather x2, blocking collectives, gather_all(): inner = lax.all_gather(values, 'exp', axis=0, tiled=False)  27.9 us
    all_gather x2, blocking collectives, gather_all(): return lax.all_gather(inner, 'seq', axis=0, tiled=False)  19.1 us
    dot_general x1, matrix products, on_device(): jnp.einsum('jnf,jfd->jnd', expert_hidden, down_pieces, preferred_element_...  18.6 us
    dot_general x3, local copies, waits for them, and re-layouts, project(): jnp.dot(attn_in, weight, preferred_element_type=jnp.float32)  11.9 us
    all_to_all x1, blocking collectives, on_device(): lax.all_to_all(jnp.broadcast_to(message[None, :], (n_dev, message.shape[0...  9.33 us
    all_gather x1, blocking collectives, on_device(): row_parts = lax.all_gather(row_part, 'seq', axis=0, tiled=False)  9 us
    all_gather x1, blocking collectives, on_device(): lax.all_gather(jnp.stack([query_part, key_part, value_part], axis=0), 'se...  8.83 us
  transfers between devices with their start and end apart: 3, of which 3 were waited for; matrix products, arithmetic and copies ran while one was open for 6% of the time, Pallas kernels for 0%

profile of v1, /device:TPU:0, one launch (start us, length us, event | category | flops | bytes accessed | tf_op | source)
XLA Modules:
  0.0 212.5 jit_solution(10068466699584656610)
XLA Ops:
  1.6 5.1 %gather_fusion = bf16[128,2048]{1,0:T(8,128)(2,1)S(1)} fusion(bf16[1600,2048]{1,0:T(8,128)(2,1)} %param.26, s32[1024]{0:T(1024)S(1)} %pad_clamp_fusion), kind=kCustom, calls=%fused_computation | custom fusion | bytes 1049088 | tf_op jit(solution)/shard_map/jit(_take)/gather | solution.py:91
  8.4 6.3 %all-to-all-start = ((bf16[8,4,4,2048]{3,2,1,0:T(4,128)(2,1)}), bf16[8,4,4,2048]{3,2,1,0:T(4,128)(2,1)S(1)}, u32[]{:S(2)}, u32[]{:S(2)}) async-start(bf16[8,4,4,2048]{3,2,1,0:T(4,128)(2,1)} %fusion.31), calls=%async_computation | async-start | bytes 1048576 | tf_op jit(solution)/shard_map/all_to_all | solution.py:94
  14.8 4.0 %copy.152 = bf16[512,2048]{1,0:T(8,128)(2,1)} copy(bf16[512,2048]{0,1:T(8,128)(2,1)} %bitcast.138) | data formatting | bytes 4194304 | tf_op jit(solution)/shard_map/dot_general | solution.py:105
  18.8 3.9 %copy.153 = bf16[512,2048]{1,0:T(8,128)(2,1)} copy(bf16[512,2048]{0,1:T(8,128)(2,1)} %bitcast.139) | data formatting | bytes 4194304 | tf_op jit(solution)/shard_map/dot_general | solution.py:105
  22.8 4.0 %copy.154 = bf16[512,2048]{1,0:T(8,128)(2,1)} copy(bf16[512,2048]{0,1:T(8,128)(2,1)} %bitcast.140) | data formatting | bytes 4194304 | tf_op jit(solution)/shard_map/dot_general | solution.py:105
  30.3 9.0 %all-gather = bf16[16,4,2048]{2,1,0:T(4,128)(2,1)S(1)} all-gather(bf16[4,4,2048]{2,1,0:T(4,128)(2,1)S(1)} %reduce_sum.137), channel_id=2, replica_groups=mesh['seq'=4,'exp'=8] {'seq'}, dimensions={0}, use_global_device_ids=true | all-gather | bytes 327680 | tf_op jit(solution)/shard_map/all_gather | solution.py:96
  45.7 8.8 %all-gather.1 = bf16[12,16,4,128]{3,1,2,0:T(8,128)(2,1)S(1)} all-gather(bf16[3,16,4,128]{3,1,2,0:T(8,128)(2,1)S(1)} %pad_maximum_fusion), channel_id=3, replica_groups=mesh['seq'=4,'exp'=8] {'seq'}, dimensions={0}, use_global_device_ids=true | all-gather | bytes 245760 | tf_op jit(solution)/shard_map/all_gather | solution.py:112
  54.7 3.5 %select_reduce_fusion = (f32[4,4,16]{0,2,1:T(8,128)S(1)}, f32[4,4,16,256]{3,0,2,1:T(4,128)S(1)}) fusion(pred[4,256]{1,0:T(4,128)(4,1)S(1)} %compare_and_fusion, bf16[4,4,16,128]{3,2,1,0:T(8,128)(2,1)S(1)} %bitcast.167, bf16[4,256,2048]{2,1,0:T(8,128)(2,1)} %param.32), kind=kOutput, calls=%fused_computation.42 | convolution fusion | flops 16973568 | bytes 4524032 | tf_op jit(solution)/shard_map/trhd,rphd->trhp/dot_general | solution.py:132
  58.7 2.9 %fusion.2 = f32[4,16,4,128]{3,2,1,0:T(4,128)S(1)} fusion(f32[4,4,16,256]{3,0,2,1:T(4,128)S(1)} %get-tuple-element.27, f32[4,4,16]{0,2,1:T(8,128)S(1)} %get-tuple-element.26, pred[4,256]{1,0:T(4,128)(4,1)S(1)} %compare_and_fusion, bf16[4,256,2048]{2,1,0:T(8,128)(2,1)} %param.33), kind=kOutput, calls=%fused_computation.3 | convolution fusion | flops 16973824 | bytes 4589568 | tf_op jit(solution)/shard_map/trhp,rphd->trhd/dot_general | solution.py:138
  63.0 3.3 %all-to-all-start.1 = ((f32[4,1,8320]{2,1,0:T(1,128)}), f32[4,1,8320]{2,1,0:T(1,128)S(1)}, u32[]{:S(2)}, u32[]{:S(2)}) async-start(f32[4,1,8320]{2,1,0:T(1,128)} %copy.135), calls=%async_computation.1 | async-start | bytes 266240 | tf_op jit(solution)/shard_map/all_to_all | solution.py:155
  66.4 4.9 %all-to-all-done.1 = f32[4,1,8320]{2,1,0:T(1,128)S(1)} async-done(((f32[4,1,8320]{2,1,0:T(1,128)}), f32[4,1,8320]{2,1,0:T(1,128)S(1)}, u32[]{:S(2)}, u32[]{:S(2)}) %all-to-all-start.1) | async-done | bytes 133152 | tf_op jit(solution)/shard_map/all_to_all | solution.py:155
  73.8 3.5 %all-to-all-start.2 = ((f32[4,4,2048]{2,1,0:T(4,128)}), f32[4,4,2048]{2,1,0:T(4,128)S(1)}, u32[]{:S(2)}, u32[]{:S(2)}) async-start(f32[4,4,2048]{2,1,0:T(4,128)} %fusion.9), calls=%async_computation.2 | async-start | bytes 262144 | tf_op jit(solution)/shard_map/all_to_all | solution.py:190
  77.4 4.9 %all-to-all-done.2 = f32[4,4,2048]{2,1,0:T(4,128)S(1)} async-done(((f32[4,4,2048]{2,1,0:T(4,128)}), f32[4,4,2048]{2,1,0:T(4,128)S(1)}, u32[]{:S(2)}, u32[]{:S(2)}) %all-to-all-start.2) | async-done | bytes 131104 | tf_op jit(solution)/shard_map/all_to_all | solution.py:190
  82.5 14.0 %all-gather.6 = bf16[8,4,2048]{2,1,0:T(4,128)(2,1)S(1)} all-gather(bf16[1,4,2048]{2,1,0:T(4,128)(2,1)S(1)} %fusion.53), channel_id=4, replica_groups=mesh['seq'=4,'exp'=8] {'exp'}, dimensions={0}, use_global_device_ids=true | all-gather | bytes 147456 | tf_op jit(solution)/shard_map/all_gather | solution.py:36
  96.5 9.8 %all-gather.3 = bf16[32,4,2048]{2,1,0:T(4,128)(2,1)S(1)} all-gather(bf16[8,4,2048]{2,1,0:T(4,128)(2,1)S(1)} %all-gather.6), channel_id=5, replica_groups=mesh['seq'=4,'exp'=8] {'seq'}, dimensions={0}, use_global_device_ids=true | all-gather | bytes 655360 | tf_op jit(solution)/shard_map/all_gather | solution.py:37
  107.1 6.2 %convolution_bitcast_fusion.1 = f32[8,128,352]{1,2,0:T(8,128)S(1)} fusion(bf16[128,2048,1]{1,0,2:T(8,128)(2,1)S(1)} %reshape.566, bf16[8,2048,352]{1,2,0:T(8,128)(2,1)} %param.36), kind=kOutput, calls=%fused_computation.14 | convolution fusion | flops 1476395008 | bytes 13500416 | tf_op jit(solution)/shard_map/nd,jdf->jnf/dot_general | solution.py:211
  113.4 18.6 %fusion.13 = bf16[8,128,2048]{2,1,0:T(8,128)(2,1)} fusion(bf16[8,352,2048]{2,1,0:T(8,128)(2,1)} %param.38, bf16[128,2048,1]{1,0,2:T(8,128)(2,1)S(1)} %reshape.566, bf16[8,2048,352]{1,2,0:T(8,128)(2,1)} %param.37, f32[8,128,352]{1,2,0:T(8,128)S(1)} %convolution_bitcast_fusion.1), kind=kOutput, calls=%fused_computation.17 | convolution fusion | flops 2954952704 | bytes 29229056 | tf_op jit(solution)/shard_map/jnf,jfd->jnd/dot_general | solution.py:214
  132.0 5.3 %fusion = f32[128,1,2048]{2,1,0:T(1,128)S(1)} fusion(bf16[8,128,1]{0,2,1:T(2,128)(2,1)S(1)} %copy.149, bf16[8,128,2048]{2,1,0:T(8,128)(2,1)} %fusion.13), kind=kOutput, calls=%fused_computation.1 | convolution fusion | flops 4194304 | bytes 5244928 | tf_op jit(solution)/shard_map/jn,jnd->nd/dot_general | solution.py:217
  139.2 3.2 %fusion.8 = f32[128,2048]{1,0:T(8,128)S(1)} fusion(f32[128,2048]{1,0:T(8,128)S(1)} %bitcast.137, s32[]{:T(128)S(6)} %select_n.86, bf16[352,2048]{1,0:T(8,128)(2,1)} %param.41, bf16[2048,352]{0,1:T(8,128)(2,1)} %param.40, bf16[128,2048]{1,0:T(8,128)(2,1)S(1)} %reshape.535, f32[32,352]{1,0:T(8,128)S(1)} %fusion.41), kind=kOutput, calls=%fused_computation.10 | convolution fusion | flops 92407808 | bytes 3589120 | tf_op jit(solution)/shard_map/dot_general | solution.py:225
  142.7 30.4 %all_to_all.36 = f32[32,4,2048]{2,1,0:T(4,128)S(1)} all-to-all(f32[32,4,2048]{2,1,0:T(4,128)S(1)} %reshape.536), channel_id=1, replica_groups=mesh['seq'=4,'exp'=8] {'seq','exp'}, dimensions={0} | all-to-all | bytes 2097152 | tf_op jit(solution)/shard_map/all_to_all | solution.py:234
  173.5 14.0 %all-gather.7 = bf16[8,4,2048]{2,1,0:T(4,128)(2,1)S(1)} all-gather(bf16[1,4,2048]{2,1,0:T(4,128)(2,1)S(1)} %fusion.54), channel_id=6, replica_groups=mesh['seq'=4,'exp'=8] {'exp'}, dimensions={0}, use_global_device_ids=true | all-gather | bytes 147456 | tf_op jit(solution)/shard_map/all_gather | solution.py:36
  187.4 9.4 %all-gather.5 = bf16[32,4,2048]{2,1,0:T(4,128)(2,1)S(1)} all-gather(bf16[8,4,2048]{2,1,0:T(4,128)(2,1)S(1)} %all-gather.7), channel_id=7, replica_groups=mesh['seq'=4,'exp'=8] {'seq'}, dimensions={0}, use_global_device_ids=true | all-gather | bytes 655360 | tf_op jit(solution)/shard_map/all_gather | solution.py:37
  196.9 4.9 %convolution_reduce_fusion = f32[128]{0:T(128)S(1)} fusion(bf16[128,2048]{1,0:T(8,128)(2,1)S(1)} %reshape.537, bf16[2048,1600]{0,1:T(8,128)(2,1)} %param.43), kind=kOutput, calls=%fused_computation.18 | convolution fusion | flops 839065472 | bytes 7078400 | tf_op jit(solution)/shard_map/dot_general | solution.py:242
  201.9 9.3 %all_to_all.37 = f32[32,1,132]{2,1,0:T(1,128)S(1)} all-to-all(f32[32,1,132]{2,1,0:T(1,128)S(1)} %broadcast_in_dim.150), channel_id=1, replica_groups=mesh['seq'=4,'exp'=8] {'seq','exp'}, dimensions={0} | all-to-all | bytes 33792 | tf_op jit(solution)/shard_map/all_to_all | solution.py:244
  (119 shorter events, 22.3 us)
Async XLA Ops:
  0.6 72.1 %copy-start = (bf16[512,2048]{1,0:T(8,128)(2,1)S(1)}, bf16[512,2048]{1,0:T(8,128)(2,1)}, u32[]{:S(2)}) copy-start(bf16[512,2048]{1,0:T(8,128)(2,1)} %param.31) | copy-start | bytes 6291460
  6.7 8.0 %copy-start.9 = (s32[32]{0:T(128)S(1)}, s32[32]{0:T(128)}, u32[]{:S(2)}) copy-start(s32[32]{0:T(128)} %param.23) | copy-start | bytes 388
  8.4 21.7 %all-to-all-start = ((bf16[8,4,4,2048]{3,2,1,0:T(4,128)(2,1)}), bf16[8,4,4,2048]{3,2,1,0:T(4,128)(2,1)S(1)}, u32[]{:S(2)}, u32[]{:S(2)}) async-start(bf16[8,4,4,2048]{3,2,1,0:T(4,128)(2,1)} %fusion.31), calls=%async_computation | async-start | bytes 1048576 | tf_op jit(solution)/shard_map/all_to_all | solution.py:94
  22.8 5.0 %copy-start.5 = (s32[4,32,6]{1,0,2:T(4,128)S(1)}, s32[4,32,6]{1,0,2:T(4,128)}, u32[]{:S(2)}) copy-start(s32[4,32,6]{1,0,2:T(4,128)} %param.25) | copy-start | bytes 9220
  22.8 16.8 %copy-start.6 = (f32[2048]{0:T(1024)S(1)}, f32[2048]{0:T(1024)}, u32[]{:S(2)}) copy-start(f32[2048]{0:T(1024)} %param.27) | copy-start | bytes 24580
  39.7 2.4 %copy-start.2 = (bf16[512,2048]{1,0:T(8,128)(2,1)S(1)}, bf16[512,2048]{1,0:T(8,128)(2,1)}, u32[]{:S(2)}) copy-start(bf16[512,2048]{1,0:T(8,128)(2,1)} %copy.153) | copy-start | bytes 6291460
  63.0 8.3 %all-to-all-start.1 = ((f32[4,1,8320]{2,1,0:T(1,128)}), f32[4,1,8320]{2,1,0:T(1,128)S(1)}, u32[]{:S(2)}, u32[]{:S(2)}) async-start(f32[4,1,8320]{2,1,0:T(1,128)} %copy.135), calls=%async_computation.1 | async-start | bytes 266240 | tf_op jit(solution)/shard_map/all_to_all | solution.py:155
  72.3 10.1 %copy-start.7 = (f32[2048]{0:T(1024)S(1)}, f32[2048]{0:T(1024)}, u32[]{:S(2)}) copy-start(f32[2048]{0:T(1024)} %param.34) | copy-start | bytes 24580
  73.8 32.7 %copy-start.4 = (bf16[2048,64]{0,1:T(8,128)(2,1)S(1)}, bf16[2048,64]{0,1:T(8,128)(2,1)}, u32[]{:S(2)}) copy-start(bf16[2048,64]{0,1:T(8,128)(2,1)} %param.35) | copy-start | bytes 786436
  73.8 8.4 %all-to-all-start.2 = ((f32[4,4,2048]{2,1,0:T(4,128)}), f32[4,4,2048]{2,1,0:T(4,128)S(1)}, u32[]{:S(2)}, u32[]{:S(2)}) async-start(f32[4,4,2048]{2,1,0:T(4,128)} %fusion.9), calls=%async_computation.2 | async-start | bytes 262144 | tf_op jit(solution)/shard_map/all_to_all | solution.py:190
  137.3 1.4 copy-start.3
  142.7 30.7 %copy-start.8 = (f32[2048]{0:T(1024)S(1)}, f32[2048]{0:T(1024)}, u32[]{:S(2)}) copy-start(f32[2048]{0:T(1024)} %param.42) | copy-start | bytes 24580
  196.9 15.6 %copy-start.1 = (bf16[512,2048]{1,0:T(8,128)(2,1)S(1)}, bf16[512,2048]{1,0:T(8,128)(2,1)}, u32[]{:S(2)}) copy-start(bf16[512,2048]{1,0:T(8,128)(2,1)} %param.31) | copy-start | bytes 6291460

commit v2 on v1

--- a/solution.py
+++ b/solution.py
@@ -75,11 +75,11 @@
     group = steps * own_count
     share = group // n_seq
 
-    def permuted(values):
+    def grouped(values):
         rest = values.shape[2:]
-        grouped = jnp.moveaxis(values.reshape((steps, n_exp, own_count) + rest), 1, 0)
-        split = grouped.reshape((n_exp, n_seq, share) + rest)
-        return jnp.swapaxes(split, 0, 1).reshape((tokens,) + rest)
+        by_group = jnp.moveaxis(values.reshape((steps, n_exp, own_count) + rest), 1, 0)
+        return by_group.reshape((tokens,) + rest)
+
 
     def natural(values):
         split = jnp.swapaxes(values.reshape(n_seq, n_exp, share), 0, 1)
@@ -186,17 +186,15 @@
     )
 
     attn_part = jnp.dot(own_heads, w_out, preferred_element_type=jnp.float32)
-    attn_sum = jnp.sum(
-        lax.all_to_all(attn_part.reshape(n_seq, share, width), "seq", 0, 0, tiled=True), axis=0
-    )
-    resid_share = lax.dynamic_slice_in_dim(embedded, seq_index * share, share, 0) + attn_sum
-    moe_in = gather_all(rms_scale(resid_share, moe_gain).astype(jnp.bfloat16)).reshape(
-        tokens, width
+    resid_group = embedded + jnp.sum(lax.all_gather(attn_part, "seq", axis=0, tiled=False), axis=0)
+    resid_share = lax.dynamic_slice_in_dim(resid_group, seq_index * share, share, 0)
+    moe_in = lax.all_gather(
+        rms_scale(resid_group, moe_gain).astype(jnp.bfloat16), "exp", axis=0, tiled=True
     )
 
     router = jax.nn.sigmoid(jnp.dot(moe_in, w_router, preferred_element_type=jnp.float32))
     expert_count = w_router.shape[1]
-    chosen_ids = permuted(expert_ids)
+    chosen_ids = grouped(expert_ids)
     picked = chosen_ids[:, :, None] == jnp.arange(expert_count, dtype=jnp.int32)[None, None, :]
     chosen = jnp.sum(jnp.where(picked, router[:, None, :], 0.0), axis=2)
     gate_weights = chosen / jnp.sum(chosen, axis=1, keepdims=True)
@@ -230,8 +228,15 @@
         0,
     )
 
+    term_rows = jnp.swapaxes(term_rows.reshape(n_exp, n_seq, share, width), 0, 1)
     term_sum = jnp.sum(
-        lax.all_to_all(term_rows.reshape(n_dev, share, width), ("seq", "exp"), 0, 0, tiled=True),
+        lax.all_to_all(
+            term_rows.reshape(n_dev, share, width).astype(jnp.bfloat16),
+            ("seq", "exp"),
+            0,
+            0,
+            tiled=True,
+        ).astype(jnp.float32),
         axis=0,
     )
     final_share = resid_share + term_sum

time: 214 us -> 195 us (0.911)
  blocking collectives: 105 us -> 74.8 us
  waiting for transfers between devices: 11.9 us -> 23.1 us
    all_to_all x1 -> x0, blocking collectives: 30.4 us -> none  [on_device(): lax.all_to_all(term_rows.reshape(n_dev, share, width), ('seq', 'exp'), 0,...]
    all_gather x0 -> x2, blocking collectives: none -> 24.3 us  [the longest x1 14.8 us: on_device(): lax.all_gather(rms_scale(resid_group, moe_gain).astype(jnp.bfloat16), 'ex...]
    all_gather x2 -> x1, blocking collectives: 27.9 us -> 14 us  [gather_all(): inner = lax.all_gather(values, 'exp', axis=0, tiled=False)]
    all_to_all x1, waiting for transfers between devices: 4.91 us -> 16.4 us  [on_device(): lax.all_to_all(term_rows.reshape(n_dev, share, width).astype(jnp.bfloat16...]
    all_gather x2 -> x1, blocking collectives: 19.1 us -> 9.37 us  [gather_all(): return lax.all_gather(inner, 'seq', axis=0, tiled=False)]
  transfers between devices with their start and end apart: 3 -> 3, of which waited for: 3 -> 3; matrix products, arithmetic and copies ran while one was open for 6% -> 7% of each run, Pallas kernels for 0% -> 0%
where the time goes in v2:
time: 195 us; the launch traced here: 194 us
  blocking collectives  74.8 us (38%)
  matrix products  51.1 us (26%)
  local copies, waits for them, and re-layouts  25.7 us (13%)
  waiting for transfers between devices  23.1 us (12%)
  starting transfers between devices  12.9 us (7%)
  other arithmetic  5.42 us (3%)
    dot_general x1, matrix products, on_device(): jnp.einsum('jnf,jfd->jnd', expert_hidden, down_pieces, preferred_element_...  18.6 us
    all_to_all x1, waiting for transfers between devices, on_device(): lax.all_to_all(term_rows.reshape(n_dev, share, width).astype(jnp.bfloat16...  16.4 us
    all_gather x1, blocking collectives, on_device(): lax.all_gather(rms_scale(resid_group, moe_gain).astype(jnp.bfloat16), 'ex...  14.8 us
    all_gather x1, blocking collectives, gather_all(): inner = lax.all_gather(values, 'exp', axis=0, tiled=False)  14 us
    dot_general x3, local copies, waits for them, and re-layouts, project(): jnp.dot(attn_in, weight, preferred_element_type=jnp.float32)  11.9 us
    all_gather x1, blocking collectives, on_device(): lax.all_gather(attn_part, 'seq', axis=0, tiled=False)  9.45 us
    all_gather x1, blocking collectives, gather_all(): return lax.all_gather(inner, 'seq', axis=0, tiled=False)  9.37 us
    all_to_all x1, blocking collectives, on_device(): lax.all_to_all(jnp.broadcast_to(message[None, :], (n_dev, message.shape[0...  9.33 us
  transfers between devices with their start and end apart: 3, of which 3 were waited for; matrix products, arithmetic and copies ran while one was open for 7% of the time, Pallas kernels for 0%

profile of v2, /device:TPU:0, one launch (start us, length us, event | category | flops | bytes accessed | tf_op | source)
XLA Modules:
  0.0 194.2 jit_solution(3105596744407225946)
XLA Ops:
  1.6 5.1 %gather_fusion = bf16[128,2048]{1,0:T(8,128)(2,1)S(1)} fusion(bf16[1600,2048]{1,0:T(8,128)(2,1)} %param.26, s32[1024]{0:T(1024)S(1)} %pad_clamp_fusion), kind=kCustom, calls=%fused_computation | custom fusion | bytes 1049088 | tf_op jit(solution)/shard_map/jit(_take)/gather | solution.py:91
  8.4 6.3 %all-to-all-start = ((bf16[8,4,4,2048]{3,2,1,0:T(4,128)(2,1)}), bf16[8,4,4,2048]{3,2,1,0:T(4,128)(2,1)S(1)}, u32[]{:S(2)}, u32[]{:S(2)}) async-start(bf16[8,4,4,2048]{3,2,1,0:T(4,128)(2,1)} %fusion.32), calls=%async_computation | async-start | bytes 1048576 | tf_op jit(solution)/shard_map/all_to_all | solution.py:94
  15.6 4.0 %copy.160 = bf16[512,2048]{1,0:T(8,128)(2,1)} copy(bf16[512,2048]{0,1:T(8,128)(2,1)} %bitcast.152) | data formatting | bytes 4194304 | tf_op jit(solution)/shard_map/dot_general | solution.py:105
  19.5 3.9 %copy.161 = bf16[512,2048]{1,0:T(8,128)(2,1)} copy(bf16[512,2048]{0,1:T(8,128)(2,1)} %bitcast.153) | data formatting | bytes 4194304 | tf_op jit(solution)/shard_map/dot_general | solution.py:105
  23.6 4.0 %copy.162 = bf16[512,2048]{1,0:T(8,128)(2,1)} copy(bf16[512,2048]{0,1:T(8,128)(2,1)} %bitcast.154) | data formatting | bytes 4194304 | tf_op jit(solution)/shard_map/dot_general | solution.py:105
  30.3 9.0 %all-gather = bf16[16,4,2048]{2,1,0:T(4,128)(2,1)S(1)} all-gather(bf16[4,4,2048]{2,1,0:T(4,128)(2,1)S(1)} %reduce_sum.137), channel_id=2, replica_groups=mesh['seq'=4,'exp'=8] {'seq'}, dimensions={0}, use_global_device_ids=true | all-gather | bytes 327680 | tf_op jit(solution)/shard_map/all_gather | solution.py:96
  39.8 2.4 %fusion.77 = f32[16,4,128]{2,0,1:T(8,128)S(1)} fusion(bf16[16,2048,1]{1,0,2:T(8,128)(2,1)S(1)} %reshape.572, bf16[4,128,2048]{2,1,0:T(8,128)(2,1)} %bitcast.149), kind=kOutput, calls=%fused_computation.136 | convolution fusion | flops 33554432 | bytes 2195456 | tf_op jit(solution)/shard_map/dot_general | solution.py:105
  45.8 8.8 %all-gather.1 = bf16[12,16,4,128]{3,1,2,0:T(8,128)(2,1)S(1)} all-gather(bf16[3,16,4,128]{3,1,2,0:T(8,128)(2,1)S(1)} %pad_maximum_fusion), channel_id=3, replica_groups=mesh['seq'=4,'exp'=8] {'seq'}, dimensions={0}, use_global_device_ids=true | all-gather | bytes 245760 | tf_op jit(solution)/shard_map/all_gather | solution.py:112
  54.8 3.5 %select_reduce_fusion = (f32[4,4,16]{0,2,1:T(8,128)S(1)}, f32[4,4,16,256]{3,0,2,1:T(4,128)S(1)}) fusion(pred[4,256]{1,0:T(4,128)(4,1)S(1)} %compare_and_fusion, bf16[4,4,16,128]{3,2,1,0:T(8,128)(2,1)S(1)} %bitcast.184, bf16[4,256,2048]{2,1,0:T(8,128)(2,1)} %param.32), kind=kOutput, calls=%fused_computation.44 | convolution fusion | flops 16973568 | bytes 4524032 | tf_op jit(solution)/shard_map/trhd,rphd->trhp/dot_general | solution.py:132
  58.8 2.9 %fusion.2 = f32[4,16,4,128]{3,2,1,0:T(4,128)S(1)} fusion(f32[4,4,16,256]{3,0,2,1:T(4,128)S(1)} %get-tuple-element.25, f32[4,4,16]{0,2,1:T(8,128)S(1)} %get-tuple-element.24, pred[4,256]{1,0:T(4,128)(4,1)S(1)} %compare_and_fusion, bf16[4,256,2048]{2,1,0:T(8,128)(2,1)} %param.33), kind=kOutput, calls=%fused_computation.3 | convolution fusion | flops 16973824 | bytes 4589568 | tf_op jit(solution)/shard_map/trhp,rphd->trhd/dot_general | solution.py:138
  63.1 3.3 %all-to-all-start.1 = ((f32[4,1,8320]{2,1,0:T(1,128)}), f32[4,1,8320]{2,1,0:T(1,128)S(1)}, u32[]{:S(2)}, u32[]{:S(2)}) async-start(f32[4,1,8320]{2,1,0:T(1,128)} %copy.140), calls=%async_computation.1 | async-start | bytes 266240 | tf_op jit(solution)/shard_map/all_to_all | solution.py:155
  66.4 4.9 %all-to-all-done.1 = f32[4,1,8320]{2,1,0:T(1,128)S(1)} async-done(((f32[4,1,8320]{2,1,0:T(1,128)}), f32[4,1,8320]{2,1,0:T(1,128)S(1)}, u32[]{:S(2)}, u32[]{:S(2)}) %all-to-all-start.1) | async-done | bytes 133152 | tf_op jit(solution)/shard_map/all_to_all | solution.py:155
  73.2 9.4 %all-gather.2 = f32[64,2048]{1,0:T(8,128)S(1)} all-gather(f32[16,2048]{1,0:T(8,128)S(1)} %fusion.55), channel_id=4, replica_groups=mesh['seq'=4,'exp'=8] {'seq'}, dimensions={0}, use_global_device_ids=true | all-gather | bytes 655360 | tf_op jit(solution)/shard_map/all_gather | solution.py:189
  82.9 14.8 %all_gather.39 = bf16[128,2048]{1,0:T(8,128)(2,1)S(1)} all-gather(bf16[16,2048]{1,0:T(8,128)(2,1)S(1)} %multiply_convert_fusion), channel_id=1, replica_groups=mesh['seq'=4,'exp'=8] {'exp'}, dimensions={0}, use_global_device_ids=true | all-gather | bytes 589824 | tf_op jit(solution)/shard_map/all_gather | solution.py:191
  97.8 6.2 %convolution_bitcast_fusion.1 = f32[8,128,352]{1,2,0:T(8,128)S(1)} fusion(bf16[8,2048,352]{1,2,0:T(8,128)(2,1)} %param.36, bf16[128,2048]{1,0:T(8,128)(2,1)S(1)} %all_gather.39), kind=kOutput, calls=%fused_computation.12 | convolution fusion | flops 1476395008 | bytes 13500416 | tf_op jit(solution)/shard_map/nd,jdf->jnf/dot_general | solution.py:209
  104.6 18.6 %fusion.11 = bf16[8,128,2048]{2,1,0:T(8,128)(2,1)} fusion(bf16[8,352,2048]{2,1,0:T(8,128)(2,1)} %param.38, bf16[8,2048,352]{1,2,0:T(8,128)(2,1)} %param.37, f32[8,128,352]{1,2,0:T(8,128)S(1)} %convolution_bitcast_fusion.1, bf16[128,2048]{1,0:T(8,128)(2,1)S(1)} %all_gather.39), kind=kOutput, calls=%fused_computation.15 | convolution fusion | flops 2954952704 | bytes 29229056 | tf_op jit(solution)/shard_map/jnf,jfd->jnd/dot_general | solution.py:212
  123.3 5.3 %fusion = f32[128,1,2048]{2,1,0:T(1,128)S(1)} fusion(bf16[8,128,1]{0,2,1:T(2,128)(2,1)S(1)} %copy.157, bf16[8,128,2048]{2,1,0:T(8,128)(2,1)} %fusion.11), kind=kOutput, calls=%fused_computation.1 | convolution fusion | flops 4194304 | bytes 5244928 | tf_op jit(solution)/shard_map/jn,jnd->nd/dot_general | solution.py:215
  130.5 2.7 %fusion.8 = f32[128,2048]{1,0:T(8,128)S(1)} fusion(f32[128,2048]{1,0:T(8,128)S(1)} %bitcast.150, s32[]{:T(128)S(6)} %select_n.86, bf16[352,2048]{1,0:T(8,128)(2,1)S(1)} %copy-done.4, bf16[2048,352]{0,1:T(8,128)(2,1)} %param.40, bf16[128,2048]{1,0:T(8,128)(2,1)S(1)} %all_gather.39, f32[32,352]{1,0:T(8,128)S(1)} %fusion.42), kind=kOutput, calls=%fused_computation.10 | convolution fusion | flops 92407808 | bytes 3589120 | tf_op jit(solution)/shard_map/dot_general | solution.py:223
  135.0 3.3 %all-to-all-start.2 = ((bf16[32,4,2048]{2,1,0:T(4,128)(2,1)}), bf16[32,4,2048]{2,1,0:T(4,128)(2,1)S(1)}, u32[]{:S(2)}, u32[]{:S(2)}) async-start(bf16[32,4,2048]{2,1,0:T(4,128)(2,1)} %copy.155), calls=%async_computation.2 | async-start | bytes 1048576 | tf_op jit(solution)/shard_map/all_to_all | solution.py:233
  138.3 16.4 %all-to-all-done.2 = bf16[32,4,2048]{2,1,0:T(4,128)(2,1)S(1)} async-done(((bf16[32,4,2048]{2,1,0:T(4,128)(2,1)}), bf16[32,4,2048]{2,1,0:T(4,128)(2,1)S(1)}, u32[]{:S(2)}, u32[]{:S(2)}) %all-to-all-start.2) | async-done | bytes 524320 | tf_op jit(solution)/shard_map/all_to_all | solution.py:233
  155.1 14.0 %all-gather.5 = bf16[8,4,2048]{2,1,0:T(4,128)(2,1)S(1)} all-gather(bf16[1,4,2048]{2,1,0:T(4,128)(2,1)S(1)} %fusion.54), channel_id=5, replica_groups=mesh['seq'=4,'exp'=8] {'exp'}, dimensions={0}, use_global_device_ids=true | all-gather | bytes 147456 | tf_op jit(solution)/shard_map/all_gather | solution.py:36
  169.1 9.4 %all-gather.4 = bf16[32,4,2048]{2,1,0:T(4,128)(2,1)S(1)} all-gather(bf16[8,4,2048]{2,1,0:T(4,128)(2,1)S(1)} %all-gather.5), channel_id=6, replica_groups=mesh['seq'=4,'exp'=8] {'seq'}, dimensions={0}, use_global_device_ids=true | all-gather | bytes 655360 | tf_op jit(solution)/shard_map/all_gather | solution.py:37
  178.6 4.9 %convolution_reduce_fusion = f32[128]{0:T(128)S(1)} fusion(bf16[128,2048]{1,0:T(8,128)(2,1)S(1)} %reshape.550, bf16[2048,1600]{0,1:T(8,128)(2,1)} %param.43), kind=kOutput, calls=%fused_computation.16 | convolution fusion | flops 839065472 | bytes 7078400 | tf_op jit(solution)/shard_map/dot_general | solution.py:247
  183.5 9.3 %all_to_all.31 = f32[32,1,132]{2,1,0:T(1,128)S(1)} all-to-all(f32[32,1,132]{2,1,0:T(1,128)S(1)} %broadcast_in_dim.150), channel_id=1, replica_groups=mesh['seq'=4,'exp'=8] {'seq','exp'}, dimensions={0} | all-to-all | bytes 33792 | tf_op jit(solution)/shard_map/all_to_all | solution.py:249
  (122 shorter events, 20.5 us)
Async XLA Ops:
  0.6 72.2 %copy-start = (bf16[512,2048]{1,0:T(8,128)(2,1)S(1)}, bf16[512,2048]{1,0:T(8,128)(2,1)}, u32[]{:S(2)}) copy-start(bf16[512,2048]{1,0:T(8,128)(2,1)} %param.31) | copy-start | bytes 6291460
  6.7 8.0 %copy-start.10 = (s32[32]{0:T(128)S(1)}, s32[32]{0:T(128)}, u32[]{:S(2)}) copy-start(s32[32]{0:T(128)} %param.23) | copy-start | bytes 388
  8.4 21.7 %all-to-all-start = ((bf16[8,4,4,2048]{3,2,1,0:T(4,128)(2,1)}), bf16[8,4,4,2048]{3,2,1,0:T(4,128)(2,1)S(1)}, u32[]{:S(2)}, u32[]{:S(2)}) async-start(bf16[8,4,4,2048]{3,2,1,0:T(4,128)(2,1)} %fusion.32), calls=%async_computation | async-start | bytes 1048576 | tf_op jit(solution)/shard_map/all_to_all | solution.py:94
  23.6 4.2 %copy-start.6 = (s32[4,32,6]{1,0,2:T(4,128)S(1)}, s32[4,32,6]{1,0,2:T(4,128)}, u32[]{:S(2)}) copy-start(s32[4,32,6]{1,0,2:T(4,128)} %param.25) | copy-start | bytes 9220
  27.6 12.1 %copy-start.7 = (f32[2048]{0:T(1024)S(1)}, f32[2048]{0:T(1024)}, u32[]{:S(2)}) copy-start(f32[2048]{0:T(1024)} %param.27) | copy-start | bytes 24580
  39.8 2.4 %copy-start.2 = (bf16[512,2048]{1,0:T(8,128)(2,1)S(1)}, bf16[512,2048]{1,0:T(8,128)(2,1)}, u32[]{:S(2)}) copy-start(bf16[512,2048]{1,0:T(8,128)(2,1)} %copy.161) | copy-start | bytes 6291460
  63.1 8.3 %all-to-all-start.1 = ((f32[4,1,8320]{2,1,0:T(1,128)}), f32[4,1,8320]{2,1,0:T(1,128)S(1)}, u32[]{:S(2)}, u32[]{:S(2)}) async-start(f32[4,1,8320]{2,1,0:T(1,128)} %copy.140), calls=%async_computation.1 | async-start | bytes 266240 | tf_op jit(solution)/shard_map/all_to_all | solution.py:155
  72.8 10.1 %copy-start.8 = (f32[2048]{0:T(1024)S(1)}, f32[2048]{0:T(1024)}, u32[]{:S(2)}) copy-start(f32[2048]{0:T(1024)} %param.34) | copy-start | bytes 24580
  97.8 6.3 %copy-start.5 = (bf16[2048,64]{0,1:T(8,128)(2,1)S(1)}, bf16[2048,64]{0,1:T(8,128)(2,1)}, u32[]{:S(2)}) copy-start(bf16[2048,64]{0,1:T(8,128)(2,1)} %param.35) | copy-start | bytes 786436
  128.6 1.4 copy-start.3
  128.6 1.9 copy-start.4
  133.5 21.5 %copy-start.9 = (f32[2048]{0:T(1024)S(1)}, f32[2048]{0:T(1024)}, u32[]{:S(2)}) copy-start(f32[2048]{0:T(1024)} %param.42) | copy-start | bytes 24580
  135.0 19.6 %all-to-all-start.2 = ((bf16[32,4,2048]{2,1,0:T(4,128)(2,1)}), bf16[32,4,2048]{2,1,0:T(4,128)(2,1)S(1)}, u32[]{:S(2)}, u32[]{:S(2)}) async-start(bf16[32,4,2048]{2,1,0:T(4,128)(2,1)} %copy.155), calls=%async_computation.2 | async-start | bytes 1048576 | tf_op jit(solution)/shard_map/all_to_all | solution.py:233
  178.6 15.6 %copy-start.1 = (bf16[512,2048]{1,0:T(8,128)(2,1)S(1)}, bf16[512,2048]{1,0:T(8,128)(2,1)}, u32[]{:S(2)}) copy-start(bf16[512,2048]{1,0:T(8,128)(2,1)} %param.31) | copy-start | bytes 6291460

commit v3 on v2

--- a/solution.py
+++ b/solution.py
@@ -86,11 +86,11 @@
         grouped = split.reshape(n_exp, steps, own_count)
         return jnp.moveaxis(grouped, 0, 1).reshape(steps, requests)
 
-    local_ids = token_ids - owner_index * vocab_local
+    group_ids = jnp.moveaxis(token_ids.reshape(steps, n_exp, own_count), 1, 0)
+    local_ids = group_ids - owner_index * vocab_local
     held = (local_ids >= 0) & (local_ids < vocab_local)
     rows = jnp.take(embed_table, jnp.clip(local_ids, 0, vocab_local - 1), axis=0)
     rows = jnp.where(held[..., None], rows, jnp.zeros((), rows.dtype))
-    rows = jnp.moveaxis(rows.reshape(steps, n_exp, own_count, width), 1, 0)
     arrived = lax.all_to_all(rows, "exp", 0, 0, tiled=True)
     row_part = jnp.sum(arrived.astype(jnp.float32), axis=0).astype(jnp.bfloat16)
     row_parts = lax.all_gather(row_part, "seq", axis=0, tiled=False)
@@ -208,11 +208,12 @@
     )
     gate_out = jnp.einsum("nd,jdf->jnf", moe_in, gate_pieces, preferred_element_type=jnp.float32)
     up_out = jnp.einsum("nd,jdf->jnf", moe_in, up_pieces, preferred_element_type=jnp.float32)
-    expert_hidden = (jax.nn.silu(gate_out) * up_out).astype(jnp.bfloat16)
-    expert_out = jnp.einsum(
-        "jnf,jfd->jnd", expert_hidden, down_pieces, preferred_element_type=jnp.float32
-    )
-    routed = jnp.einsum("jn,jnd->nd", token_weight, expert_out)
+    weighted_hidden = (jax.nn.silu(gate_out) * up_out * token_weight[:, :, None]).astype(
+        jnp.bfloat16
+    )
+    routed = jnp.einsum(
+        "jnf,jfd->nd", weighted_hidden, down_pieces, preferred_element_type=jnp.float32
+    )
     share_count = tokens // n_seq
     share_start = seq_index * share_count
     share_rows = lax.dynamic_slice_in_dim(moe_in, share_start, share_count, 0)

time: 195 us -> 185 us (0.949)
  matrix products: 51.1 us -> 42 us
    dot_general x2 -> x1, matrix products: 24 us -> 14.7 us  [on_device(): jnp.einsum('jnf,jfd->nd', weighted_hidden, down_pieces, preferred_element...]
where the time goes in v3:
time: 185 us; the launch traced here: 184 us
  blocking collectives  75 us (41%)
  matrix products  42 us (23%)
  local copies, waits for them, and re-layouts  24.2 us (13%)
  waiting for transfers between devices  23.1 us (12%)
  starting transfers between devices  12.9 us (7%)
  other arithmetic  6.12 us (3%)
    all_to_all x1, waiting for transfers between devices, on_device(): lax.all_to_all(term_rows.reshape(n_dev, share, width).astype(jnp.bfloat16...  16.4 us
    all_gather x1, blocking collectives, on_device(): lax.all_gather(rms_scale(resid_group, moe_gain).astype(jnp.bfloat16), 'ex...  15 us
    dot_general x1, matrix products, on_device(): jnp.einsum('jnf,jfd->nd', weighted_hidden, down_pieces, preferred_element...  14.7 us
    all_gather x1, blocking collectives, gather_all(): inner = lax.all_gather(values, 'exp', axis=0, tiled=False)  14 us
    dot_general x3, local copies, waits for them, and re-layouts, project(): jnp.dot(attn_in, weight, preferred_element_type=jnp.float32)  11.9 us
    all_gather x1, blocking collectives, on_device(): lax.all_gather(attn_part, 'seq', axis=0, tiled=False)  9.45 us
    all_gather x1, blocking collectives, gather_all(): return lax.all_gather(inner, 'seq', axis=0, tiled=False)  9.37 us
    all_to_all x1, blocking collectives, on_device(): lax.all_to_all(jnp.broadcast_to(message[None, :], (n_dev, message.shape[0...  9.32 us
  transfers between devices with their start and end apart: 3, of which 3 were waited for; matrix products, arithmetic and copies ran while one was open for 7% of the time, Pallas kernels for 0%

profile of v3, /device:TPU:0, one launch (start us, length us, event | category | flops | bytes accessed | tf_op | source)
XLA Modules:
  0.0 184.5 jit_solution(12790132844402433581)
XLA Ops:
  2.4 5.1 %gather_fusion = bf16[128,2048]{1,0:T(8,128)(2,1)S(1)} fusion(bf16[1600,2048]{1,0:T(8,128)(2,1)} %param.26, s32[1024]{0:T(1024)S(1)} %pad_clamp_fusion), kind=kCustom, calls=%fused_computation | custom fusion | bytes 1049088 | tf_op jit(solution)/shard_map/jit(_take)/gather | solution.py:92
  9.1 6.3 %all-to-all-start = ((bf16[8,4,4,2048]{3,2,1,0:T(4,128)(2,1)}), bf16[8,4,4,2048]{3,2,1,0:T(4,128)(2,1)S(1)}, u32[]{:S(2)}, u32[]{:S(2)}) async-start(bf16[8,4,4,2048]{3,2,1,0:T(4,128)(2,1)} %select_select_fusion), calls=%async_computation | async-start | bytes 1048576 | tf_op jit(solution)/shard_map/all_to_all | solution.py:94
  16.3 4.0 %copy.166 = bf16[512,2048]{1,0:T(8,128)(2,1)} copy(bf16[512,2048]{0,1:T(8,128)(2,1)} %bitcast.153) | data formatting | bytes 4194304 | tf_op jit(solution)/shard_map/dot_general | solution.py:105
  20.3 3.9 %copy.167 = bf16[512,2048]{1,0:T(8,128)(2,1)} copy(bf16[512,2048]{0,1:T(8,128)(2,1)} %bitcast.154) | data formatting | bytes 4194304 | tf_op jit(solution)/shard_map/dot_general | solution.py:105
  24.3 4.0 %copy.168 = bf16[512,2048]{1,0:T(8,128)(2,1)} copy(bf16[512,2048]{0,1:T(8,128)(2,1)} %bitcast.155) | data formatting | bytes 4194304 | tf_op jit(solution)/shard_map/dot_general | solution.py:105
  31.1 9.0 %all-gather = bf16[16,4,2048]{2,1,0:T(4,128)(2,1)S(1)} all-gather(bf16[4,4,2048]{2,1,0:T(4,128)(2,1)S(1)} %reduce_sum.137), channel_id=2, replica_groups=mesh['seq'=4,'exp'=8] {'seq'}, dimensions={0}, use_global_device_ids=true | all-gather | bytes 327680 | tf_op jit(solution)/shard_map/all_gather | solution.py:96
  40.5 2.4 %fusion.72 = f32[16,4,128]{2,0,1:T(8,128)S(1)} fusion(bf16[16,2048,1]{1,0,2:T(8,128)(2,1)S(1)} %reshape.577, bf16[4,128,2048]{2,1,0:T(8,128)(2,1)} %bitcast.151), kind=kOutput, calls=%fused_computation.132 | convolution fusion | flops 33554432 | bytes 2195456 | tf_op jit(solution)/shard_map/dot_general | solution.py:105
  44.2 2.2 %convolution_convert_fusion = bf16[16,4,128]{2,0,1:T(8,128)(2,1)S(1)} fusion(bf16[16,2048,1]{1,0,2:T(8,128)(2,1)S(1)} %reshape.577, bf16[4,128,2048]{2,1,0:T(8,128)(2,1)} %bitcast.149), kind=kOutput, calls=%fused_computation.31 | convolution fusion | flops 33562624 | bytes 2179072 | tf_op jit(solution)/shard_map/dot_general | solution.py:105
  46.6 8.8 %all-gather.1 = bf16[12,16,4,128]{3,1,2,0:T(8,128)(2,1)S(1)} all-gather(bf16[3,16,4,128]{3,1,2,0:T(8,128)(2,1)S(1)} %pad_maximum_fusion), channel_id=3, replica_groups=mesh['seq'=4,'exp'=8] {'seq'}, dimensions={0}, use_global_device_ids=true | all-gather | bytes 245760 | tf_op jit(solution)/shard_map/all_gather | solution.py:112
  55.5 3.5 %select_reduce_fusion = (f32[4,4,16]{0,2,1:T(8,128)S(1)}, f32[4,4,16,256]{3,0,2,1:T(4,128)S(1)}) fusion(pred[4,256]{1,0:T(4,128)(4,1)S(1)} %compare_and_fusion.1, bf16[4,4,16,128]{3,2,1,0:T(8,128)(2,1)S(1)} %bitcast.185, bf16[4,256,2048]{2,1,0:T(8,128)(2,1)} %param.32), kind=kOutput, calls=%fused_computation.39 | convolution fusion | flops 16973568 | bytes 4524032 | tf_op jit(solution)/shard_map/trhd,rphd->trhp/dot_general | solution.py:132
  59.6 2.9 %fusion = f32[4,16,4,128]{3,2,1,0:T(4,128)S(1)} fusion(f32[4,4,16,256]{3,0,2,1:T(4,128)S(1)} %get-tuple-element.22, f32[4,4,16]{0,2,1:T(8,128)S(1)} %get-tuple-element.21, pred[4,256]{1,0:T(4,128)(4,1)S(1)} %compare_and_fusion.1, bf16[4,256,2048]{2,1,0:T(8,128)(2,1)} %param.33), kind=kOutput, calls=%fused_computation.1 | convolution fusion | flops 16973824 | bytes 4589568 | tf_op jit(solution)/shard_map/trhp,rphd->trhd/dot_general | solution.py:138
  63.8 3.3 %all-to-all-start.1 = ((f32[4,1,8320]{2,1,0:T(1,128)}), f32[4,1,8320]{2,1,0:T(1,128)S(1)}, u32[]{:S(2)}, u32[]{:S(2)}) async-start(f32[4,1,8320]{2,1,0:T(1,128)} %copy.149), calls=%async_computation.1 | async-start | bytes 266240 | tf_op jit(solution)/shard_map/all_to_all | solution.py:155
  67.2 4.9 %all-to-all-done.1 = f32[4,1,8320]{2,1,0:T(1,128)S(1)} async-done(((f32[4,1,8320]{2,1,0:T(1,128)}), f32[4,1,8320]{2,1,0:T(1,128)S(1)}, u32[]{:S(2)}, u32[]{:S(2)}) %all-to-all-start.1) | async-done | bytes 133152 | tf_op jit(solution)/shard_map/all_to_all | solution.py:155
  74.0 9.4 %all-gather.2 = f32[64,2048]{1,0:T(8,128)S(1)} all-gather(f32[16,2048]{1,0:T(8,128)S(1)} %fusion.50), channel_id=4, replica_groups=mesh['seq'=4,'exp'=8] {'seq'}, dimensions={0}, use_global_device_ids=true | all-gather | bytes 655360 | tf_op jit(solution)/shard_map/all_gather | solution.py:189
  83.7 15.0 %all_gather.39 = bf16[128,2048]{1,0:T(8,128)(2,1)S(1)} all-gather(bf16[16,2048]{1,0:T(8,128)(2,1)S(1)} %multiply_convert_fusion), channel_id=1, replica_groups=mesh['seq'=4,'exp'=8] {'exp'}, dimensions={0}, use_global_device_ids=true | all-gather | bytes 589824 | tf_op jit(solution)/shard_map/all_gather | solution.py:191
  99.0 6.1 %convolution_bitcast_fusion.2 = f32[8,128,352]{1,2,0:T(8,128)S(1)} fusion(bf16[8,2048,352]{1,2,0:T(8,128)(2,1)} %param.36, bf16[128,2048]{1,0:T(8,128)(2,1)S(1)} %all_gather.39), kind=kOutput, calls=%fused_computation.11 | convolution fusion | flops 1476395008 | bytes 13500416 | tf_op jit(solution)/shard_map/nd,jdf->jnf/dot_general | solution.py:209
  105.9 14.7 %convolution_bitcast_fusion = f32[128,2048]{1,0:T(8,128)S(1)} fusion(bf16[8,352,2048]{2,1,0:T(8,128)(2,1)} %param.38, bf16[8,2048,352]{1,2,0:T(8,128)(2,1)} %param.37, f32[8,128,352]{1,2,0:T(8,128)S(1)} %convolution_bitcast_fusion.2, f32[8,128]{1,0:T(8,128)S(1)} %select_reduce_fusion.4, bf16[128,2048]{1,0:T(8,128)(2,1)S(1)} %all_gather.39), kind=kOutput, calls=%fused_computation.7 | convolution fusion | flops 2955313152 | bytes 26087424 | tf_op jit(solution)/shard_map/jnf,jfd->nd/dot_general | solution.py:214
  120.6 2.9 %fusion.6 = f32[128,2048]{1,0:T(8,128)S(1)} fusion(f32[128,2048]{1,0:T(8,128)S(1)} %convolution_bitcast_fusion, s32[]{:T(128)S(6)} %select_n.84, bf16[352,2048]{1,0:T(8,128)(2,1)} %param.41, bf16[2048,352]{0,1:T(8,128)(2,1)} %param.40, bf16[128,2048]{1,0:T(8,128)(2,1)S(1)} %all_gather.39, f32[32,352]{1,0:T(8,128)S(1)} %fusion.37), kind=kOutput, calls=%fused_computation.9 | convolution fusion | flops 92407808 | bytes 3589120 | tf_op jit(solution)/shard_map/dot_general | solution.py:224
  125.3 3.3 %all-to-all-start.2 = ((bf16[32,4,2048]{2,1,0:T(4,128)(2,1)}), bf16[32,4,2048]{2,1,0:T(4,128)(2,1)S(1)}, u32[]{:S(2)}, u32[]{:S(2)}) async-start(bf16[32,4,2048]{2,1,0:T(4,128)(2,1)} %copy.164), calls=%async_computation.2 | async-start | bytes 1048576 | tf_op jit(solution)/shard_map/all_to_all | solution.py:234
  128.6 16.4 %all-to-all-done.2 = bf16[32,4,2048]{2,1,0:T(4,128)(2,1)S(1)} async-done(((bf16[32,4,2048]{2,1,0:T(4,128)(2,1)}), bf16[32,4,2048]{2,1,0:T(4,128)(2,1)S(1)}, u32[]{:S(2)}, u32[]{:S(2)}) %all-to-all-start.2) | async-done | bytes 524320 | tf_op jit(solution)/shard_map/all_to_all | solution.py:234
  145.4 14.0 %all-gather.5 = bf16[8,4,2048]{2,1,0:T(4,128)(2,1)S(1)} all-gather(bf16[1,4,2048]{2,1,0:T(4,128)(2,1)S(1)} %fusion.49), channel_id=5, replica_groups=mesh['seq'=4,'exp'=8] {'exp'}, dimensions={0}, use_global_device_ids=true | all-gather | bytes 147456 | tf_op jit(solution)/shard_map/all_gather | solution.py:36
  159.3 9.4 %all-gather.4 = bf16[32,4,2048]{2,1,0:T(4,128)(2,1)S(1)} all-gather(bf16[8,4,2048]{2,1,0:T(4,128)(2,1)S(1)} %all-gather.5), channel_id=6, replica_groups=mesh['seq'=4,'exp'=8] {'seq'}, dimensions={0}, use_global_device_ids=true | all-gather | bytes 655360 | tf_op jit(solution)/shard_map/all_gather | solution.py:37
  168.9 4.9 %convolution_reduce_fusion = f32[128]{0:T(128)S(1)} fusion(bf16[128,2048]{1,0:T(8,128)(2,1)S(1)} %reshape.556, bf16[2048,1600]{0,1:T(8,128)(2,1)} %param.43), kind=kOutput, calls=%fused_computation.15 | convolution fusion | flops 839065472 | bytes 7078400 | tf_op jit(solution)/shard_map/dot_general | solution.py:248
  173.8 9.3 %all_to_all.31 = f32[32,1,132]{2,1,0:T(1,128)S(1)} all-to-all(f32[32,1,132]{2,1,0:T(1,128)S(1)} %broadcast_in_dim.145), channel_id=1, replica_groups=mesh['seq'=4,'exp'=8] {'seq','exp'}, dimensions={0} | all-to-all | bytes 33792 | tf_op jit(solution)/shard_map/all_to_all | solution.py:250
  (121 shorter events, 17.5 us)
Async XLA Ops:
  0.6 72.9 %copy-start = (bf16[512,2048]{1,0:T(8,128)(2,1)S(1)}, bf16[512,2048]{1,0:T(8,128)(2,1)}, u32[]{:S(2)}) copy-start(bf16[512,2048]{1,0:T(8,128)(2,1)} %param.31) | copy-start | bytes 6291460
  7.6 7.9 %copy-start.9 = (s32[32]{0:T(128)S(1)}, s32[32]{0:T(128)}, u32[]{:S(2)}) copy-start(s32[32]{0:T(128)} %param.23) | copy-start | bytes 388
  9.1 21.7 %all-to-all-start = ((bf16[8,4,4,2048]{3,2,1,0:T(4,128)(2,1)}), bf16[8,4,4,2048]{3,2,1,0:T(4,128)(2,1)S(1)}, u32[]{:S(2)}, u32[]{:S(2)}) async-start(bf16[8,4,4,2048]{3,2,1,0:T(4,128)(2,1)} %select_select_fusion), calls=%async_computation | async-start | bytes 1048576 | tf_op jit(solution)/shard_map/all_to_all | solution.py:94
  24.3 4.2 %copy-start.5 = (s32[4,32,6]{1,0,2:T(4,128)S(1)}, s32[4,32,6]{1,0,2:T(4,128)}, u32[]{:S(2)}) copy-start(s32[4,32,6]{1,0,2:T(4,128)} %param.25) | copy-start | bytes 9220
  28.3 12.1 %copy-start.6 = (f32[2048]{0:T(1024)S(1)}, f32[2048]{0:T(1024)}, u32[]{:S(2)}) copy-start(f32[2048]{0:T(1024)} %param.27) | copy-start | bytes 24580
  40.5 2.4 %copy-start.2 = (bf16[512,2048]{1,0:T(8,128)(2,1)S(1)}, bf16[512,2048]{1,0:T(8,128)(2,1)}, u32[]{:S(2)}) copy-start(bf16[512,2048]{1,0:T(8,128)(2,1)} %copy.167) | copy-start | bytes 6291460
  63.8 8.3 %all-to-all-start.1 = ((f32[4,1,8320]{2,1,0:T(1,128)}), f32[4,1,8320]{2,1,0:T(1,128)S(1)}, u32[]{:S(2)}, u32[]{:S(2)}) async-start(f32[4,1,8320]{2,1,0:T(1,128)} %copy.149), calls=%async_computation.1 | async-start | bytes 266240 | tf_op jit(solution)/shard_map/all_to_all | solution.py:155
  73.5 10.1 %copy-start.7 = (f32[2048]{0:T(1024)S(1)}, f32[2048]{0:T(1024)}, u32[]{:S(2)}) copy-start(f32[2048]{0:T(1024)} %param.34) | copy-start | bytes 24580
  73.6 25.2 %copy-start.4 = (bf16[2048,64]{0,1:T(8,128)(2,1)S(1)}, bf16[2048,64]{0,1:T(8,128)(2,1)}, u32[]{:S(2)}) copy-start(bf16[2048,64]{0,1:T(8,128)(2,1)} %param.35) | copy-start | bytes 786436
  99.0 6.3 %copy-start.3 = (bf16[2048,352]{0,1:T(8,128)(2,1)S(1)}, bf16[2048,352]{0,1:T(8,128)(2,1)}, u32[]{:S(2)}) copy-start(bf16[2048,352]{0,1:T(8,128)(2,1)} %param.39) | copy-start | bytes 4325380
  123.8 21.5 %copy-start.8 = (f32[2048]{0:T(1024)S(1)}, f32[2048]{0:T(1024)}, u32[]{:S(2)}) copy-start(f32[2048]{0:T(1024)} %param.42) | copy-start | bytes 24580
  125.3 19.6 %all-to-all-start.2 = ((bf16[32,4,2048]{2,1,0:T(4,128)(2,1)}), bf16[32,4,2048]{2,1,0:T(4,128)(2,1)S(1)}, u32[]{:S(2)}, u32[]{:S(2)}) async-start(bf16[32,4,2048]{2,1,0:T(4,128)(2,1)} %copy.164), calls=%async_computation.2 | async-start | bytes 1048576 | tf_op jit(solution)/shard_map/all_to_all | solution.py:234
  168.8 15.6 %copy-start.1 = (bf16[512,2048]{1,0:T(8,128)(2,1)S(1)}, bf16[512,2048]{1,0:T(8,128)(2,1)}, u32[]{:S(2)}) copy-start(bf16[512,2048]{1,0:T(8,128)(2,1)} %param.31) | copy-start | bytes 6291460

commit v4 on v3

--- a/solution.py
+++ b/solution.py
@@ -3,6 +3,8 @@
 import jax
 import jax.numpy as jnp
 from jax import lax
+from jax.experimental import pallas as pl
+from jax.experimental.pallas import tpu as pltpu
 from jax.sharding import PartitionSpec as P
 
 HDIM = 128
@@ -35,6 +37,67 @@
 def gather_all(values):
     inner = lax.all_gather(values, "exp", axis=0, tiled=False)
     return lax.all_gather(inner, "seq", axis=0, tiled=False)
+
+
+def experts_kernel(pieces, x_ref, weight_ref, gate_ref, up_ref, down_ref, sgate_ref, sup_ref, sdown_ref, mask_ref, out_ref):
+    step = pl.program_id(0)
+
+    @pl.when(step == 0)
+    def _():
+        out_ref[...] = jnp.zeros_like(out_ref)
+
+    def one_piece(gate, up, down, scale):
+        rows = x_ref[...]
+        along = (((1,), (1,)), ((), ()))
+        gate_out = lax.dot_general(rows, gate, along, preferred_element_type=jnp.float32)
+        up_out = lax.dot_general(rows, up, along, preferred_element_type=jnp.float32)
+        hidden = (gate_out * jax.nn.sigmoid(gate_out) * up_out * scale).astype(jnp.bfloat16)
+        out_ref[...] += jnp.dot(hidden, down, preferred_element_type=jnp.float32)
+
+    @pl.when(step < pieces)
+    def _():
+        one_piece(gate_ref[0], up_ref[0], down_ref[0], weight_ref[0])
+
+    @pl.when(step == pieces)
+    def _():
+        one_piece(sgate_ref[...], sup_ref[...], sdown_ref[...], mask_ref[...])
+
+
+def experts(rows, token_weight, gate_pieces, up_pieces, down_pieces, shared_gate, shared_up, shared_down, shared_mask):
+    gate_pieces = jnp.swapaxes(gate_pieces, 1, 2)
+    up_pieces = jnp.swapaxes(up_pieces, 1, 2)
+    shared_gate = shared_gate.T
+    shared_up = shared_up.T
+    pieces, units, width = gate_pieces.shape
+    count = rows.shape[0]
+    last = pieces - 1
+
+    def piece_map(step):
+        return (jnp.minimum(step, last), 0, 0)
+
+    weight_bytes = 2 * 3 * width * (pieces * units + shared_gate.shape[0])
+    return pl.pallas_call(
+        lambda *refs: experts_kernel(pieces, *refs),
+        grid=(pieces + 1,),
+        in_specs=[
+            pl.BlockSpec((count, width), lambda step: (0, 0)),
+            pl.BlockSpec((1, count, 1), piece_map),
+            pl.BlockSpec((1, units, width), piece_map),
+            pl.BlockSpec((1, units, width), piece_map),
+            pl.BlockSpec((1, units, width), piece_map),
+            pl.BlockSpec(shared_gate.shape, lambda step: (0, 0)),
+            pl.BlockSpec(shared_up.shape, lambda step: (0, 0)),
+            pl.BlockSpec(shared_down.shape, lambda step: (0, 0)),
+            pl.BlockSpec((count, 1), lambda step: (0, 0)),
+        ],
+        out_specs=pl.BlockSpec((count, width), lambda step: (0, 0)),
+        out_shape=jax.ShapeDtypeStruct((count, width), jnp.float32),
+        cost_estimate=pl.CostEstimate(
+            flops=6 * count * width * (pieces * units + shared_gate.shape[0]),
+            transcendentals=count * (pieces * units + shared_gate.shape[0]),
+            bytes_accessed=weight_bytes + 2 * count * width + 4 * count * width,
+        ),
+    )(rows, token_weight[:, :, None], gate_pieces, up_pieces, down_pieces, shared_gate, shared_up, shared_down, shared_mask)
 
 
 def on_device(
@@ -206,27 +269,15 @@
         ),
         axis=2,
     )
-    gate_out = jnp.einsum("nd,jdf->jnf", moe_in, gate_pieces, preferred_element_type=jnp.float32)
-    up_out = jnp.einsum("nd,jdf->jnf", moe_in, up_pieces, preferred_element_type=jnp.float32)
-    weighted_hidden = (jax.nn.silu(gate_out) * up_out * token_weight[:, :, None]).astype(
-        jnp.bfloat16
-    )
-    routed = jnp.einsum(
-        "jnf,jfd->nd", weighted_hidden, down_pieces, preferred_element_type=jnp.float32
-    )
     share_count = tokens // n_seq
     share_start = seq_index * share_count
-    share_rows = lax.dynamic_slice_in_dim(moe_in, share_start, share_count, 0)
-    shared_hidden = (
-        jax.nn.silu(jnp.dot(share_rows, shared_gate, preferred_element_type=jnp.float32))
-        * jnp.dot(share_rows, shared_up, preferred_element_type=jnp.float32)
-    ).astype(jnp.bfloat16)
-    shared_out = jnp.dot(shared_hidden, shared_down, preferred_element_type=jnp.float32)
-    term_rows = lax.dynamic_update_slice_in_dim(
-        routed,
-        lax.dynamic_slice_in_dim(routed, share_start, share_count, 0) + shared_out,
-        share_start,
-        0,
+    token_place = jnp.arange(tokens, dtype=jnp.int32)
+    shared_mask = (
+        (token_place >= share_start) & (token_place < share_start + share_count)
+    ).astype(jnp.float32)[:, None]
+    term_rows = experts(
+        moe_in, token_weight, gate_pieces, up_pieces, down_pieces,
+        shared_gate, shared_up, shared_down, shared_mask,
     )
 
     term_rows = jnp.swapaxes(term_rows.reshape(n_exp, n_seq, share, width), 0, 1)

time: 185 us -> 180 us (0.973)
  matrix products: 42 us -> 13.4 us
  Pallas kernels: 0 us -> 21.1 us
    dot_general x4 -> x0, matrix products: 24.3 us -> none  [the longest x1 14.7 us: on_device(): jnp.einsum('jnf,jfd->nd', weighted_hidden, down_pieces, preferred_element...]
    pallas_call x0 -> x1, Pallas kernels: none -> 21.1 us  [experts(): pl.pallas_call(lambda *refs: experts_kernel(pieces, *refs), grid=(pieces...]
    dot_general x1, matrix products: 3.45 us -> 1.27 us  [on_device(): jnp.einsum('trhd,rphd->trhp', queries, cache_keys, preferred_element_type...]
    dot_general x1, matrix products: 2.9 us -> 0.71 us  [on_device(): jnp.einsum('trhp,rphd->trhd', local_weights.astype(jnp.bfloat16), cache_v...]
  transfers between devices with their start and end apart: 3 -> 3, of which waited for: 3 -> 3; matrix products, arithmetic and copies ran while one was open for 7% -> 8% of each run, Pallas kernels for 0% -> 0%
where the time goes in v4:
time: 180 us; the launch traced here: 179 us
  blocking collectives  75.2 us (42%)
  local copies, waits for them, and re-layouts  25.3 us (14%)
  waiting for transfers between devices  21.9 us (12%)
  Pallas kernels  21.1 us (12%)
  starting transfers between devices  13.4 us (7%)
  matrix products  13.4 us (7%)
  other arithmetic  7.97 us (4%)
    pallas_call x1, Pallas kernels, experts(): pl.pallas_call(lambda *refs: experts_kernel(pieces, *refs), grid=(pieces...  21.1 us
    all_to_all x1, waiting for transfers between devices, on_device(): lax.all_to_all(term_rows.reshape(n_dev, share, width).astype(jnp.bfloat16...  16.4 us
    all_gather x1, blocking collectives, on_device(): lax.all_gather(rms_scale(resid_group, moe_gain).astype(jnp.bfloat16), 'ex...  15.1 us
    all_gather x1, blocking collectives, gather_all(): inner = lax.all_gather(values, 'exp', axis=0, tiled=False)  14 us
    dot_general x3, local copies, waits for them, and re-layouts, project(): jnp.dot(attn_in, weight, preferred_element_type=jnp.float32)  11.9 us
    all_gather x1, blocking collectives, on_device(): lax.all_gather(attn_part, 'seq', axis=0, tiled=False)  9.45 us
    all_gather x1, blocking collectives, gather_all(): return lax.all_gather(inner, 'seq', axis=0, tiled=False)  9.37 us
    all_to_all x1, blocking collectives, on_device(): lax.all_to_all(jnp.broadcast_to(message[None, :], (n_dev, message.shape[0...  9.32 us
  transfers between devices with their start and end apart: 3, of which 3 were waited for; matrix products, arithmetic and copies ran while one was open for 8% of the time, Pallas kernels for 0%

profile of v4, /device:TPU:0, one launch (start us, length us, event | category | flops | bytes accessed | tf_op | source)
XLA Modules:
  0.0 179.4 jit_solution(7493331889798530650)
XLA Ops:
  2.4 5.1 %gather_fusion = bf16[128,2048]{1,0:T(8,128)(2,1)S(1)} fusion(bf16[1600,2048]{1,0:T(8,128)(2,1)} %param.26, s32[1024]{0:T(1024)S(1)} %pad_clamp_fusion), kind=kCustom, calls=%fused_computation | custom fusion | bytes 1049088 | tf_op jit(solution)/shard_map/jit(_take)/gather | solution.py:155
  7.9 1.2 select_select_fusion
  9.1 6.3 %all-to-all-start = ((bf16[8,4,4,2048]{3,2,1,0:T(4,128)(2,1)}), bf16[8,4,4,2048]{3,2,1,0:T(4,128)(2,1)S(1)}, u32[]{:S(2)}, u32[]{:S(2)}) async-start(bf16[8,4,4,2048]{3,2,1,0:T(4,128)(2,1)} %select_select_fusion), calls=%async_computation | async-start | bytes 1048576 | tf_op jit(solution)/shard_map/all_to_all | solution.py:157
  16.5 4.0 %copy.205 = bf16[512,2048]{1,0:T(8,128)(2,1)} copy(bf16[512,2048]{0,1:T(8,128)(2,1)} %bitcast.134) | data formatting | bytes 4194304 | tf_op jit(solution)/shard_map/dot_general | solution.py:168
  20.5 4.0 %copy.203 = bf16[512,2048]{1,0:T(8,128)(2,1)} copy(bf16[512,2048]{0,1:T(8,128)(2,1)} %bitcast.135) | data formatting | bytes 4194304 | tf_op jit(solution)/shard_map/dot_general | solution.py:168
  24.6 3.9 %copy.204 = bf16[512,2048]{1,0:T(8,128)(2,1)} copy(bf16[512,2048]{0,1:T(8,128)(2,1)} %bitcast.136) | data formatting | bytes 4194304 | tf_op jit(solution)/shard_map/dot_general | solution.py:168
  31.1 9.0 %all-gather = bf16[16,4,2048]{2,1,0:T(4,128)(2,1)S(1)} all-gather(bf16[4,4,2048]{2,1,0:T(4,128)(2,1)S(1)} %reduce_sum.137), channel_id=2, replica_groups=mesh['seq'=4,'exp'=8] {'seq'}, dimensions={0}, use_global_device_ids=true | all-gather | bytes 327680 | tf_op jit(solution)/shard_map/all_gather | solution.py:159
  40.5 2.4 %convolution_convert_fusion = bf16[16,4,128]{2,0,1:T(8,128)(2,1)S(1)} fusion(bf16[16,2048,1]{1,0,2:T(8,128)(2,1)S(1)} %reshape.595, bf16[4,128,2048]{2,1,0:T(8,128)(2,1)} %bitcast.131), kind=kOutput, calls=%fused_computation.21 | convolution fusion | flops 33562624 | bytes 2179072 | tf_op jit(solution)/shard_map/dot_general | solution.py:168
  42.9 2.3 %fusion.51 = f32[16,4,128]{2,0,1:T(8,128)S(1)} fusion(bf16[16,2048,1]{1,0,2:T(8,128)(2,1)S(1)} %reshape.595, bf16[4,128,2048]{2,1,0:T(8,128)(2,1)} %bitcast.130), kind=kOutput, calls=%fused_computation.111 | convolution fusion | flops 33554432 | bytes 2195456 | tf_op jit(solution)/shard_map/dot_general | solution.py:168
  46.1 9.0 %all-gather.1 = bf16[12,16,4,128]{3,1,2,0:T(8,128)(2,1)S(1)} all-gather(bf16[3,16,4,128]{3,1,2,0:T(8,128)(2,1)S(1)} %pad_maximum_fusion), channel_id=3, replica_groups=mesh['seq'=4,'exp'=8] {'seq'}, dimensions={0}, use_global_device_ids=true | all-gather | bytes 245760 | tf_op jit(solution)/shard_map/all_gather | solution.py:175
  55.2 1.3 select_reduce_fusion
  59.1 3.3 %all-to-all-start.1 = ((f32[4,1,8320]{2,1,0:T(1,128)}), f32[4,1,8320]{2,1,0:T(1,128)S(1)}, u32[]{:S(2)}, u32[]{:S(2)}) async-start(f32[4,1,8320]{2,1,0:T(1,128)} %copy.184), calls=%async_computation.1 | async-start | bytes 266240 | tf_op jit(solution)/shard_map/all_to_all | solution.py:218
  63.0 4.4 %all-to-all-done.1 = f32[4,1,8320]{2,1,0:T(1,128)S(1)} async-done(((f32[4,1,8320]{2,1,0:T(1,128)}), f32[4,1,8320]{2,1,0:T(1,128)S(1)}, u32[]{:S(2)}, u32[]{:S(2)}) %all-to-all-start.1) | async-done | bytes 133152 | tf_op jit(solution)/shard_map/all_to_all | solution.py:218
  69.3 9.4 %all-gather.2 = f32[64,2048]{1,0:T(8,128)S(1)} all-gather(f32[16,2048]{1,0:T(8,128)S(1)} %fusion.34), channel_id=4, replica_groups=mesh['seq'=4,'exp'=8] {'seq'}, dimensions={0}, use_global_device_ids=true | all-gather | bytes 655360 | tf_op jit(solution)/shard_map/all_gather | solution.py:252
  79.0 15.1 %all_gather.39.refs_0_ = bf16[128,2048]{1,0:T(8,128)(2,1)S(1)} all-gather(bf16[16,2048]{1,0:T(8,128)(2,1)S(1)} %multiply_convert_fusion), channel_id=1, replica_groups=mesh['seq'=4,'exp'=8] {'exp'}, dimensions={0}, use_global_device_ids=true | all-gather | bytes 589824 | tf_op jit(solution)/shard_map/all_gather | solution.py:254
  95.7 21.1 %shard_map.221 = f32[128,2048]{1,0:T(8,128)} custom-call(bf16[128,2048]{1,0:T(8,128)(2,1)} %copy-done.3, f32[8,128,1]{2,1,0:T(8,128)} %copy.199.refs_1_, bf16[8,352,2048]{2,1,0:T(8,128)(2,1)} %bitcast.128, bf16[8,352,2048]{2,1,0:T(8,128)(2,1)} %bitcast.129, bf16[8,352,2048]{2,1,0:T(8,128)(2,1)} %refs_4_.1, bf16[352,2048]{1,0:T(8,128)(2,1)} %bitcast.138, ...), custom_call_target="tpu_custom_call" | custom-call | flops 4982833152 | bytes 40501248 | tf_op jit(solution)/shard_map/pallas_call | solution.py:79
  116.8 1.3 convert_element_type.108
  118.6 1.2 copy.201
  119.8 3.7 %all-to-all-start.2 = ((bf16[32,4,2048]{2,1,0:T(4,128)(2,1)}), bf16[32,4,2048]{2,1,0:T(4,128)(2,1)S(1)}, u32[]{:S(2)}, u32[]{:S(2)}) async-start(bf16[32,4,2048]{2,1,0:T(4,128)(2,1)} %copy.201), calls=%async_computation.2 | async-start | bytes 1048576 | tf_op jit(solution)/shard_map/all_to_all | solution.py:285
  123.5 16.4 %all-to-all-done.2 = bf16[32,4,2048]{2,1,0:T(4,128)(2,1)S(1)} async-done(((bf16[32,4,2048]{2,1,0:T(4,128)(2,1)}), bf16[32,4,2048]{2,1,0:T(4,128)(2,1)S(1)}, u32[]{:S(2)}, u32[]{:S(2)}) %all-to-all-start.2) | async-done | bytes 524320 | tf_op jit(solution)/shard_map/all_to_all | solution.py:285
  140.3 14.0 %all-gather.5 = bf16[8,4,2048]{2,1,0:T(4,128)(2,1)S(1)} all-gather(bf16[1,4,2048]{2,1,0:T(4,128)(2,1)S(1)} %fusion.33), channel_id=5, replica_groups=mesh['seq'=4,'exp'=8] {'exp'}, dimensions={0}, use_global_device_ids=true | all-gather | bytes 147456 | tf_op jit(solution)/shard_map/all_gather | solution.py:38
  154.3 9.4 %all-gather.4 = bf16[32,4,2048]{2,1,0:T(4,128)(2,1)S(1)} all-gather(bf16[8,4,2048]{2,1,0:T(4,128)(2,1)S(1)} %all-gather.5), channel_id=6, replica_groups=mesh['seq'=4,'exp'=8] {'seq'}, dimensions={0}, use_global_device_ids=true | all-gather | bytes 655360 | tf_op jit(solution)/shard_map/all_gather | solution.py:39
  163.8 4.9 %convolution_reduce_fusion = f32[128]{0:T(128)S(1)} fusion(bf16[128,2048]{1,0:T(8,128)(2,1)S(1)} %reshape.574, bf16[2048,1600]{0,1:T(8,128)(2,1)} %param.43), kind=kOutput, calls=%fused_computation.7 | convolution fusion | flops 839065472 | bytes 7078400 | tf_op jit(solution)/shard_map/dot_general | solution.py:299
  168.7 9.3 %all_to_all.31 = f32[32,1,132]{2,1,0:T(1,128)S(1)} all-to-all(f32[32,1,132]{2,1,0:T(1,128)S(1)} %broadcast_in_dim.149), channel_id=1, replica_groups=mesh['seq'=4,'exp'=8] {'seq','exp'}, dimensions={0} | all-to-all | bytes 33792 | tf_op jit(solution)/shard_map/all_to_all | solution.py:301
  (124 shorter events, 16.2 us)
Async XLA Ops:
  0.6 68.2 %copy-start = (bf16[512,2048]{1,0:T(8,128)(2,1)S(1)}, bf16[512,2048]{1,0:T(8,128)(2,1)}, u32[]{:S(2)}) copy-start(bf16[512,2048]{1,0:T(8,128)(2,1)} %param.31) | copy-start | bytes 6291460
  0.6 14.8 %copy-start.11 = (s32[32]{0:T(128)S(1)}, s32[32]{0:T(128)}, u32[]{:S(2)}) copy-start(s32[32]{0:T(128)} %param.23) | copy-start | bytes 388
  9.1 21.7 %all-to-all-start = ((bf16[8,4,4,2048]{3,2,1,0:T(4,128)(2,1)}), bf16[8,4,4,2048]{3,2,1,0:T(4,128)(2,1)S(1)}, u32[]{:S(2)}, u32[]{:S(2)}) async-start(bf16[8,4,4,2048]{3,2,1,0:T(4,128)(2,1)} %select_select_fusion), calls=%async_computation | async-start | bytes 1048576 | tf_op jit(solution)/shard_map/all_to_all | solution.py:157
  20.5 8.0 %copy-start.5 = (s32[4,32,6]{1,0,2:T(4,128)S(1)}, s32[4,32,6]{1,0,2:T(4,128)}, u32[]{:S(2)}) copy-start(s32[4,32,6]{1,0,2:T(4,128)} %param.25) | copy-start | bytes 9220
  24.5 15.9 %copy-start.6 = (f32[2048]{0:T(1024)S(1)}, f32[2048]{0:T(1024)}, u32[]{:S(2)}) copy-start(f32[2048]{0:T(1024)} %param.27) | copy-start | bytes 24580
  40.5 4.7 %copy-start.2 = (bf16[512,2048]{1,0:T(8,128)(2,1)S(1)}, bf16[512,2048]{1,0:T(8,128)(2,1)}, u32[]{:S(2)}) copy-start(bf16[512,2048]{1,0:T(8,128)(2,1)} %copy.204) | copy-start | bytes 6291460
  40.5 14.6 %copy-start.9 = (bf16[4,256,2048]{2,1,0:T(8,128)(2,1)S(1)}, bf16[4,256,2048]{2,1,0:T(8,128)(2,1)}, u32[]{:S(2)}) copy-start(bf16[4,256,2048]{2,1,0:T(8,128)(2,1)} %param.32) | copy-start | bytes 12582916
  45.2 11.5 %copy-start.10 = (bf16[4,256,2048]{2,1,0:T(8,128)(2,1)S(1)}, bf16[4,256,2048]{2,1,0:T(8,128)(2,1)}, u32[]{:S(2)}) copy-start(bf16[4,256,2048]{2,1,0:T(8,128)(2,1)} %param.33) | copy-start | bytes 12582916
  57.5 21.4 %copy-start.7 = (f32[2048]{0:T(1024)S(1)}, f32[2048]{0:T(1024)}, u32[]{:S(2)}) copy-start(f32[2048]{0:T(1024)} %param.34) | copy-start | bytes 24580
  57.5 36.6 %copy-start.4 = (bf16[2048,64]{0,1:T(8,128)(2,1)S(1)}, bf16[2048,64]{0,1:T(8,128)(2,1)}, u32[]{:S(2)}) copy-start(bf16[2048,64]{0,1:T(8,128)(2,1)} %param.35) | copy-start | bytes 786436
  59.1 8.3 %all-to-all-start.1 = ((f32[4,1,8320]{2,1,0:T(1,128)}), f32[4,1,8320]{2,1,0:T(1,128)S(1)}, u32[]{:S(2)}, u32[]{:S(2)}) async-start(f32[4,1,8320]{2,1,0:T(1,128)} %copy.184), calls=%async_computation.1 | async-start | bytes 266240 | tf_op jit(solution)/shard_map/all_to_all | solution.py:218
  94.1 1.5 copy-start.3
  116.8 23.4 %copy-start.8 = (f32[2048]{0:T(1024)S(1)}, f32[2048]{0:T(1024)}, u32[]{:S(2)}) copy-start(f32[2048]{0:T(1024)} %param.42) | copy-start | bytes 24580
  119.8 20.1 %all-to-all-start.2 = ((bf16[32,4,2048]{2,1,0:T(4,128)(2,1)}), bf16[32,4,2048]{2,1,0:T(4,128)(2,1)S(1)}, u32[]{:S(2)}, u32[]{:S(2)}) async-start(bf16[32,4,2048]{2,1,0:T(4,128)(2,1)} %copy.201), calls=%async_computation.2 | async-start | bytes 1048576 | tf_op jit(solution)/shard_map/all_to_all | solution.py:285
  163.7 15.7 %copy-start.1 = (bf16[512,2048]{1,0:T(8,128)(2,1)S(1)}, bf16[512,2048]{1,0:T(8,128)(2,1)}, u32[]{:S(2)}) copy-start(bf16[512,2048]{1,0:T(8,128)(2,1)} %param.31) | copy-start | bytes 6291460

commit v5 on v4

--- a/solution.py
+++ b/solution.py
@@ -39,7 +39,7 @@
     return lax.all_gather(inner, "seq", axis=0, tiled=False)
 
 
-def experts_kernel(pieces, x_ref, weight_ref, gate_ref, up_ref, down_ref, sgate_ref, sup_ref, sdown_ref, mask_ref, out_ref):
+def experts_kernel(pieces, x_ref, weight_ref, gate_ref, up_ref, down_ref, sgate_ref, sup_ref, sdown_ref, out_ref):
     step = pl.program_id(0)
 
     @pl.when(step == 0)
@@ -54,16 +54,20 @@
         hidden = (gate_out * jax.nn.sigmoid(gate_out) * up_out * scale).astype(jnp.bfloat16)
         out_ref[...] += jnp.dot(hidden, down, preferred_element_type=jnp.float32)
 
+    table = weight_ref[...]
+    column = lax.broadcasted_iota(jnp.int32, table.shape, 1)
+    scale = jnp.sum(jnp.where(column == step, table, 0.0), axis=1, keepdims=True)
+
     @pl.when(step < pieces)
     def _():
-        one_piece(gate_ref[0], up_ref[0], down_ref[0], weight_ref[0])
+        one_piece(gate_ref[0], up_ref[0], down_ref[0], scale)
 
     @pl.when(step == pieces)
     def _():
-        one_piece(sgate_ref[...], sup_ref[...], sdown_ref[...], mask_ref[...])
-
-
-def experts(rows, token_weight, gate_pieces, up_pieces, down_pieces, shared_gate, shared_up, shared_down, shared_mask):
+        one_piece(sgate_ref[...], sup_ref[...], sdown_ref[...], scale)
+
+
+def experts(rows, weight_table, gate_pieces, up_pieces, down_pieces, shared_gate, shared_up, shared_down):
     gate_pieces = jnp.swapaxes(gate_pieces, 1, 2)
     up_pieces = jnp.swapaxes(up_pieces, 1, 2)
     shared_gate = shared_gate.T
@@ -81,14 +85,13 @@
         grid=(pieces + 1,),
         in_specs=[
             pl.BlockSpec((count, width), lambda step: (0, 0)),
-            pl.BlockSpec((1, count, 1), piece_map),
+            pl.BlockSpec(weight_table.shape, lambda step: (0, 0)),
             pl.BlockSpec((1, units, width), piece_map),
             pl.BlockSpec((1, units, width), piece_map),
             pl.BlockSpec((1, units, width), piece_map),
             pl.BlockSpec(shared_gate.shape, lambda step: (0, 0)),
             pl.BlockSpec(shared_up.shape, lambda step: (0, 0)),
             pl.BlockSpec(shared_down.shape, lambda step: (0, 0)),
-            pl.BlockSpec((count, 1), lambda step: (0, 0)),
         ],
         out_specs=pl.BlockSpec((count, width), lambda step: (0, 0)),
         out_shape=jax.ShapeDtypeStruct((count, width), jnp.float32),
@@ -97,7 +100,7 @@
             transcendentals=count * (pieces * units + shared_gate.shape[0]),
             bytes_accessed=weight_bytes + 2 * count * width + 4 * count * width,
         ),
-    )(rows, token_weight[:, :, None], gate_pieces, up_pieces, down_pieces, shared_gate, shared_up, shared_down, shared_mask)
+    )(rows, weight_table, gate_pieces, up_pieces, down_pieces, shared_gate, shared_up, shared_down)
 
 
 def on_device(
@@ -249,7 +252,8 @@
     )
 
     attn_part = jnp.dot(own_heads, w_out, preferred_element_type=jnp.float32)
-    resid_group = embedded + jnp.sum(lax.all_gather(attn_part, "seq", axis=0, tiled=False), axis=0)
+    attn_parts = lax.all_gather(attn_part.astype(jnp.bfloat16), "seq", axis=0, tiled=False)
+    resid_group = embedded + jnp.sum(attn_parts.astype(jnp.float32), axis=0)
     resid_share = lax.dynamic_slice_in_dim(resid_group, seq_index * share, share, 0)
     moe_in = lax.all_gather(
         rms_scale(resid_group, moe_gain).astype(jnp.bfloat16), "exp", axis=0, tiled=True
@@ -265,9 +269,9 @@
     row_expert = (owner_index * rows_here + jnp.arange(rows_here, dtype=jnp.int32)) // PIECES
     token_weight = jnp.sum(
         jnp.where(
-            chosen_ids[None, :, :] == row_expert[:, None, None], gate_weights[None, :, :], 0.0
+            chosen_ids[:, :, None] == row_expert[None, None, :], gate_weights[:, :, None], 0.0
         ),
-        axis=2,
+        axis=1,
     )
     share_count = tokens // n_seq
     share_start = seq_index * share_count
@@ -275,9 +279,13 @@
     shared_mask = (
         (token_place >= share_start) & (token_place < share_start + share_count)
     ).astype(jnp.float32)[:, None]
+    lanes = -(-(rows_here + 1) // 128) * 128
+    weight_table = jnp.pad(
+        jnp.concatenate([token_weight, shared_mask], axis=1), ((0, 0), (0, lanes - rows_here - 1))
+    )
     term_rows = experts(
-        moe_in, token_weight, gate_pieces, up_pieces, down_pieces,
-        shared_gate, shared_up, shared_down, shared_mask,
+        moe_in, weight_table, gate_pieces, up_pieces, down_pieces,
+        shared_gate, shared_up, shared_down,
     )
 
     term_rows = jnp.swapaxes(term_rows.reshape(n_exp, n_seq, share, width), 0, 1)
@@ -293,10 +301,20 @@
     )
     final_share = resid_share + term_sum
     norms_share = jnp.sqrt(jnp.mean(final_share * final_share, axis=-1))
-    head_in = gather_all(rms_scale(final_share, final_gain).astype(jnp.bfloat16)).reshape(
-        tokens, width
-    )
-    local_best = jnp.max(jnp.dot(head_in, w_head, preferred_element_type=jnp.float32), axis=-1)
+    head_share = rms_scale(final_share, final_gain).astype(jnp.bfloat16)
+    rounds = n_exp.bit_length() - 1
+    if n_exp == 1 << rounds:
+        for level in reversed(range(rounds)):
+            partner = [(i, i ^ (1 << level)) for i in range(n_exp)]
+            head_share = jnp.concatenate([head_share, lax.ppermute(head_share, "exp", partner)], 0)
+        head_in = lax.all_gather(head_share, "seq", axis=0, tiled=False).reshape(tokens, width)
+        local_best = jnp.max(jnp.dot(head_in, w_head, preferred_element_type=jnp.float32), axis=-1)
+        flipped = jnp.arange(n_exp, dtype=jnp.int32) ^ lax.axis_index("exp")
+        block = sum(((flipped >> bit) & 1) << (rounds - 1 - bit) for bit in range(rounds))
+        local_best = jnp.take(local_best.reshape(n_seq, n_exp, share), block, axis=1).reshape(tokens)
+    else:
+        head_in = gather_all(head_share).reshape(tokens, width)
+        local_best = jnp.max(jnp.dot(head_in, w_head, preferred_element_type=jnp.float32), axis=-1)
     message = jnp.concatenate([local_best, norms_share], axis=0)
     heard = lax.all_to_all(
         jnp.broadcast_to(message[None, :], (n_dev, message.shape[0])),

time: 180 us -> 175 us (0.972)
  blocking collectives: 75.2 us -> 59.9 us
  waiting for transfers between devices: 21.9 us -> 32.3 us
    all_gather x3 -> x2, blocking collectives: 32.8 us -> 17.6 us  [the longest x1 9.2 us: on_device(): lax.all_gather(head_share, 'seq', axis=0, tiled=False)]
    ppermute x0 -> x3, waiting for transfers between devices: none -> 9.72 us  [on_device(): lax.ppermute(head_share, 'exp', partner)]
  transfers between devices with their start and end apart: 3 -> 6, of which waited for: 3 -> 6; matrix products, arithmetic and copies ran while one was open for 8% -> 8% of each run, Pallas kernels for 0% -> 0%
where the time goes in v5:
time: 175 us; the launch traced here: 174 us
  blocking collectives  59.9 us (34%)
  waiting for transfers between devices  32.3 us (18%)
  local copies, waits for them, and re-layouts  25.7 us (15%)
  Pallas kernels  21.5 us (12%)
  starting transfers between devices  13.2 us (8%)
  matrix products  13.2 us (8%)
  other arithmetic  7.54 us (4%)
    pallas_call x1, Pallas kernels, experts(): pl.pallas_call(lambda *refs: experts_kernel(pieces, *refs), grid=(pieces...  21.5 us
    all_to_all x1, waiting for transfers between devices, on_device(): lax.all_to_all(term_rows.reshape(n_dev, share, width).astype(jnp.bfloat16...  16.4 us
    all_gather x1, blocking collectives, on_device(): lax.all_gather(rms_scale(resid_group, moe_gain).astype(jnp.bfloat16), 'ex...  15 us
    dot_general x3, local copies, waits for them, and re-layouts, project(): jnp.dot(attn_in, weight, preferred_element_type=jnp.float32)  11.9 us
    ppermute x3, waiting for transfers between devices, on_device(): lax.ppermute(head_share, 'exp', partner)  9.72 us
    all_to_all x1, blocking collectives, on_device(): lax.all_to_all(jnp.broadcast_to(message[None, :], (n_dev, message.shape[0...  9.3 us
    all_gather x1, blocking collectives, on_device(): lax.all_gather(head_share, 'seq', axis=0, tiled=False)  9.2 us
    all_gather x1, blocking collectives, on_device(): row_parts = lax.all_gather(row_part, 'seq', axis=0, tiled=False)  9 us
  transfers between devices with their start and end apart: 6, of which 6 were waited for; matrix products, arithmetic and copies ran while one was open for 8% of the time, Pallas kernels for 0%

profile of v5, /device:TPU:0, one launch (start us, length us, event | category | flops | bytes accessed | tf_op | source)
XLA Modules:
  0.0 174.5 jit_solution(14032599227111314631)
XLA Ops:
  2.4 5.1 %gather_fusion = bf16[128,2048]{1,0:T(8,128)(2,1)S(1)} fusion(bf16[1600,2048]{1,0:T(8,128)(2,1)} %param.26, s32[1024]{0:T(1024)S(1)} %pad_clamp_fusion.1), kind=kCustom, calls=%fused_computation | custom fusion | bytes 1049088 | tf_op jit(solution)/shard_map/jit(_take)/gather | solution.py:158
  9.1 6.3 %all-to-all-start = ((bf16[8,4,4,2048]{3,2,1,0:T(4,128)(2,1)}), bf16[8,4,4,2048]{3,2,1,0:T(4,128)(2,1)S(1)}, u32[]{:S(2)}, u32[]{:S(2)}) async-start(bf16[8,4,4,2048]{3,2,1,0:T(4,128)(2,1)} %select_select_fusion), calls=%async_computation | async-start | bytes 1048576 | tf_op jit(solution)/shard_map/all_to_all | solution.py:160
  16.5 4.0 %copy.178 = bf16[512,2048]{1,0:T(8,128)(2,1)} copy(bf16[512,2048]{0,1:T(8,128)(2,1)} %bitcast.135) | data formatting | bytes 4194304 | tf_op jit(solution)/shard_map/dot_general | solution.py:171
  20.5 4.0 %copy.176 = bf16[512,2048]{1,0:T(8,128)(2,1)} copy(bf16[512,2048]{0,1:T(8,128)(2,1)} %bitcast.136) | data formatting | bytes 4194304 | tf_op jit(solution)/shard_map/dot_general | solution.py:171
  24.6 3.9 %copy.177 = bf16[512,2048]{1,0:T(8,128)(2,1)} copy(bf16[512,2048]{0,1:T(8,128)(2,1)} %bitcast.137) | data formatting | bytes 4194304 | tf_op jit(solution)/shard_map/dot_general | solution.py:171
  29.0 1.8 %all-to-all-done = bf16[8,4,4,2048]{3,2,1,0:T(4,128)(2,1)S(1)} async-done(((bf16[8,4,4,2048]{3,2,1,0:T(4,128)(2,1)}), bf16[8,4,4,2048]{3,2,1,0:T(4,128)(2,1)S(1)}, u32[]{:S(2)}, u32[]{:S(2)}) %all-to-all-start) | async-done | bytes 524320 | tf_op jit(solution)/shard_map/all_to_all | solution.py:160
  31.1 9.0 %all-gather = bf16[16,4,2048]{2,1,0:T(4,128)(2,1)S(1)} all-gather(bf16[4,4,2048]{2,1,0:T(4,128)(2,1)S(1)} %reduce_sum.137), channel_id=2, replica_groups=mesh['seq'=4,'exp'=8] {'seq'}, dimensions={0}, use_global_device_ids=true | all-gather | bytes 327680 | tf_op jit(solution)/shard_map/all_gather | solution.py:162
  40.5 2.4 %convolution_convert_fusion.1 = bf16[16,4,128]{2,0,1:T(8,128)(2,1)S(1)} fusion(bf16[16,2048,1]{1,0,2:T(8,128)(2,1)S(1)} %reshape.666, bf16[4,128,2048]{2,1,0:T(8,128)(2,1)} %bitcast.133), kind=kOutput, calls=%fused_computation.23 | convolution fusion | flops 33562624 | bytes 2179072 | tf_op jit(solution)/shard_map/dot_general | solution.py:171
  42.9 2.3 %fusion.48 = f32[16,4,128]{2,0,1:T(8,128)S(1)} fusion(bf16[16,2048,1]{1,0,2:T(8,128)(2,1)S(1)} %reshape.666, bf16[4,128,2048]{2,1,0:T(8,128)(2,1)} %bitcast.132), kind=kOutput, calls=%fused_computation.119 | convolution fusion | flops 33554432 | bytes 2195456 | tf_op jit(solution)/shard_map/dot_general | solution.py:171
  46.1 9.0 %all-gather.1 = bf16[12,16,4,128]{3,1,2,0:T(8,128)(2,1)S(1)} all-gather(bf16[3,16,4,128]{3,1,2,0:T(8,128)(2,1)S(1)} %pad_maximum_fusion.2), channel_id=3, replica_groups=mesh['seq'=4,'exp'=8] {'seq'}, dimensions={0}, use_global_device_ids=true | all-gather | bytes 245760 | tf_op jit(solution)/shard_map/all_gather | solution.py:178
  55.2 1.3 select_reduce_fusion
  59.1 3.3 %all-to-all-start.1 = ((f32[4,1,8320]{2,1,0:T(1,128)}), f32[4,1,8320]{2,1,0:T(1,128)S(1)}, u32[]{:S(2)}, u32[]{:S(2)}) async-start(f32[4,1,8320]{2,1,0:T(1,128)} %copy.156), calls=%async_computation.1 | async-start | bytes 266240 | tf_op jit(solution)/shard_map/all_to_all | solution.py:221
  63.0 4.4 %all-to-all-done.1 = f32[4,1,8320]{2,1,0:T(1,128)S(1)} async-done(((f32[4,1,8320]{2,1,0:T(1,128)}), f32[4,1,8320]{2,1,0:T(1,128)S(1)}, u32[]{:S(2)}, u32[]{:S(2)}) %all-to-all-start.1) | async-done | bytes 133152 | tf_op jit(solution)/shard_map/all_to_all | solution.py:221
  69.3 8.4 %all-gather.2 = bf16[64,2048]{1,0:T(8,128)(2,1)S(1)} all-gather(bf16[16,2048]{1,0:T(8,128)(2,1)S(1)} %convolution_convert_fusion), channel_id=4, replica_groups=mesh['seq'=4,'exp'=8] {'seq'}, dimensions={0}, use_global_device_ids=true | all-gather | bytes 327680 | tf_op jit(solution)/shard_map/all_gather | solution.py:255
  77.9 15.0 %all_gather.33.refs_0_ = bf16[128,2048]{1,0:T(8,128)(2,1)S(1)} all-gather(bf16[16,2048]{1,0:T(8,128)(2,1)S(1)} %multiply_convert_fusion), channel_id=1, replica_groups=mesh['seq'=4,'exp'=8] {'exp'}, dimensions={0}, use_global_device_ids=true | all-gather | bytes 589824 | tf_op jit(solution)/shard_map/all_gather | solution.py:258
  94.2 21.5 %shard_map.221 = f32[128,2048]{1,0:T(8,128)} custom-call(bf16[128,2048]{1,0:T(8,128)(2,1)} %copy-done.3, f32[128,128]{1,0:T(8,128)} %pad.4.refs_1_, bf16[8,352,2048]{2,1,0:T(8,128)(2,1)} %bitcast.130, bf16[8,352,2048]{2,1,0:T(8,128)(2,1)} %bitcast.131, bf16[8,352,2048]{2,1,0:T(8,128)(2,1)} %refs_4_.1, bf16[352,2048]{1,0:T(8,128)(2,1)} %bitcast.139, ...), custom_call_target="tpu_custom_call" | custom-call | flops 4982833152 | bytes 40501248 | tf_op jit(solution)/shard_map/pallas_call | solution.py:83
  115.7 1.3 convert_element_type.118
  118.7 3.3 %all-to-all-start.2 = ((bf16[32,4,2048]{2,1,0:T(4,128)(2,1)}), bf16[32,4,2048]{2,1,0:T(4,128)(2,1)S(1)}, u32[]{:S(2)}, u32[]{:S(2)}) async-start(bf16[32,4,2048]{2,1,0:T(4,128)(2,1)} %copy.172), calls=%async_computation.2 | async-start | bytes 1048576 | tf_op jit(solution)/shard_map/all_to_all | solution.py:293
  122.0 16.4 %all-to-all-done.2 = bf16[32,4,2048]{2,1,0:T(4,128)(2,1)S(1)} async-done(((bf16[32,4,2048]{2,1,0:T(4,128)(2,1)}), bf16[32,4,2048]{2,1,0:T(4,128)(2,1)S(1)}, u32[]{:S(2)}, u32[]{:S(2)}) %all-to-all-start.2) | async-done | bytes 524320 | tf_op jit(solution)/shard_map/all_to_all | solution.py:293
  138.9 4.6 %collective-permute-done = bf16[4,2048]{1,0:T(4,128)(2,1)S(1)} collective-permute-done((bf16[4,2048]{1,0:T(4,128)(2,1)S(1)}, bf16[4,2048]{1,0:T(4,128)(2,1)S(1)}, u32[]{:S(2)}, u32[]{:S(2)}) %collective-permute-start) | collective-permute-done | bytes 16416 | tf_op jit(solution)/shard_map/ppermute | solution.py:309
  143.6 3.9 %collective-permute-done.1 = bf16[8,2048]{1,0:T(8,128)(2,1)S(1)} collective-permute-done((bf16[8,2048]{1,0:T(8,128)(2,1)S(1)}, bf16[8,2048]{1,0:T(8,128)(2,1)S(1)}, u32[]{:S(2)}, u32[]{:S(2)}) %collective-permute-start.1) | collective-permute-done | bytes 32800 | tf_op jit(solution)/shard_map/ppermute | solution.py:309
  148.9 9.2 %all-gather.3 = bf16[128,2048]{1,0:T(8,128)(2,1)S(1)} all-gather(bf16[32,2048]{1,0:T(8,128)(2,1)S(1)} %pad_maximum_fusion), channel_id=5, replica_groups=mesh['seq'=4,'exp'=8] {'seq'}, dimensions={0}, use_global_device_ids=true | all-gather | bytes 655360 | tf_op jit(solution)/shard_map/all_gather | solution.py:310
  158.1 4.7 %convolution_reduce_fusion = f32[128]{0:T(128)S(1)} fusion(bf16[128,2048]{1,0:T(8,128)(2,1)S(1)} %all-gather.3, bf16[2048,1600]{0,1:T(8,128)(2,1)} %param.43), kind=kOutput, calls=%fused_computation.9 | convolution fusion | flops 839065472 | bytes 7078400 | tf_op jit(solution)/shard_map/dot_general | solution.py:311
  163.8 9.3 %all_to_all.31 = f32[32,1,132]{2,1,0:T(1,128)S(1)} all-to-all(f32[32,1,132]{2,1,0:T(1,128)S(1)} %broadcast_in_dim.157), channel_id=1, replica_groups=mesh['seq'=4,'exp'=8] {'seq','exp'}, dimensions={0} | all-to-all | bytes 33792 | tf_op jit(solution)/shard_map/all_to_all | solution.py:319
  (142 shorter events, 18.8 us)
Async XLA Ops:
  0.6 68.2 %copy-start = (bf16[512,2048]{1,0:T(8,128)(2,1)S(1)}, bf16[512,2048]{1,0:T(8,128)(2,1)}, u32[]{:S(2)}) copy-start(bf16[512,2048]{1,0:T(8,128)(2,1)} %param.31) | copy-start | bytes 6291460
  0.6 14.8 %copy-start.11 = (s32[32]{0:T(128)S(1)}, s32[32]{0:T(128)}, u32[]{:S(2)}) copy-start(s32[32]{0:T(128)} %param.23) | copy-start | bytes 388
  9.1 21.7 %all-to-all-start = ((bf16[8,4,4,2048]{3,2,1,0:T(4,128)(2,1)}), bf16[8,4,4,2048]{3,2,1,0:T(4,128)(2,1)S(1)}, u32[]{:S(2)}, u32[]{:S(2)}) async-start(bf16[8,4,4,2048]{3,2,1,0:T(4,128)(2,1)} %select_select_fusion), calls=%async_computation | async-start | bytes 1048576 | tf_op jit(solution)/shard_map/all_to_all | solution.py:160
  20.5 8.0 %copy-start.5 = (s32[4,32,6]{1,0,2:T(4,128)S(1)}, s32[4,32,6]{1,0,2:T(4,128)}, u32[]{:S(2)}) copy-start(s32[4,32,6]{1,0,2:T(4,128)} %param.25) | copy-start | bytes 9220
  24.5 15.9 %copy-start.6 = (f32[2048]{0:T(1024)S(1)}, f32[2048]{0:T(1024)}, u32[]{:S(2)}) copy-start(f32[2048]{0:T(1024)} %param.27) | copy-start | bytes 24580
  40.5 4.7 %copy-start.2 = (bf16[512,2048]{1,0:T(8,128)(2,1)S(1)}, bf16[512,2048]{1,0:T(8,128)(2,1)}, u32[]{:S(2)}) copy-start(bf16[512,2048]{1,0:T(8,128)(2,1)} %copy.177) | copy-start | bytes 6291460
  40.5 14.6 %copy-start.9 = (bf16[4,256,2048]{2,1,0:T(8,128)(2,1)S(1)}, bf16[4,256,2048]{2,1,0:T(8,128)(2,1)}, u32[]{:S(2)}) copy-start(bf16[4,256,2048]{2,1,0:T(8,128)(2,1)} %param.32) | copy-start | bytes 12582916
  45.2 11.5 %copy-start.10 = (bf16[4,256,2048]{2,1,0:T(8,128)(2,1)S(1)}, bf16[4,256,2048]{2,1,0:T(8,128)(2,1)}, u32[]{:S(2)}) copy-start(bf16[4,256,2048]{2,1,0:T(8,128)(2,1)} %param.33) | copy-start | bytes 12582916
  57.5 20.4 %copy-start.7 = (f32[2048]{0:T(1024)S(1)}, f32[2048]{0:T(1024)}, u32[]{:S(2)}) copy-start(f32[2048]{0:T(1024)} %param.34) | copy-start | bytes 24580
  57.5 35.5 %copy-start.4 = (bf16[2048,64]{0,1:T(8,128)(2,1)S(1)}, bf16[2048,64]{0,1:T(8,128)(2,1)}, u32[]{:S(2)}) copy-start(bf16[2048,64]{0,1:T(8,128)(2,1)} %param.35) | copy-start | bytes 786436
  59.1 8.3 %all-to-all-start.1 = ((f32[4,1,8320]{2,1,0:T(1,128)}), f32[4,1,8320]{2,1,0:T(1,128)S(1)}, u32[]{:S(2)}, u32[]{:S(2)}) async-start(f32[4,1,8320]{2,1,0:T(1,128)} %copy.156), calls=%async_computation.1 | async-start | bytes 266240 | tf_op jit(solution)/shard_map/all_to_all | solution.py:221
  93.0 1.2 copy-start.3
  115.7 23.1 %copy-start.8 = (f32[2048]{0:T(1024)S(1)}, f32[2048]{0:T(1024)}, u32[]{:S(2)}) copy-start(f32[2048]{0:T(1024)} %param.42) | copy-start | bytes 24580
  118.7 19.7 %all-to-all-start.2 = ((bf16[32,4,2048]{2,1,0:T(4,128)(2,1)}), bf16[32,4,2048]{2,1,0:T(4,128)(2,1)S(1)}, u32[]{:S(2)}, u32[]{:S(2)}) async-start(bf16[32,4,2048]{2,1,0:T(4,128)(2,1)} %copy.172), calls=%async_computation.2 | async-start | bytes 1048576 | tf_op jit(solution)/shard_map/all_to_all | solution.py:293
  138.8 4.7 %collective-permute-start = (bf16[4,2048]{1,0:T(4,128)(2,1)S(1)}, bf16[4,2048]{1,0:T(4,128)(2,1)S(1)}, u32[]{:S(2)}, u32[]{:S(2)}) collective-permute-start(bf16[4,2048]{1,0:T(4,128)(2,1)S(1)} %multiply_convert_fusion.2), channel_id=1, source_target_pairs={{0,4},{1,5},{2,6},{3,7},{4,0},{5,1},{6,2},{7,3},{8,12},{9,13},{10,... | collective-permute-start | bytes 49160 | tf_op jit(solution)/shard_map/ppermute | solution.py:309
  143.5 4.0 %collective-permute-start.1 = (bf16[8,2048]{1,0:T(8,128)(2,1)S(1)}, bf16[8,2048]{1,0:T(8,128)(2,1)S(1)}, u32[]{:S(2)}, u32[]{:S(2)}) collective-permute-start(bf16[8,2048]{1,0:T(8,128)(2,1)S(1)} %pad_maximum_fusion.3), channel_id=1, source_target_pairs={{0,2},{1,3},{2,0},{3,1},{4,6},{5,7},{6,4},{7,5},{8,10},{9,11},{10,... | collective-permute-start | bytes 98312 | tf_op jit(solution)/shard_map/ppermute | solution.py:309
  147.6 1.3 collective-permute-start.2
  148.9 25.5 %copy-start.1 = (bf16[512,2048]{1,0:T(8,128)(2,1)S(1)}, bf16[512,2048]{1,0:T(8,128)(2,1)}, u32[]{:S(2)}) copy-start(bf16[512,2048]{1,0:T(8,128)(2,1)} %param.31) | copy-start | bytes 6291460

commit v6 on v5

--- a/solution.py
+++ b/solution.py
@@ -39,12 +39,12 @@
     return lax.all_gather(inner, "seq", axis=0, tiled=False)
 
 
-def experts_kernel(pieces, x_ref, weight_ref, gate_ref, up_ref, down_ref, sgate_ref, sup_ref, sdown_ref, out_ref):
+def experts_kernel(pieces, x_ref, weight_ref, gate_ref, up_ref, down_ref, sgate_ref, sup_ref, sdown_ref, out_ref, total_ref):
     step = pl.program_id(0)
 
     @pl.when(step == 0)
     def _():
-        out_ref[...] = jnp.zeros_like(out_ref)
+        total_ref[...] = jnp.zeros_like(total_ref)
 
     def one_piece(gate, up, down, scale):
         rows = x_ref[...]
@@ -52,7 +52,7 @@
         gate_out = lax.dot_general(rows, gate, along, preferred_element_type=jnp.float32)
         up_out = lax.dot_general(rows, up, along, preferred_element_type=jnp.float32)
         hidden = (gate_out * jax.nn.sigmoid(gate_out) * up_out * scale).astype(jnp.bfloat16)
-        out_ref[...] += jnp.dot(hidden, down, preferred_element_type=jnp.float32)
+        total_ref[...] += jnp.dot(hidden, down, preferred_element_type=jnp.float32)
 
     table = weight_ref[...]
     column = lax.broadcasted_iota(jnp.int32, table.shape, 1)
@@ -65,6 +65,7 @@
     @pl.when(step == pieces)
     def _():
         one_piece(sgate_ref[...], sup_ref[...], sdown_ref[...], scale)
+        out_ref[...] = total_ref[...].astype(out_ref.dtype)
 
 
 def experts(rows, weight_table, gate_pieces, up_pieces, down_pieces, shared_gate, shared_up, shared_down):
@@ -94,11 +95,12 @@
             pl.BlockSpec(shared_down.shape, lambda step: (0, 0)),
         ],
         out_specs=pl.BlockSpec((count, width), lambda step: (0, 0)),
-        out_shape=jax.ShapeDtypeStruct((count, width), jnp.float32),
+        out_shape=jax.ShapeDtypeStruct((count, width), jnp.bfloat16),
+        scratch_shapes=[pltpu.VMEM((count, width), jnp.float32)],
         cost_estimate=pl.CostEstimate(
             flops=6 * count * width * (pieces * units + shared_gate.shape[0]),
             transcendentals=count * (pieces * units + shared_gate.shape[0]),
-            bytes_accessed=weight_bytes + 2 * count * width + 4 * count * width,
+            bytes_accessed=weight_bytes + 4 * count * width,
         ),
     )(rows, weight_table, gate_pieces, up_pieces, down_pieces, shared_gate, shared_up, shared_down)
 
@@ -288,11 +290,10 @@
         shared_gate, shared_up, shared_down,
     )
 
-    term_rows = jnp.swapaxes(term_rows.reshape(n_exp, n_seq, share, width), 0, 1)
     term_sum = jnp.sum(
         lax.all_to_all(
-            term_rows.reshape(n_dev, share, width).astype(jnp.bfloat16),
-            ("seq", "exp"),
+            term_rows.reshape(n_dev, share, width),
+            ("exp", "seq"),
             0,
             0,
             tiled=True,

time: 175 us -> 175 us (level)
    reshape x0 -> x1, local copies, waits for them, and re-layouts: none -> 2.05 us  [on_device(): term_rows.reshape(n_dev, share, width)]
where the time goes in v6:
time: 175 us; the launch traced here: 174 us
  blocking collectives  60.4 us (35%)
  waiting for transfers between devices  31.2 us (18%)
  local copies, waits for them, and re-layouts  26 us (15%)
  Pallas kernels  21.3 us (12%)
  starting transfers between devices  14.1 us (8%)
  matrix products  13.2 us (8%)
  other arithmetic  6.25 us (4%)
    pallas_call x1, Pallas kernels, experts(): pl.pallas_call(lambda *refs: experts_kernel(pieces, *refs), grid=(pieces...  21.3 us
    all_to_all x1, waiting for transfers between devices, on_device(): lax.all_to_all(term_rows.reshape(n_dev, share, width), ('exp', 'seq'), 0,...  16.2 us
    all_gather x1, blocking collectives, on_device(): lax.all_gather(rms_scale(resid_group, moe_gain).astype(jnp.bfloat16), 'ex...  15 us
    dot_general x3, local copies, waits for them, and re-layouts, project(): jnp.dot(attn_in, weight, preferred_element_type=jnp.float32)  11.9 us
    all_to_all x1, blocking collectives, on_device(): lax.all_to_all(jnp.broadcast_to(message[None, :], (n_dev, message.shape[0...  9.95 us
    all_gather x1, blocking collectives, on_device(): lax.all_gather(head_share, 'seq', axis=0, tiled=False)  9.07 us
    all_gather x1, blocking collectives, on_device(): row_parts = lax.all_gather(row_part, 'seq', axis=0, tiled=False)  9 us
    all_gather x1, blocking collectives, on_device(): lax.all_gather(jnp.stack([query_part, key_part, value_part], axis=0), 'se...  8.97 us
  transfers between devices with their start and end apart: 6, of which 6 were waited for; matrix products, arithmetic and copies ran while one was open for 8% of the time, Pallas kernels for 0%

profile of v6, /device:TPU:0, one launch (start us, length us, event | category | flops | bytes accessed | tf_op | source)
XLA Modules:
  0.0 173.7 jit_solution(2833305176559019343)
XLA Ops:
  2.4 5.1 %gather_fusion = bf16[128,2048]{1,0:T(8,128)(2,1)S(1)} fusion(bf16[1600,2048]{1,0:T(8,128)(2,1)} %param.26, s32[1024]{0:T(1024)S(1)} %pad_clamp_fusion.1), kind=kCustom, calls=%fused_computation | custom fusion | bytes 1049088 | tf_op jit(solution)/shard_map/jit(_take)/gather | solution.py:160
  9.1 6.3 %all-to-all-start = ((bf16[8,4,4,2048]{3,2,1,0:T(4,128)(2,1)}), bf16[8,4,4,2048]{3,2,1,0:T(4,128)(2,1)S(1)}, u32[]{:S(2)}, u32[]{:S(2)}) async-start(bf16[8,4,4,2048]{3,2,1,0:T(4,128)(2,1)} %select_select_fusion), calls=%async_computation | async-start | bytes 1048576 | tf_op jit(solution)/shard_map/all_to_all | solution.py:162
  16.5 4.0 %copy.172 = bf16[512,2048]{1,0:T(8,128)(2,1)} copy(bf16[512,2048]{0,1:T(8,128)(2,1)} %bitcast.130) | data formatting | bytes 4194304 | tf_op jit(solution)/shard_map/dot_general | solution.py:173
  20.5 4.0 %copy.170 = bf16[512,2048]{1,0:T(8,128)(2,1)} copy(bf16[512,2048]{0,1:T(8,128)(2,1)} %bitcast.131) | data formatting | bytes 4194304 | tf_op jit(solution)/shard_map/dot_general | solution.py:173
  24.6 3.9 %copy.171 = bf16[512,2048]{1,0:T(8,128)(2,1)} copy(bf16[512,2048]{0,1:T(8,128)(2,1)} %bitcast.132) | data formatting | bytes 4194304 | tf_op jit(solution)/shard_map/dot_general | solution.py:173
  29.0 1.8 %all-to-all-done = bf16[8,4,4,2048]{3,2,1,0:T(4,128)(2,1)S(1)} async-done(((bf16[8,4,4,2048]{3,2,1,0:T(4,128)(2,1)}), bf16[8,4,4,2048]{3,2,1,0:T(4,128)(2,1)S(1)}, u32[]{:S(2)}, u32[]{:S(2)}) %all-to-all-start) | async-done | bytes 524320 | tf_op jit(solution)/shard_map/all_to_all | solution.py:162
  31.1 9.0 %all-gather = bf16[16,4,2048]{2,1,0:T(4,128)(2,1)S(1)} all-gather(bf16[4,4,2048]{2,1,0:T(4,128)(2,1)S(1)} %reduce_sum.137), channel_id=2, replica_groups=mesh['seq'=4,'exp'=8] {'seq'}, dimensions={0}, use_global_device_ids=true | all-gather | bytes 327680 | tf_op jit(solution)/shard_map/all_gather | solution.py:164
  40.5 2.4 %convolution_convert_fusion.1 = bf16[16,4,128]{2,0,1:T(8,128)(2,1)S(1)} fusion(bf16[16,2048,1]{1,0,2:T(8,128)(2,1)S(1)} %reshape.666, bf16[4,128,2048]{2,1,0:T(8,128)(2,1)} %bitcast.128), kind=kOutput, calls=%fused_computation.23 | convolution fusion | flops 33562624 | bytes 2179072 | tf_op jit(solution)/shard_map/dot_general | solution.py:173
  42.9 2.3 %fusion.48 = f32[16,4,128]{2,0,1:T(8,128)S(1)} fusion(bf16[16,2048,1]{1,0,2:T(8,128)(2,1)S(1)} %reshape.666, bf16[4,128,2048]{2,1,0:T(8,128)(2,1)} %bitcast.127), kind=kOutput, calls=%fused_computation.118 | convolution fusion | flops 33554432 | bytes 2195456 | tf_op jit(solution)/shard_map/dot_general | solution.py:173
  46.1 9.0 %all-gather.1 = bf16[12,16,4,128]{3,1,2,0:T(8,128)(2,1)S(1)} all-gather(bf16[3,16,4,128]{3,1,2,0:T(8,128)(2,1)S(1)} %pad_maximum_fusion.2), channel_id=3, replica_groups=mesh['seq'=4,'exp'=8] {'seq'}, dimensions={0}, use_global_device_ids=true | all-gather | bytes 245760 | tf_op jit(solution)/shard_map/all_gather | solution.py:180
  55.2 1.3 select_reduce_fusion
  59.1 3.3 %all-to-all-start.1 = ((f32[4,1,8320]{2,1,0:T(1,128)}), f32[4,1,8320]{2,1,0:T(1,128)S(1)}, u32[]{:S(2)}, u32[]{:S(2)}) async-start(f32[4,1,8320]{2,1,0:T(1,128)} %copy.152), calls=%async_computation.1 | async-start | bytes 266240 | tf_op jit(solution)/shard_map/all_to_all | solution.py:223
  63.0 4.4 %all-to-all-done.1 = f32[4,1,8320]{2,1,0:T(1,128)S(1)} async-done(((f32[4,1,8320]{2,1,0:T(1,128)}), f32[4,1,8320]{2,1,0:T(1,128)S(1)}, u32[]{:S(2)}, u32[]{:S(2)}) %all-to-all-start.1) | async-done | bytes 133152 | tf_op jit(solution)/shard_map/all_to_all | solution.py:223
  69.3 8.4 %all-gather.2 = bf16[64,2048]{1,0:T(8,128)(2,1)S(1)} all-gather(bf16[16,2048]{1,0:T(8,128)(2,1)S(1)} %convolution_convert_fusion), channel_id=4, replica_groups=mesh['seq'=4,'exp'=8] {'seq'}, dimensions={0}, use_global_device_ids=true | all-gather | bytes 327680 | tf_op jit(solution)/shard_map/all_gather | solution.py:257
  77.9 15.0 %all_gather.33.refs_0_ = bf16[128,2048]{1,0:T(8,128)(2,1)S(1)} all-gather(bf16[16,2048]{1,0:T(8,128)(2,1)S(1)} %multiply_convert_fusion), channel_id=1, replica_groups=mesh['seq'=4,'exp'=8] {'exp'}, dimensions={0}, use_global_device_ids=true | all-gather | bytes 589824 | tf_op jit(solution)/shard_map/all_gather | solution.py:260
  94.2 21.3 %shard_map.221 = bf16[128,2048]{1,0:T(8,128)(2,1)} custom-call(bf16[128,2048]{1,0:T(8,128)(2,1)} %copy-done.3, f32[128,128]{1,0:T(8,128)} %pad.4.refs_1_, bf16[8,352,2048]{2,1,0:T(8,128)(2,1)} %bitcast.125, bf16[8,352,2048]{2,1,0:T(8,128)(2,1)} %bitcast.126, bf16[8,352,2048]{2,1,0:T(8,128)(2,1)} %refs_4_.1, bf16[352,2048]{1,0:T(8,128)(2,1)} %bitcast.133, ...), custom_call_target="tpu_custom_call" | custom-call | flops 4982833152 | bytes 39976960 | tf_op jit(solution)/shard_map/pallas_call | solution.py:84
  115.5 2.0 %reshape.638 = bf16[32,4,2048]{2,1,0:T(4,128)(2,1)} reshape(bf16[128,2048]{1,0:T(8,128)(2,1)} %shard_map.221) | data formatting | bytes 1048576 | tf_op jit(solution)/shard_map/reshape | solution.py:295
  117.5 3.3 %all-to-all-start.2 = ((bf16[32,4,2048]{2,1,0:T(4,128)(2,1)}), bf16[32,4,2048]{2,1,0:T(4,128)(2,1)S(1)}, u32[]{:S(2)}, u32[]{:S(2)}) async-start(bf16[32,4,2048]{2,1,0:T(4,128)(2,1)} %reshape.638), calls=%async_computation.2 | async-start | bytes 1048576 | tf_op jit(solution)/shard_map/all_to_all | solution.py:294
  120.9 16.2 %all-to-all-done.2 = bf16[32,4,2048]{2,1,0:T(4,128)(2,1)S(1)} async-done(((bf16[32,4,2048]{2,1,0:T(4,128)(2,1)}), bf16[32,4,2048]{2,1,0:T(4,128)(2,1)S(1)}, u32[]{:S(2)}, u32[]{:S(2)}) %all-to-all-start.2) | async-done | bytes 524320 | tf_op jit(solution)/shard_map/all_to_all | solution.py:294
  137.7 4.6 %collective-permute-done = bf16[4,2048]{1,0:T(4,128)(2,1)S(1)} collective-permute-done((bf16[4,2048]{1,0:T(4,128)(2,1)S(1)}, bf16[4,2048]{1,0:T(4,128)(2,1)S(1)}, u32[]{:S(2)}, u32[]{:S(2)}) %collective-permute-start) | collective-permute-done | bytes 16416 | tf_op jit(solution)/shard_map/ppermute | solution.py:310
  143.3 2.9 %collective-permute-done.1 = bf16[8,2048]{1,0:T(8,128)(2,1)S(1)} collective-permute-done((bf16[8,2048]{1,0:T(8,128)(2,1)S(1)}, bf16[8,2048]{1,0:T(8,128)(2,1)S(1)}, u32[]{:S(2)}, u32[]{:S(2)}) %collective-permute-start.1) | collective-permute-done | bytes 32800 | tf_op jit(solution)/shard_map/ppermute | solution.py:310
  147.7 9.1 %all-gather.3 = bf16[128,2048]{1,0:T(8,128)(2,1)S(1)} all-gather(bf16[32,2048]{1,0:T(8,128)(2,1)S(1)} %pad_maximum_fusion), channel_id=5, replica_groups=mesh['seq'=4,'exp'=8] {'seq'}, dimensions={0}, use_global_device_ids=true | all-gather | bytes 655360 | tf_op jit(solution)/shard_map/all_gather | solution.py:311
  156.7 4.7 %convolution_reduce_fusion = f32[128]{0:T(128)S(1)} fusion(bf16[128,2048]{1,0:T(8,128)(2,1)S(1)} %all-gather.3, bf16[2048,1600]{0,1:T(8,128)(2,1)} %param.43), kind=kOutput, calls=%fused_computation.9 | convolution fusion | flops 839065472 | bytes 7078400 | tf_op jit(solution)/shard_map/dot_general | solution.py:312
  162.4 9.9 %all_to_all.31 = f32[32,1,132]{2,1,0:T(1,128)S(1)} all-to-all(f32[32,1,132]{2,1,0:T(1,128)S(1)} %broadcast_in_dim.157), channel_id=1, replica_groups=mesh['seq'=4,'exp'=8] {'seq','exp'}, dimensions={0} | all-to-all | bytes 33792 | tf_op jit(solution)/shard_map/all_to_all | solution.py:320
  (139 shorter events, 18.1 us)
Async XLA Ops:
  0.6 68.2 %copy-start = (bf16[512,2048]{1,0:T(8,128)(2,1)S(1)}, bf16[512,2048]{1,0:T(8,128)(2,1)}, u32[]{:S(2)}) copy-start(bf16[512,2048]{1,0:T(8,128)(2,1)} %param.31) | copy-start | bytes 6291460
  0.6 14.8 %copy-start.11 = (s32[32]{0:T(128)S(1)}, s32[32]{0:T(128)}, u32[]{:S(2)}) copy-start(s32[32]{0:T(128)} %param.23) | copy-start | bytes 388
  9.1 21.7 %all-to-all-start = ((bf16[8,4,4,2048]{3,2,1,0:T(4,128)(2,1)}), bf16[8,4,4,2048]{3,2,1,0:T(4,128)(2,1)S(1)}, u32[]{:S(2)}, u32[]{:S(2)}) async-start(bf16[8,4,4,2048]{3,2,1,0:T(4,128)(2,1)} %select_select_fusion), calls=%async_computation | async-start | bytes 1048576 | tf_op jit(solution)/shard_map/all_to_all | solution.py:162
  20.5 8.0 %copy-start.5 = (s32[4,32,6]{1,0,2:T(4,128)S(1)}, s32[4,32,6]{1,0,2:T(4,128)}, u32[]{:S(2)}) copy-start(s32[4,32,6]{1,0,2:T(4,128)} %param.25) | copy-start | bytes 9220
  24.5 15.9 %copy-start.6 = (f32[2048]{0:T(1024)S(1)}, f32[2048]{0:T(1024)}, u32[]{:S(2)}) copy-start(f32[2048]{0:T(1024)} %param.27) | copy-start | bytes 24580
  40.5 4.7 %copy-start.2 = (bf16[512,2048]{1,0:T(8,128)(2,1)S(1)}, bf16[512,2048]{1,0:T(8,128)(2,1)}, u32[]{:S(2)}) copy-start(bf16[512,2048]{1,0:T(8,128)(2,1)} %copy.171) | copy-start | bytes 6291460
  40.5 14.6 %copy-start.9 = (bf16[4,256,2048]{2,1,0:T(8,128)(2,1)S(1)}, bf16[4,256,2048]{2,1,0:T(8,128)(2,1)}, u32[]{:S(2)}) copy-start(bf16[4,256,2048]{2,1,0:T(8,128)(2,1)} %param.32) | copy-start | bytes 12582916
  45.2 11.5 %copy-start.10 = (bf16[4,256,2048]{2,1,0:T(8,128)(2,1)S(1)}, bf16[4,256,2048]{2,1,0:T(8,128)(2,1)}, u32[]{:S(2)}) copy-start(bf16[4,256,2048]{2,1,0:T(8,128)(2,1)} %param.33) | copy-start | bytes 12582916
  57.5 20.4 %copy-start.7 = (f32[2048]{0:T(1024)S(1)}, f32[2048]{0:T(1024)}, u32[]{:S(2)}) copy-start(f32[2048]{0:T(1024)} %param.34) | copy-start | bytes 24580
  57.5 35.5 %copy-start.4 = (bf16[2048,64]{0,1:T(8,128)(2,1)S(1)}, bf16[2048,64]{0,1:T(8,128)(2,1)}, u32[]{:S(2)}) copy-start(bf16[2048,64]{0,1:T(8,128)(2,1)} %param.35) | copy-start | bytes 786436
  59.1 8.3 %all-to-all-start.1 = ((f32[4,1,8320]{2,1,0:T(1,128)}), f32[4,1,8320]{2,1,0:T(1,128)S(1)}, u32[]{:S(2)}, u32[]{:S(2)}) async-start(f32[4,1,8320]{2,1,0:T(1,128)} %copy.152), calls=%async_computation.1 | async-start | bytes 266240 | tf_op jit(solution)/shard_map/all_to_all | solution.py:223
  93.0 1.2 copy-start.3
  94.2 43.3 %copy-start.8 = (f32[2048]{0:T(1024)S(1)}, f32[2048]{0:T(1024)}, u32[]{:S(2)}) copy-start(f32[2048]{0:T(1024)} %param.42) | copy-start | bytes 24580
  117.5 19.6 %all-to-all-start.2 = ((bf16[32,4,2048]{2,1,0:T(4,128)(2,1)}), bf16[32,4,2048]{2,1,0:T(4,128)(2,1)S(1)}, u32[]{:S(2)}, u32[]{:S(2)}) async-start(bf16[32,4,2048]{2,1,0:T(4,128)(2,1)} %reshape.638), calls=%async_computation.2 | async-start | bytes 1048576 | tf_op jit(solution)/shard_map/all_to_all | solution.py:294
  137.6 4.7 %collective-permute-start = (bf16[4,2048]{1,0:T(4,128)(2,1)S(1)}, bf16[4,2048]{1,0:T(4,128)(2,1)S(1)}, u32[]{:S(2)}, u32[]{:S(2)}) collective-permute-start(bf16[4,2048]{1,0:T(4,128)(2,1)S(1)} %multiply_convert_fusion.2), channel_id=1, source_target_pairs={{0,4},{1,5},{2,6},{3,7},{4,0},{5,1},{6,2},{7,3},{8,12},{9,13},{10,... | collective-permute-start | bytes 49160 | tf_op jit(solution)/shard_map/ppermute | solution.py:310
  142.3 4.0 %collective-permute-start.1 = (bf16[8,2048]{1,0:T(8,128)(2,1)S(1)}, bf16[8,2048]{1,0:T(8,128)(2,1)S(1)}, u32[]{:S(2)}, u32[]{:S(2)}) collective-permute-start(bf16[8,2048]{1,0:T(8,128)(2,1)S(1)} %pad_maximum_fusion.3), channel_id=1, source_target_pairs={{0,2},{1,3},{2,0},{3,1},{4,6},{5,7},{6,4},{7,5},{8,10},{9,11},{10,... | collective-permute-start | bytes 98312 | tf_op jit(solution)/shard_map/ppermute | solution.py:310
  146.3 1.3 collective-permute-start.2
  147.7 26.1 %copy-start.1 = (bf16[512,2048]{1,0:T(8,128)(2,1)S(1)}, bf16[512,2048]{1,0:T(8,128)(2,1)}, u32[]{:S(2)}) copy-start(bf16[512,2048]{1,0:T(8,128)(2,1)} %param.31) | copy-start | bytes 6291460

commit v7 on v6

--- a/solution.py
+++ b/solution.py
@@ -257,9 +257,19 @@
     attn_parts = lax.all_gather(attn_part.astype(jnp.bfloat16), "seq", axis=0, tiled=False)
     resid_group = embedded + jnp.sum(attn_parts.astype(jnp.float32), axis=0)
     resid_share = lax.dynamic_slice_in_dim(resid_group, seq_index * share, share, 0)
-    moe_in = lax.all_gather(
-        rms_scale(resid_group, moe_gain).astype(jnp.bfloat16), "exp", axis=0, tiled=True
-    )
+    moe_group = rms_scale(resid_group, moe_gain).astype(jnp.bfloat16)
+    rounds = n_exp.bit_length() - 1
+    if n_exp == 1 << rounds:
+        flipped = jnp.arange(n_exp, dtype=jnp.int32) ^ lax.axis_index("exp")
+        block = sum(((flipped >> bit) & 1) << (rounds - 1 - bit) for bit in range(rounds))
+        for level in reversed(range(rounds)):
+            partner = [(i, i ^ (1 << level)) for i in range(n_exp)]
+            moe_group = jnp.concatenate([moe_group, lax.ppermute(moe_group, "exp", partner)], 0)
+        moe_in = jnp.take(moe_group.reshape(n_exp, group, width), block, axis=0).reshape(
+            tokens, width
+        )
+    else:
+        moe_in = lax.all_gather(moe_group, "exp", axis=0, tiled=True)
 
     router = jax.nn.sigmoid(jnp.dot(moe_in, w_router, preferred_element_type=jnp.float32))
     expert_count = w_router.shape[1]
@@ -303,15 +313,12 @@
     final_share = resid_share + term_sum
     norms_share = jnp.sqrt(jnp.mean(final_share * final_share, axis=-1))
     head_share = rms_scale(final_share, final_gain).astype(jnp.bfloat16)
-    rounds = n_exp.bit_length() - 1
     if n_exp == 1 << rounds:
         for level in reversed(range(rounds)):
             partner = [(i, i ^ (1 << level)) for i in range(n_exp)]
             head_share = jnp.concatenate([head_share, lax.ppermute(head_share, "exp", partner)], 0)
         head_in = lax.all_gather(head_share, "seq", axis=0, tiled=False).reshape(tokens, width)
         local_best = jnp.max(jnp.dot(head_in, w_head, preferred_element_type=jnp.float32), axis=-1)
-        flipped = jnp.arange(n_exp, dtype=jnp.int32) ^ lax.axis_index("exp")
-        block = sum(((flipped >> bit) & 1) << (rounds - 1 - bit) for bit in range(rounds))
         local_best = jnp.take(local_best.reshape(n_seq, n_exp, share), block, axis=1).reshape(tokens)
     else:
         head_in = gather_all(head_share).reshape(tokens, width)

time: 175 us -> 173 us (0.989)
  blocking collectives: 60.4 us -> 45.6 us
  waiting for transfers between devices: 31.2 us -> 42 us
    all_gather x1 -> x0, blocking collectives: 15 us -> none  [on_device(): lax.all_gather(rms_scale(resid_group, moe_gain).astype(jnp.bfloat16), 'ex...]
    ppermute x0 -> x3, waiting for transfers between devices: none -> 10.4 us  [on_device(): lax.ppermute(moe_group, 'exp', partner)]
  transfers between devices with their start and end apart: 6 -> 9, of which waited for: 6 -> 9; matrix products, arithmetic and copies ran while one was open for 8% -> 8% of each run, Pallas kernels for 0% -> 0%
where the time goes in v7:
time: 173 us; the launch traced here: 172 us
  blocking collectives  45.6 us (26%)
  waiting for transfers between devices  42 us (24%)
  local copies, waits for them, and re-layouts  26.8 us (15%)
  Pallas kernels  21.3 us (12%)
  starting transfers between devices  15.3 us (9%)
  matrix products  13.2 us (8%)
  other arithmetic  6.44 us (4%)
    pallas_call x1, Pallas kernels, experts(): pl.pallas_call(lambda *refs: experts_kernel(pieces, *refs), grid=(pieces...  21.3 us
    all_to_all x1, waiting for transfers between devices, on_device(): lax.all_to_all(term_rows.reshape(n_dev, share, width), ('exp', 'seq'), 0,...  16.2 us
    dot_general x3, local copies, waits for them, and re-layouts, project(): jnp.dot(attn_in, weight, preferred_element_type=jnp.float32)  11.9 us
    ppermute x3, waiting for transfers between devices, on_device(): lax.ppermute(moe_group, 'exp', partner)  10.4 us
    all_to_all x1, blocking collectives, on_device(): lax.all_to_all(jnp.broadcast_to(message[None, :], (n_dev, message.shape[0...  9.95 us
    all_gather x1, blocking collectives, on_device(): lax.all_gather(head_share, 'seq', axis=0, tiled=False)  9.07 us
    all_gather x1, blocking collectives, on_device(): row_parts = lax.all_gather(row_part, 'seq', axis=0, tiled=False)  9 us
    all_gather x1, blocking collectives, on_device(): lax.all_gather(jnp.stack([query_part, key_part, value_part], axis=0), 'se...  8.97 us
  transfers between devices with their start and end apart: 9, of which 9 were waited for; matrix products, arithmetic and copies ran while one was open for 8% of the time, Pallas kernels for 0%

profile of v7, /device:TPU:0, one launch (start us, length us, event | category | flops | bytes accessed | tf_op | source)
XLA Modules:
  0.0 171.8 jit_solution(2174879916198257784)
XLA Ops:
  2.4 5.1 %gather_fusion = bf16[128,2048]{1,0:T(8,128)(2,1)S(1)} fusion(bf16[1600,2048]{1,0:T(8,128)(2,1)} %param.26, s32[1024]{0:T(1024)S(1)} %pad_clamp_fusion.1), kind=kCustom, calls=%fused_computation | custom fusion | bytes 1049088 | tf_op jit(solution)/shard_map/jit(_take)/gather | solution.py:160
  9.1 6.3 %all-to-all-start = ((bf16[8,4,4,2048]{3,2,1,0:T(4,128)(2,1)}), bf16[8,4,4,2048]{3,2,1,0:T(4,128)(2,1)S(1)}, u32[]{:S(2)}, u32[]{:S(2)}) async-start(bf16[8,4,4,2048]{3,2,1,0:T(4,128)(2,1)} %select_select_fusion), calls=%async_computation | async-start | bytes 1048576 | tf_op jit(solution)/shard_map/all_to_all | solution.py:162
  16.5 4.0 %copy.172 = bf16[512,2048]{1,0:T(8,128)(2,1)} copy(bf16[512,2048]{0,1:T(8,128)(2,1)} %bitcast.133) | data formatting | bytes 4194304 | tf_op jit(solution)/shard_map/dot_general | solution.py:173
  20.5 4.0 %copy.170 = bf16[512,2048]{1,0:T(8,128)(2,1)} copy(bf16[512,2048]{0,1:T(8,128)(2,1)} %bitcast.134) | data formatting | bytes 4194304 | tf_op jit(solution)/shard_map/dot_general | solution.py:173
  24.5 3.9 %copy.171 = bf16[512,2048]{1,0:T(8,128)(2,1)} copy(bf16[512,2048]{0,1:T(8,128)(2,1)} %bitcast.135) | data formatting | bytes 4194304 | tf_op jit(solution)/shard_map/dot_general | solution.py:173
  28.7 2.1 %all-to-all-done = bf16[8,4,4,2048]{3,2,1,0:T(4,128)(2,1)S(1)} async-done(((bf16[8,4,4,2048]{3,2,1,0:T(4,128)(2,1)}), bf16[8,4,4,2048]{3,2,1,0:T(4,128)(2,1)S(1)}, u32[]{:S(2)}, u32[]{:S(2)}) %all-to-all-start) | async-done | bytes 524320 | tf_op jit(solution)/shard_map/all_to_all | solution.py:162
  31.1 9.0 %all-gather = bf16[16,4,2048]{2,1,0:T(4,128)(2,1)S(1)} all-gather(bf16[4,4,2048]{2,1,0:T(4,128)(2,1)S(1)} %reduce_sum.137), channel_id=2, replica_groups=mesh['seq'=4,'exp'=8] {'seq'}, dimensions={0}, use_global_device_ids=true | all-gather | bytes 327680 | tf_op jit(solution)/shard_map/all_gather | solution.py:164
  40.5 2.4 %convolution_convert_fusion.1 = bf16[16,4,128]{2,0,1:T(8,128)(2,1)S(1)} fusion(bf16[16,2048,1]{1,0,2:T(8,128)(2,1)S(1)} %reshape.681, bf16[4,128,2048]{2,1,0:T(8,128)(2,1)} %bitcast.131), kind=kOutput, calls=%fused_computation.24 | convolution fusion | flops 33562624 | bytes 2179072 | tf_op jit(solution)/shard_map/dot_general | solution.py:173
  42.9 2.3 %fusion.48 = f32[16,4,128]{2,0,1:T(8,128)S(1)} fusion(bf16[16,2048,1]{1,0,2:T(8,128)(2,1)S(1)} %reshape.681, bf16[4,128,2048]{2,1,0:T(8,128)(2,1)} %bitcast.130), kind=kOutput, calls=%fused_computation.123 | convolution fusion | flops 33554432 | bytes 2195456 | tf_op jit(solution)/shard_map/dot_general | solution.py:173
  46.1 9.0 %all-gather.1 = bf16[12,16,4,128]{3,1,2,0:T(8,128)(2,1)S(1)} all-gather(bf16[3,16,4,128]{3,1,2,0:T(8,128)(2,1)S(1)} %pad_maximum_fusion.5), channel_id=3, replica_groups=mesh['seq'=4,'exp'=8] {'seq'}, dimensions={0}, use_global_device_ids=true | all-gather | bytes 245760 | tf_op jit(solution)/shard_map/all_gather | solution.py:180
  59.1 3.3 %all-to-all-start.1 = ((f32[4,1,8320]{2,1,0:T(1,128)}), f32[4,1,8320]{2,1,0:T(1,128)S(1)}, u32[]{:S(2)}, u32[]{:S(2)}) async-start(f32[4,1,8320]{2,1,0:T(1,128)} %copy.152), calls=%async_computation.1 | async-start | bytes 266240 | tf_op jit(solution)/shard_map/all_to_all | solution.py:223
  63.0 4.4 %all-to-all-done.1 = f32[4,1,8320]{2,1,0:T(1,128)S(1)} async-done(((f32[4,1,8320]{2,1,0:T(1,128)}), f32[4,1,8320]{2,1,0:T(1,128)S(1)}, u32[]{:S(2)}, u32[]{:S(2)}) %all-to-all-start.1) | async-done | bytes 133152 | tf_op jit(solution)/shard_map/all_to_all | solution.py:223
  69.3 8.6 %all-gather.2 = bf16[64,2048]{1,0:T(8,128)(2,1)S(1)} all-gather(bf16[16,2048]{1,0:T(8,128)(2,1)S(1)} %convolution_convert_fusion), channel_id=4, replica_groups=mesh['seq'=4,'exp'=8] {'seq'}, dimensions={0}, use_global_device_ids=true | all-gather | bytes 327680 | tf_op jit(solution)/shard_map/all_gather | solution.py:257
  78.9 4.5 %collective-permute-done = bf16[16,2048]{1,0:T(8,128)(2,1)S(1)} collective-permute-done((bf16[16,2048]{1,0:T(8,128)(2,1)S(1)}, bf16[16,2048]{1,0:T(8,128)(2,1)S(1)}, u32[]{:S(2)}, u32[]{:S(2)}) %collective-permute-start) | collective-permute-done | bytes 65568 | tf_op jit(solution)/shard_map/ppermute | solution.py:267
  83.5 4.9 %collective-permute-done.1 = bf16[32,2048]{1,0:T(8,128)(2,1)S(1)} collective-permute-done((bf16[32,2048]{1,0:T(8,128)(2,1)S(1)}, bf16[32,2048]{1,0:T(8,128)(2,1)S(1)}, u32[]{:S(2)}, u32[]{:S(2)}) %collective-permute-start.1) | collective-permute-done | bytes 131104 | tf_op jit(solution)/shard_map/ppermute | solution.py:267
  92.0 21.3 %shard_map.221 = bf16[128,2048]{1,0:T(8,128)(2,1)} custom-call(bf16[128,2048]{1,0:T(8,128)(2,1)} %copy-done.3, f32[128,128]{1,0:T(8,128)} %pad.4.refs_1_, bf16[8,352,2048]{2,1,0:T(8,128)(2,1)} %bitcast.128, bf16[8,352,2048]{2,1,0:T(8,128)(2,1)} %bitcast.129, bf16[8,352,2048]{2,1,0:T(8,128)(2,1)} %refs_4_.1, bf16[352,2048]{1,0:T(8,128)(2,1)} %bitcast.137, ...), custom_call_target="tpu_custom_call" | custom-call | flops 4982833152 | bytes 39976960 | tf_op jit(solution)/shard_map/pallas_call | solution.py:84
  113.3 2.0 %reshape.645 = bf16[32,4,2048]{2,1,0:T(4,128)(2,1)} reshape(bf16[128,2048]{1,0:T(8,128)(2,1)} %shard_map.221) | data formatting | bytes 1048576 | tf_op jit(solution)/shard_map/reshape | solution.py:305
  115.4 3.6 %all-to-all-start.2 = ((bf16[32,4,2048]{2,1,0:T(4,128)(2,1)}), bf16[32,4,2048]{2,1,0:T(4,128)(2,1)S(1)}, u32[]{:S(2)}, u32[]{:S(2)}) async-start(bf16[32,4,2048]{2,1,0:T(4,128)(2,1)} %reshape.645), calls=%async_computation.2 | async-start | bytes 1048576 | tf_op jit(solution)/shard_map/all_to_all | solution.py:304
  118.9 16.2 %all-to-all-done.2 = bf16[32,4,2048]{2,1,0:T(4,128)(2,1)S(1)} async-done(((bf16[32,4,2048]{2,1,0:T(4,128)(2,1)}), bf16[32,4,2048]{2,1,0:T(4,128)(2,1)S(1)}, u32[]{:S(2)}, u32[]{:S(2)}) %all-to-all-start.2) | async-done | bytes 524320 | tf_op jit(solution)/shard_map/all_to_all | solution.py:304
  135.7 4.6 %collective-permute-done.3 = bf16[4,2048]{1,0:T(4,128)(2,1)S(1)} collective-permute-done((bf16[4,2048]{1,0:T(4,128)(2,1)S(1)}, bf16[4,2048]{1,0:T(4,128)(2,1)S(1)}, u32[]{:S(2)}, u32[]{:S(2)}) %collective-permute-start.3) | collective-permute-done | bytes 16416 | tf_op jit(solution)/shard_map/ppermute | solution.py:319
  141.4 2.9 %collective-permute-done.4 = bf16[8,2048]{1,0:T(8,128)(2,1)S(1)} collective-permute-done((bf16[8,2048]{1,0:T(8,128)(2,1)S(1)}, bf16[8,2048]{1,0:T(8,128)(2,1)S(1)}, u32[]{:S(2)}, u32[]{:S(2)}) %collective-permute-start.4) | collective-permute-done | bytes 32800 | tf_op jit(solution)/shard_map/ppermute | solution.py:319
  145.7 9.1 %all-gather.3 = bf16[128,2048]{1,0:T(8,128)(2,1)S(1)} all-gather(bf16[32,2048]{1,0:T(8,128)(2,1)S(1)} %pad_maximum_fusion.3), channel_id=5, replica_groups=mesh['seq'=4,'exp'=8] {'seq'}, dimensions={0}, use_global_device_ids=true | all-gather | bytes 655360 | tf_op jit(solution)/shard_map/all_gather | solution.py:320
  154.8 4.7 %convolution_reduce_fusion = f32[128]{0:T(128)S(1)} fusion(bf16[128,2048]{1,0:T(8,128)(2,1)S(1)} %all-gather.3, bf16[2048,1600]{0,1:T(8,128)(2,1)} %param.43), kind=kOutput, calls=%fused_computation.10 | convolution fusion | flops 839065472 | bytes 7078400 | tf_op jit(solution)/shard_map/dot_general | solution.py:321
  160.5 9.9 %all_to_all.31 = f32[32,1,132]{2,1,0:T(1,128)S(1)} all-to-all(f32[32,1,132]{2,1,0:T(1,128)S(1)} %broadcast_in_dim.175), channel_id=1, replica_groups=mesh['seq'=4,'exp'=8] {'seq','exp'}, dimensions={0} | all-to-all | bytes 33792 | tf_op jit(solution)/shard_map/all_to_all | solution.py:327
  (151 shorter events, 22.3 us)
Async XLA Ops:
  0.6 68.2 %copy-start = (bf16[512,2048]{1,0:T(8,128)(2,1)S(1)}, bf16[512,2048]{1,0:T(8,128)(2,1)}, u32[]{:S(2)}) copy-start(bf16[512,2048]{1,0:T(8,128)(2,1)} %param.31) | copy-start | bytes 6291460
  0.6 15.8 %copy-start.11 = (s32[32]{0:T(128)S(1)}, s32[32]{0:T(128)}, u32[]{:S(2)}) copy-start(s32[32]{0:T(128)} %param.23) | copy-start | bytes 388
  9.1 21.7 %all-to-all-start = ((bf16[8,4,4,2048]{3,2,1,0:T(4,128)(2,1)}), bf16[8,4,4,2048]{3,2,1,0:T(4,128)(2,1)S(1)}, u32[]{:S(2)}, u32[]{:S(2)}) async-start(bf16[8,4,4,2048]{3,2,1,0:T(4,128)(2,1)} %select_select_fusion), calls=%async_computation | async-start | bytes 1048576 | tf_op jit(solution)/shard_map/all_to_all | solution.py:162
  20.5 19.9 %copy-start.6 = (f32[2048]{0:T(1024)S(1)}, f32[2048]{0:T(1024)}, u32[]{:S(2)}) copy-start(f32[2048]{0:T(1024)} %param.27) | copy-start | bytes 24580
  40.5 4.7 %copy-start.2 = (bf16[512,2048]{1,0:T(8,128)(2,1)S(1)}, bf16[512,2048]{1,0:T(8,128)(2,1)}, u32[]{:S(2)}) copy-start(bf16[512,2048]{1,0:T(8,128)(2,1)} %copy.171) | copy-start | bytes 6291460
  40.5 14.6 %copy-start.9 = (bf16[4,256,2048]{2,1,0:T(8,128)(2,1)S(1)}, bf16[4,256,2048]{2,1,0:T(8,128)(2,1)}, u32[]{:S(2)}) copy-start(bf16[4,256,2048]{2,1,0:T(8,128)(2,1)} %param.32) | copy-start | bytes 12582916
  45.2 11.5 %copy-start.10 = (bf16[4,256,2048]{2,1,0:T(8,128)(2,1)S(1)}, bf16[4,256,2048]{2,1,0:T(8,128)(2,1)}, u32[]{:S(2)}) copy-start(bf16[4,256,2048]{2,1,0:T(8,128)(2,1)} %param.33) | copy-start | bytes 12582916
  57.5 20.6 %copy-start.7 = (f32[2048]{0:T(1024)S(1)}, f32[2048]{0:T(1024)}, u32[]{:S(2)}) copy-start(f32[2048]{0:T(1024)} %param.34) | copy-start | bytes 24580
  57.5 31.2 %copy-start.5 = (s32[4,32,6]{1,0,2:T(4,128)S(1)}, s32[4,32,6]{1,0,2:T(4,128)}, u32[]{:S(2)}) copy-start(s32[4,32,6]{1,0,2:T(4,128)} %param.25) | copy-start | bytes 9220
  59.1 8.3 %all-to-all-start.1 = ((f32[4,1,8320]{2,1,0:T(1,128)}), f32[4,1,8320]{2,1,0:T(1,128)S(1)}, u32[]{:S(2)}, u32[]{:S(2)}) async-start(f32[4,1,8320]{2,1,0:T(1,128)} %copy.152), calls=%async_computation.1 | async-start | bytes 266240 | tf_op jit(solution)/shard_map/all_to_all | solution.py:223
  68.6 22.2 %copy-start.4 = (bf16[2048,64]{0,1:T(8,128)(2,1)S(1)}, bf16[2048,64]{0,1:T(8,128)(2,1)}, u32[]{:S(2)}) copy-start(bf16[2048,64]{0,1:T(8,128)(2,1)} %param.35) | copy-start | bytes 786436
  78.1 5.2 %collective-permute-start = (bf16[16,2048]{1,0:T(8,128)(2,1)S(1)}, bf16[16,2048]{1,0:T(8,128)(2,1)S(1)}, u32[]{:S(2)}, u32[]{:S(2)}) collective-permute-start(bf16[16,2048]{1,0:T(8,128)(2,1)S(1)} %multiply_convert_fusion), channel_id=1, source_target_pairs={{0,4},{1,5},{2,6},{3,7},{4,0},{5,1},{6,2},{7,3},{8,12},{9,13},{10,... | collective-permute-start | bytes 196616 | tf_op jit(solution)/shard_map/ppermute | solution.py:267
  83.4 5.0 %collective-permute-start.1 = (bf16[32,2048]{1,0:T(8,128)(2,1)S(1)}, bf16[32,2048]{1,0:T(8,128)(2,1)S(1)}, u32[]{:S(2)}, u32[]{:S(2)}) collective-permute-start(bf16[32,2048]{1,0:T(8,128)(2,1)S(1)} %pad_maximum_fusion.2), channel_id=1, source_target_pairs={{0,2},{1,3},{2,0},{3,1},{4,6},{5,7},{6,4},{7,5},{8,10},{9,11},{10,... | collective-permute-start | bytes 393224 | tf_op jit(solution)/shard_map/ppermute | solution.py:267
  88.4 1.6 collective-permute-start.2
  90.8 1.2 copy-start.3
  92.0 43.5 %copy-start.8 = (f32[2048]{0:T(1024)S(1)}, f32[2048]{0:T(1024)}, u32[]{:S(2)}) copy-start(f32[2048]{0:T(1024)} %param.42) | copy-start | bytes 24580
  115.4 19.8 %all-to-all-start.2 = ((bf16[32,4,2048]{2,1,0:T(4,128)(2,1)}), bf16[32,4,2048]{2,1,0:T(4,128)(2,1)S(1)}, u32[]{:S(2)}, u32[]{:S(2)}) async-start(bf16[32,4,2048]{2,1,0:T(4,128)(2,1)} %reshape.645), calls=%async_computation.2 | async-start | bytes 1048576 | tf_op jit(solution)/shard_map/all_to_all | solution.py:304
  135.6 4.7 %collective-permute-start.3 = (bf16[4,2048]{1,0:T(4,128)(2,1)S(1)}, bf16[4,2048]{1,0:T(4,128)(2,1)S(1)}, u32[]{:S(2)}, u32[]{:S(2)}) collective-permute-start(bf16[4,2048]{1,0:T(4,128)(2,1)S(1)} %multiply_convert_fusion.2), channel_id=1, source_target_pairs={{0,4},{1,5},{2,6},{3,7},{4,0},{5,1},{6,2},{7,3},{8,12},{9,13},{10,... | collective-permute-start | bytes 49160 | tf_op jit(solution)/shard_map/ppermute | solution.py:319
  140.4 4.0 %collective-permute-start.4 = (bf16[8,2048]{1,0:T(8,128)(2,1)S(1)}, bf16[8,2048]{1,0:T(8,128)(2,1)S(1)}, u32[]{:S(2)}, u32[]{:S(2)}) collective-permute-start(bf16[8,2048]{1,0:T(8,128)(2,1)S(1)} %pad_maximum_fusion.6), channel_id=1, source_target_pairs={{0,2},{1,3},{2,0},{3,1},{4,6},{5,7},{6,4},{7,5},{8,10},{9,11},{10,... | collective-permute-start | bytes 98312 | tf_op jit(solution)/shard_map/ppermute | solution.py:319
  144.4 1.3 collective-permute-start.5
  145.7 26.1 %copy-start.1 = (bf16[512,2048]{1,0:T(8,128)(2,1)S(1)}, bf16[512,2048]{1,0:T(8,128)(2,1)}, u32[]{:S(2)}) copy-start(bf16[512,2048]{1,0:T(8,128)(2,1)} %param.31) | copy-start | bytes 6291460

commit v8 on v7

--- a/solution.py
+++ b/solution.py
@@ -37,6 +37,25 @@
 def gather_all(values):
     inner = lax.all_gather(values, "exp", axis=0, tiled=False)
     return lax.all_gather(inner, "seq", axis=0, tiled=False)
+
+
+def butterfly(values, axis, count):
+    rounds = count.bit_length() - 1
+    stacked = values[None]
+    for level in reversed(range(rounds)):
+        partner = [(i, i ^ (1 << level)) for i in range(count)]
+        stacked = jnp.concatenate([stacked, lax.ppermute(stacked, axis, partner)], 0)
+    flipped = jnp.arange(count, dtype=jnp.int32) ^ lax.axis_index(axis)
+    block = sum(((flipped >> bit) & 1) << (rounds - 1 - bit) for bit in range(rounds))
+    return stacked, block
+
+
+def gather_seq(values, ordered):
+    count = lax.axis_size("seq")
+    if count != 1 << (count.bit_length() - 1):
+        return lax.all_gather(values, "seq", axis=0, tiled=False)
+    stacked, block = butterfly(values, "seq", count)
+    return jnp.take(stacked, block, axis=0) if ordered else stacked
 
 
 def experts_kernel(pieces, x_ref, weight_ref, gate_ref, up_ref, down_ref, sgate_ref, sup_ref, sdown_ref, out_ref, total_ref):
@@ -161,7 +180,7 @@
     rows = jnp.where(held[..., None], rows, jnp.zeros((), rows.dtype))
     arrived = lax.all_to_all(rows, "exp", 0, 0, tiled=True)
     row_part = jnp.sum(arrived.astype(jnp.float32), axis=0).astype(jnp.bfloat16)
-    row_parts = lax.all_gather(row_part, "seq", axis=0, tiled=False)
+    row_parts = gather_seq(row_part, False)
     embedded = jnp.sum(row_parts.astype(jnp.float32), axis=0).reshape(group, width)
 
     attn_in = rms_scale(embedded, attn_gain).astype(jnp.bfloat16)
@@ -177,9 +196,7 @@
     query_part = rotate(project(w_query), places).astype(jnp.bfloat16)
     key_part = rotate(project(w_key), places).astype(jnp.bfloat16)
     value_part = project(w_value).astype(jnp.bfloat16)
-    every = lax.all_gather(
-        jnp.stack([query_part, key_part, value_part], axis=0), "seq", axis=0, tiled=False
-    )
+    every = gather_seq(jnp.stack([query_part, key_part, value_part], axis=0), True)
     head_count = n_seq * heads_here
     every = jnp.moveaxis(every, 0, 2).reshape(3, steps, own_count, head_count, HDIM)
     queries = every[0]
@@ -254,7 +271,7 @@
     )
 
     attn_part = jnp.dot(own_heads, w_out, preferred_element_type=jnp.float32)
-    attn_parts = lax.all_gather(attn_part.astype(jnp.bfloat16), "seq", axis=0, tiled=False)
+    attn_parts = gather_seq(attn_part.astype(jnp.bfloat16), False)
     resid_group = embedded + jnp.sum(attn_parts.astype(jnp.float32), axis=0)
     resid_share = lax.dynamic_slice_in_dim(resid_group, seq_index * share, share, 0)
     moe_group = rms_scale(resid_group, moe_gain).astype(jnp.bfloat16)

time: 173 us -> 184 us (1.064)
  waiting for transfers between devices: 42 us -> 71.1 us
  blocking collectives: 45.6 us -> 19 us
  starting transfers between devices: 15.3 us -> 21.2 us
  matrix products: 13.2 us -> 15.5 us
    all_gather x3 -> x0, blocking collectives: 26.5 us -> none  [the longest x1 9 us: on_device(): row_parts = lax.all_gather(row_part, 'seq', axis=0, tiled=False)]
    ppermute x0 -> x6, waiting for transfers between devices: none -> 16.1 us  [butterfly(): lax.ppermute(stacked, axis, partner)]
    all_to_all x1, waiting for transfers between devices: 2.11 us -> 14 us  [on_device(): arrived = lax.all_to_all(rows, 'exp', 0, 0, tiled=True)]
    ppermute x0 -> x6, starting transfers between devices: none -> 7.38 us  [butterfly(): lax.ppermute(stacked, axis, partner)]
    dot_general x1, matrix products: 1.26 us -> 3.6 us  [on_device(): jnp.einsum('trhd,rphd->trhp', queries, cache_keys, preferred_element_type...]
  transfers between devices with their start and end apart: 9 -> 15, of which waited for: 9 -> 14; matrix products, arithmetic and copies ran while one was open for 8% -> 8% of each run, Pallas kernels for 0% -> 0%
where the time goes in v8:
time: 184 us; the launch traced here: 183 us
  waiting for transfers between devices  71.1 us (39%)
  local copies, waits for them, and re-layouts  27.3 us (15%)
  Pallas kernels  21.3 us (12%)
  starting transfers between devices  21.2 us (12%)
  blocking collectives  19 us (10%)
  matrix products  15.5 us (8%)
  other arithmetic  6.7 us (4%)
    pallas_call x1, Pallas kernels, experts(): pl.pallas_call(lambda *refs: experts_kernel(pieces, *refs), grid=(pieces...  21.3 us
    all_to_all x1, waiting for transfers between devices, on_device(): lax.all_to_all(term_rows.reshape(n_dev, share, width), ('exp', 'seq'), 0,...  16.2 us
    ppermute x6, waiting for transfers between devices, butterfly(): lax.ppermute(stacked, axis, partner)  16.1 us
    all_to_all x1, waiting for transfers between devices, on_device(): arrived = lax.all_to_all(rows, 'exp', 0, 0, tiled=True)  14 us
    dot_general x3, local copies, waits for them, and re-layouts, project(): jnp.dot(attn_in, weight, preferred_element_type=jnp.float32)  11.9 us
    ppermute x3, waiting for transfers between devices, on_device(): lax.ppermute(moe_group, 'exp', partner)  11.1 us
    all_to_all x1, blocking collectives, on_device(): lax.all_to_all(jnp.broadcast_to(message[None, :], (n_dev, message.shape[0...  9.93 us
    all_gather x1, blocking collectives, on_device(): lax.all_gather(head_share, 'seq', axis=0, tiled=False)  9.07 us
  transfers between devices with their start and end apart: 15, of which 14 were waited for; matrix products, arithmetic and copies ran while one was open for 8% of the time, Pallas kernels for 0%

profile of v8, /device:TPU:0, one launch (start us, length us, event | category | flops | bytes accessed | tf_op | source)
XLA Modules:
  0.0 183.3 jit_solution(16037469284948570275)
XLA Ops:
  2.4 5.1 %gather_fusion = bf16[128,2048]{1,0:T(8,128)(2,1)S(1)} fusion(bf16[1600,2048]{1,0:T(8,128)(2,1)} %param.26, s32[1024]{0:T(1024)S(1)} %pad_clamp_fusion.2), kind=kCustom, calls=%fused_computation | custom fusion | bytes 1049088 | tf_op jit(solution)/shard_map/jit(_take)/gather | solution.py:179
  9.1 6.3 %all-to-all-start = ((bf16[8,4,4,2048]{3,2,1,0:T(4,128)(2,1)}), bf16[8,4,4,2048]{3,2,1,0:T(4,128)(2,1)S(1)}, u32[]{:S(2)}, u32[]{:S(2)}) async-start(bf16[8,4,4,2048]{3,2,1,0:T(4,128)(2,1)} %select_select_fusion), calls=%async_computation | async-start | bytes 1048576 | tf_op jit(solution)/shard_map/all_to_all | solution.py:181
  16.8 14.0 %all-to-all-done = bf16[8,4,4,2048]{3,2,1,0:T(4,128)(2,1)S(1)} async-done(((bf16[8,4,4,2048]{3,2,1,0:T(4,128)(2,1)}), bf16[8,4,4,2048]{3,2,1,0:T(4,128)(2,1)S(1)}, u32[]{:S(2)}, u32[]{:S(2)}) %all-to-all-start) | async-done | bytes 524320 | tf_op jit(solution)/shard_map/all_to_all | solution.py:181
  32.6 2.7 %collective-permute-done = bf16[1,4,4,2048]{3,2,1,0:T(4,128)(2,1)S(1)} collective-permute-done((bf16[1,4,4,2048]{3,2,1,0:T(4,128)(2,1)S(1)}, bf16[1,4,4,2048]{3,2,1,0:T(4,128)(2,1)S(1)}, u32[]{:S(2)}, u32[]{:S(2)}) %collective-permute-start) | collective-permute-done | bytes 65568 | tf_op jit(solution)/shard_map/ppermute | solution.py:47
  37.0 4.0 %copy.169 = bf16[512,2048]{1,0:T(8,128)(2,1)} copy(bf16[512,2048]{0,1:T(8,128)(2,1)} %bitcast.134) | data formatting | bytes 4194304 | tf_op jit(solution)/shard_map/dot_general | solution.py:192
  41.0 4.0 %copy.167 = bf16[512,2048]{1,0:T(8,128)(2,1)} copy(bf16[512,2048]{0,1:T(8,128)(2,1)} %bitcast.135) | data formatting | bytes 4194304 | tf_op jit(solution)/shard_map/dot_general | solution.py:192
  45.0 3.9 %copy.168 = bf16[512,2048]{1,0:T(8,128)(2,1)} copy(bf16[512,2048]{0,1:T(8,128)(2,1)} %bitcast.136) | data formatting | bytes 4194304 | tf_op jit(solution)/shard_map/dot_general | solution.py:192
  56.5 2.5 %collective-permute-done.2 = bf16[1,3,16,4,128]{4,2,3,1,0:T(8,128)(2,1)S(1)} collective-permute-done((bf16[1,3,16,4,128]{4,2,3,1,0:T(8,128)(2,1)S(1)}, bf16[1,3,16,4,128]{4,2,3,1,0:T(8,128)(2,1)S(1)}, u32[]{:S(2)}, u32[]{:S(2)}) %collective-permute-start.2) | collective-permute-done | bytes 49184 | tf_op jit(solution)/shard_map/ppermute | solution.py:47
  60.1 3.6 %collective-permute-done.3 = bf16[2,3,16,4,128]{4,2,3,1,0:T(8,128)(2,1)S(1)} collective-permute-done((bf16[2,3,16,4,128]{4,2,3,1,0:T(8,128)(2,1)S(1)}, bf16[2,3,16,4,128]{4,2,3,1,0:T(8,128)(2,1)S(1)}, u32[]{:S(2)}, u32[]{:S(2)}) %collective-permute-start.3) | collective-permute-done | bytes 98336 | tf_op jit(solution)/shard_map/ppermute | solution.py:47
  64.5 3.6 %select_reduce_fusion = (f32[4,4,16]{0,2,1:T(8,128)S(1)}, f32[4,4,16,256]{3,0,2,1:T(4,128)S(1)}) fusion(pred[4,256]{1,0:T(4,128)(4,1)S(1)} %compare_and_fusion.1, bf16[4,4,16,128]{3,1,0,2:T(4,128)(2,1)S(1)} %bitcast.168, bf16[4,256,2048]{2,1,0:T(8,128)(2,1)} %param.32), kind=kOutput, calls=%fused_computation.35 | convolution fusion | flops 16973568 | bytes 4524032 | tf_op jit(solution)/shard_map/trhd,rphd->trhp/dot_general | solution.py:217
  70.8 3.5 %all-to-all-start.1 = ((f32[4,1,8320]{2,1,0:T(1,128)}), f32[4,1,8320]{2,1,0:T(1,128)S(1)}, u32[]{:S(2)}, u32[]{:S(2)}) async-start(f32[4,1,8320]{2,1,0:T(1,128)} %copy.149), calls=%async_computation.1 | async-start | bytes 266240 | tf_op jit(solution)/shard_map/all_to_all | solution.py:240
  74.3 4.9 %all-to-all-done.1 = f32[4,1,8320]{2,1,0:T(1,128)S(1)} async-done(((f32[4,1,8320]{2,1,0:T(1,128)}), f32[4,1,8320]{2,1,0:T(1,128)S(1)}, u32[]{:S(2)}, u32[]{:S(2)}) %all-to-all-start.1) | async-done | bytes 133152 | tf_op jit(solution)/shard_map/all_to_all | solution.py:240
  81.8 3.5 %collective-permute-done.4 = bf16[1,16,2048]{2,1,0:T(8,128)(2,1)S(1)} collective-permute-done((bf16[1,16,2048]{2,1,0:T(8,128)(2,1)S(1)}, bf16[1,16,2048]{2,1,0:T(8,128)(2,1)S(1)}, u32[]{:S(2)}, u32[]{:S(2)}) %collective-permute-start.4) | collective-permute-done | bytes 65568 | tf_op jit(solution)/shard_map/ppermute | solution.py:47
  86.6 3.8 %collective-permute-done.5 = bf16[2,16,2048]{2,1,0:T(8,128)(2,1)S(1)} collective-permute-done((bf16[2,16,2048]{2,1,0:T(8,128)(2,1)S(1)}, bf16[2,16,2048]{2,1,0:T(8,128)(2,1)S(1)}, u32[]{:S(2)}, u32[]{:S(2)}) %collective-permute-start.5) | collective-permute-done | bytes 131104 | tf_op jit(solution)/shard_map/ppermute | solution.py:47
  90.7 5.2 %collective-permute-done.6 = bf16[16,2048]{1,0:T(8,128)(2,1)S(1)} collective-permute-done((bf16[16,2048]{1,0:T(8,128)(2,1)S(1)}, bf16[16,2048]{1,0:T(8,128)(2,1)S(1)}, u32[]{:S(2)}, u32[]{:S(2)}) %collective-permute-start.6) | collective-permute-done | bytes 65568 | tf_op jit(solution)/shard_map/ppermute | solution.py:284
  96.0 4.9 %collective-permute-done.7 = bf16[32,2048]{1,0:T(8,128)(2,1)S(1)} collective-permute-done((bf16[32,2048]{1,0:T(8,128)(2,1)S(1)}, bf16[32,2048]{1,0:T(8,128)(2,1)S(1)}, u32[]{:S(2)}, u32[]{:S(2)}) %collective-permute-start.7) | collective-permute-done | bytes 131104 | tf_op jit(solution)/shard_map/ppermute | solution.py:284
  104.5 21.3 %shard_map.221 = bf16[128,2048]{1,0:T(8,128)(2,1)} custom-call(bf16[128,2048]{1,0:T(8,128)(2,1)} %copy-done.3, f32[128,128]{1,0:T(8,128)} %pad.4.refs_1_, bf16[8,352,2048]{2,1,0:T(8,128)(2,1)} %bitcast.129, bf16[8,352,2048]{2,1,0:T(8,128)(2,1)} %bitcast.130, bf16[8,352,2048]{2,1,0:T(8,128)(2,1)} %refs_4_.1, bf16[352,2048]{1,0:T(8,128)(2,1)} %bitcast.138, ...), custom_call_target="tpu_custom_call" | custom-call | flops 4982833152 | bytes 39976960 | tf_op jit(solution)/shard_map/pallas_call | solution.py:103
  127.8 2.6 %all-to-all-start.2 = ((bf16[32,4,2048]{2,1,0:T(4,128)(2,1)}), bf16[32,4,2048]{2,1,0:T(4,128)(2,1)S(1)}, u32[]{:S(2)}, u32[]{:S(2)}) async-start(bf16[32,4,2048]{2,1,0:T(4,128)(2,1)} %reshape.687), calls=%async_computation.2 | async-start | bytes 1048576 | tf_op jit(solution)/shard_map/all_to_all | solution.py:321
  130.5 16.2 %all-to-all-done.2 = bf16[32,4,2048]{2,1,0:T(4,128)(2,1)S(1)} async-done(((bf16[32,4,2048]{2,1,0:T(4,128)(2,1)}), bf16[32,4,2048]{2,1,0:T(4,128)(2,1)S(1)}, u32[]{:S(2)}, u32[]{:S(2)}) %all-to-all-start.2) | async-done | bytes 524320 | tf_op jit(solution)/shard_map/all_to_all | solution.py:321
  147.2 4.6 %collective-permute-done.9 = bf16[4,2048]{1,0:T(4,128)(2,1)S(1)} collective-permute-done((bf16[4,2048]{1,0:T(4,128)(2,1)S(1)}, bf16[4,2048]{1,0:T(4,128)(2,1)S(1)}, u32[]{:S(2)}, u32[]{:S(2)}) %collective-permute-start.9) | collective-permute-done | bytes 16416 | tf_op jit(solution)/shard_map/ppermute | solution.py:336
  152.9 2.9 %collective-permute-done.10 = bf16[8,2048]{1,0:T(8,128)(2,1)S(1)} collective-permute-done((bf16[8,2048]{1,0:T(8,128)(2,1)S(1)}, bf16[8,2048]{1,0:T(8,128)(2,1)S(1)}, u32[]{:S(2)}, u32[]{:S(2)}) %collective-permute-start.10) | collective-permute-done | bytes 32800 | tf_op jit(solution)/shard_map/ppermute | solution.py:336
  157.3 9.1 %all-gather = bf16[128,2048]{1,0:T(8,128)(2,1)S(1)} all-gather(bf16[32,2048]{1,0:T(8,128)(2,1)S(1)} %pad_maximum_fusion.6), channel_id=2, replica_groups=mesh['seq'=4,'exp'=8] {'seq'}, dimensions={0}, use_global_device_ids=true | all-gather | bytes 655360 | tf_op jit(solution)/shard_map/all_gather | solution.py:337
  166.4 4.7 %convolution_reduce_fusion = f32[128]{0:T(128)S(1)} fusion(bf16[128,2048]{1,0:T(8,128)(2,1)S(1)} %all-gather, bf16[2048,1600]{0,1:T(8,128)(2,1)} %param.43), kind=kOutput, calls=%fused_computation.12 | convolution fusion | flops 839065472 | bytes 7078400 | tf_op jit(solution)/shard_map/dot_general | solution.py:338
  172.0 9.9 %all_to_all.31 = f32[32,1,132]{2,1,0:T(1,128)S(1)} all-to-all(f32[32,1,132]{2,1,0:T(1,128)S(1)} %broadcast_in_dim.199), channel_id=1, replica_groups=mesh['seq'=4,'exp'=8] {'seq','exp'}, dimensions={0} | all-to-all | bytes 33792 | tf_op jit(solution)/shard_map/all_to_all | solution.py:344
  (166 shorter events, 35.1 us)
Async XLA Ops:
  0.6 80.0 %copy-start = (bf16[512,2048]{1,0:T(8,128)(2,1)S(1)}, bf16[512,2048]{1,0:T(8,128)(2,1)}, u32[]{:S(2)}) copy-start(bf16[512,2048]{1,0:T(8,128)(2,1)} %param.31) | copy-start | bytes 6291460
  0.6 15.7 %copy-start.10 = (s32[32]{0:T(128)S(1)}, s32[32]{0:T(128)}, u32[]{:S(2)}) copy-start(s32[32]{0:T(128)} %param.23) | copy-start | bytes 388
  9.1 21.7 %all-to-all-start = ((bf16[8,4,4,2048]{3,2,1,0:T(4,128)(2,1)}), bf16[8,4,4,2048]{3,2,1,0:T(4,128)(2,1)S(1)}, u32[]{:S(2)}, u32[]{:S(2)}) async-start(bf16[8,4,4,2048]{3,2,1,0:T(4,128)(2,1)} %select_select_fusion), calls=%async_computation | async-start | bytes 1048576 | tf_op jit(solution)/shard_map/all_to_all | solution.py:181
  31.0 4.3 %collective-permute-start = (bf16[1,4,4,2048]{3,2,1,0:T(4,128)(2,1)S(1)}, bf16[1,4,4,2048]{3,2,1,0:T(4,128)(2,1)S(1)}, u32[]{:S(2)}, u32[]{:S(2)}) collective-permute-start(bf16[1,4,4,2048]{3,2,1,0:T(4,128)(2,1)S(1)} %bitcast.140), channel_id=1, source_target_pairs={{0,16},{8,24},{16,0},{24,8},{1,17},{9,25},{17,1},{25,9},{2,18},{10... | collective-permute-start | bytes 196616 | tf_op jit(solution)/shard_map/ppermute | solution.py:47
  35.5 13.5 %collective-permute-start.1 = (bf16[2,4,4,2048]{3,2,1,0:T(4,128)(2,1)S(1)}, bf16[2,4,4,2048]{3,2,1,0:T(4,128)(2,1)S(1)}, u32[]{:S(2)}, u32[]{:S(2)}) collective-permute-start(bf16[2,4,4,2048]{3,2,1,0:T(4,128)(2,1)S(1)} %pad_maximum_fusion.3), channel_id=1, source_target_pairs={{0,8},{8,0},{16,24},{24,16},{1,9},{9,1},{17,25},{25,17},{2,10},{10... | collective-permute-start | bytes 393224 | tf_op jit(solution)/shard_map/ppermute | solution.py:47
  41.0 8.2 %copy-start.6 = (f32[2048]{0:T(1024)S(1)}, f32[2048]{0:T(1024)}, u32[]{:S(2)}) copy-start(f32[2048]{0:T(1024)} %param.27) | copy-start | bytes 24580
  49.4 4.6 %copy-start.2 = (bf16[512,2048]{1,0:T(8,128)(2,1)S(1)}, bf16[512,2048]{1,0:T(8,128)(2,1)}, u32[]{:S(2)}) copy-start(bf16[512,2048]{1,0:T(8,128)(2,1)} %copy.168) | copy-start | bytes 6291460
  54.9 4.2 %collective-permute-start.2 = (bf16[1,3,16,4,128]{4,2,3,1,0:T(8,128)(2,1)S(1)}, bf16[1,3,16,4,128]{4,2,3,1,0:T(8,128)(2,1)S(1)}, u32[]{:S(2)}, u32[]{:S(2)}) collective-permute-start(bf16[1,3,16,4,128]{4,2,3,1,0:T(8,128)(2,1)S(1)} %maximum_bitcast_fusion), channel_id=1, source_target_pairs={{0,16},{8,24},{16,0},{24,8},{1,17},{9,25},{17,1},{25,9},{2,18},{10... | collective-permute-start | bytes 147464 | tf_op jit(solution)/shard_map/ppermute | solution.py:47
  59.1 4.7 %collective-permute-start.3 = (bf16[2,3,16,4,128]{4,2,3,1,0:T(8,128)(2,1)S(1)}, bf16[2,3,16,4,128]{4,2,3,1,0:T(8,128)(2,1)S(1)}, u32[]{:S(2)}, u32[]{:S(2)}) collective-permute-start(bf16[2,3,16,4,128]{4,2,3,1,0:T(8,128)(2,1)S(1)} %pad_maximum_fusion.7), channel_id=1, source_target_pairs={{0,8},{8,0},{16,24},{24,16},{1,9},{9,1},{17,25},{25,17},{2,10},{10... | collective-permute-start | bytes 294920 | tf_op jit(solution)/shard_map/ppermute | solution.py:47
  69.1 21.4 %copy-start.7 = (f32[2048]{0:T(1024)S(1)}, f32[2048]{0:T(1024)}, u32[]{:S(2)}) copy-start(f32[2048]{0:T(1024)} %param.34) | copy-start | bytes 24580
  69.1 32.1 %copy-start.5 = (s32[4,32,6]{1,0,2:T(4,128)S(1)}, s32[4,32,6]{1,0,2:T(4,128)}, u32[]{:S(2)}) copy-start(s32[4,32,6]{1,0,2:T(4,128)} %param.25) | copy-start | bytes 9220
  70.8 8.4 %all-to-all-start.1 = ((f32[4,1,8320]{2,1,0:T(1,128)}), f32[4,1,8320]{2,1,0:T(1,128)S(1)}, u32[]{:S(2)}, u32[]{:S(2)}) async-start(f32[4,1,8320]{2,1,0:T(1,128)} %copy.149), calls=%async_computation.1 | async-start | bytes 266240 | tf_op jit(solution)/shard_map/all_to_all | solution.py:240
  80.4 22.9 %copy-start.4 = (bf16[2048,64]{0,1:T(8,128)(2,1)S(1)}, bf16[2048,64]{0,1:T(8,128)(2,1)}, u32[]{:S(2)}) copy-start(bf16[2048,64]{0,1:T(8,128)(2,1)} %param.35) | copy-start | bytes 786436
  81.0 4.3 %collective-permute-start.4 = (bf16[1,16,2048]{2,1,0:T(8,128)(2,1)S(1)}, bf16[1,16,2048]{2,1,0:T(8,128)(2,1)S(1)}, u32[]{:S(2)}, u32[]{:S(2)}) collective-permute-start(bf16[1,16,2048]{2,1,0:T(8,128)(2,1)S(1)} %fusion.6), channel_id=1, source_target_pairs={{0,16},{8,24},{16,0},{24,8},{1,17},{9,25},{17,1},{25,9},{2,18},{10... | collective-permute-start | bytes 196616 | tf_op jit(solution)/shard_map/ppermute | solution.py:47
  85.3 5.0 %collective-permute-start.5 = (bf16[2,16,2048]{2,1,0:T(8,128)(2,1)S(1)}, bf16[2,16,2048]{2,1,0:T(8,128)(2,1)S(1)}, u32[]{:S(2)}, u32[]{:S(2)}) collective-permute-start(bf16[2,16,2048]{2,1,0:T(8,128)(2,1)S(1)} %pad_maximum_fusion.4), channel_id=1, source_target_pairs={{0,8},{8,0},{16,24},{24,16},{1,9},{9,1},{17,25},{25,17},{2,10},{10... | collective-permute-start | bytes 393224 | tf_op jit(solution)/shard_map/ppermute | solution.py:47
  90.6 5.2 %collective-permute-start.6 = (bf16[16,2048]{1,0:T(8,128)(2,1)S(1)}, bf16[16,2048]{1,0:T(8,128)(2,1)S(1)}, u32[]{:S(2)}, u32[]{:S(2)}) collective-permute-start(bf16[16,2048]{1,0:T(8,128)(2,1)S(1)} %multiply_convert_fusion), channel_id=1, source_target_pairs={{0,4},{1,5},{2,6},{3,7},{4,0},{5,1},{6,2},{7,3},{8,12},{9,13},{10,... | collective-permute-start | bytes 196616 | tf_op jit(solution)/shard_map/ppermute | solution.py:284
  95.9 5.0 %collective-permute-start.7 = (bf16[32,2048]{1,0:T(8,128)(2,1)S(1)}, bf16[32,2048]{1,0:T(8,128)(2,1)S(1)}, u32[]{:S(2)}, u32[]{:S(2)}) collective-permute-start(bf16[32,2048]{1,0:T(8,128)(2,1)S(1)} %pad_maximum_fusion.5), channel_id=1, source_target_pairs={{0,2},{1,3},{2,0},{3,1},{4,6},{5,7},{6,4},{7,5},{8,10},{9,11},{10,... | collective-permute-start | bytes 393224 | tf_op jit(solution)/shard_map/ppermute | solution.py:284
  100.9 1.6 collective-permute-start.8
  104.5 42.6 %copy-start.8 = (f32[2048]{0:T(1024)S(1)}, f32[2048]{0:T(1024)}, u32[]{:S(2)}) copy-start(f32[2048]{0:T(1024)} %param.42) | copy-start | bytes 24580
  127.8 18.9 %all-to-all-start.2 = ((bf16[32,4,2048]{2,1,0:T(4,128)(2,1)}), bf16[32,4,2048]{2,1,0:T(4,128)(2,1)S(1)}, u32[]{:S(2)}, u32[]{:S(2)}) async-start(bf16[32,4,2048]{2,1,0:T(4,128)(2,1)} %reshape.687), calls=%async_computation.2 | async-start | bytes 1048576 | tf_op jit(solution)/shard_map/all_to_all | solution.py:321
  147.2 4.7 %collective-permute-start.9 = (bf16[4,2048]{1,0:T(4,128)(2,1)S(1)}, bf16[4,2048]{1,0:T(4,128)(2,1)S(1)}, u32[]{:S(2)}, u32[]{:S(2)}) collective-permute-start(bf16[4,2048]{1,0:T(4,128)(2,1)S(1)} %multiply_convert_fusion.2), channel_id=1, source_target_pairs={{0,4},{1,5},{2,6},{3,7},{4,0},{5,1},{6,2},{7,3},{8,12},{9,13},{10,... | collective-permute-start | bytes 49160 | tf_op jit(solution)/shard_map/ppermute | solution.py:336
  151.9 4.0 %collective-permute-start.10 = (bf16[8,2048]{1,0:T(8,128)(2,1)S(1)}, bf16[8,2048]{1,0:T(8,128)(2,1)S(1)}, u32[]{:S(2)}, u32[]{:S(2)}) collective-permute-start(bf16[8,2048]{1,0:T(8,128)(2,1)S(1)} %pad_maximum_fusion.9), channel_id=1, source_target_pairs={{0,2},{1,3},{2,0},{3,1},{4,6},{5,7},{6,4},{7,5},{8,10},{9,11},{10,... | collective-permute-start | bytes 98312 | tf_op jit(solution)/shard_map/ppermute | solution.py:336
  155.9 1.3 collective-permute-start.11
  157.3 26.0 %copy-start.1 = (bf16[512,2048]{1,0:T(8,128)(2,1)S(1)}, bf16[512,2048]{1,0:T(8,128)(2,1)}, u32[]{:S(2)}) copy-start(bf16[512,2048]{1,0:T(8,128)(2,1)} %param.31) | copy-start | bytes 6291460
  (2 other events, 5.2 us)

commit v9 on v7

--- a/solution.py
+++ b/solution.py
@@ -314,12 +314,13 @@
     norms_share = jnp.sqrt(jnp.mean(final_share * final_share, axis=-1))
     head_share = rms_scale(final_share, final_gain).astype(jnp.bfloat16)
     if n_exp == 1 << rounds:
+        head_in = lax.all_gather(head_share, "seq", axis=0, tiled=True)
         for level in reversed(range(rounds)):
             partner = [(i, i ^ (1 << level)) for i in range(n_exp)]
-            head_share = jnp.concatenate([head_share, lax.ppermute(head_share, "exp", partner)], 0)
-        head_in = lax.all_gather(head_share, "seq", axis=0, tiled=False).reshape(tokens, width)
+            head_in = jnp.concatenate([head_in, lax.ppermute(head_in, "exp", partner)], 0)
         local_best = jnp.max(jnp.dot(head_in, w_head, preferred_element_type=jnp.float32), axis=-1)
-        local_best = jnp.take(local_best.reshape(n_seq, n_exp, share), block, axis=1).reshape(tokens)
+        local_best = jnp.take(local_best.reshape(n_exp, n_seq, share), block, axis=0)
+        local_best = jnp.swapaxes(local_best, 0, 1).reshape(tokens)
     else:
         head_in = gather_all(head_share).reshape(tokens, width)
         local_best = jnp.max(jnp.dot(head_in, w_head, preferred_element_type=jnp.float32), axis=-1)

time: 173 us -> 173 us (level)
  waiting for transfers between devices: 42 us -> 44.5 us
  blocking collectives: 45.6 us -> 43.4 us
    ppermute x3, waiting for transfers between devices: 8.81 us -> 11.3 us  [on_device(): lax.ppermute(head_in, 'exp', partner)]
    all_gather x1, blocking collectives: 9.07 us -> 6.95 us  [on_device(): head_in = lax.all_gather(head_share, 'seq', axis=0, tiled=True)]
where the time goes in v9:
time: 173 us; the launch traced here: 172 us
  waiting for transfers between devices  44.5 us (26%)
  blocking collectives  43.4 us (25%)
  local copies, waits for them, and re-layouts  26.8 us (15%)
  Pallas kernels  21.3 us (12%)
  starting transfers between devices  15.4 us (9%)
  matrix products  13.2 us (8%)
  other arithmetic  6.38 us (4%)
    pallas_call x1, Pallas kernels, experts(): pl.pallas_call(lambda *refs: experts_kernel(pieces, *refs), grid=(pieces...  21.3 us
    all_to_all x1, waiting for transfers between devices, on_device(): lax.all_to_all(term_rows.reshape(n_dev, share, width), ('exp', 'seq'), 0,...  16.2 us
    dot_general x3, local copies, waits for them, and re-layouts, project(): jnp.dot(attn_in, weight, preferred_element_type=jnp.float32)  11.9 us
    ppermute x3, waiting for transfers between devices, on_device(): lax.ppermute(head_in, 'exp', partner)  11.3 us
    ppermute x3, waiting for transfers between devices, on_device(): lax.ppermute(moe_group, 'exp', partner)  10.4 us
    all_to_all x1, blocking collectives, on_device(): lax.all_to_all(jnp.broadcast_to(message[None, :], (n_dev, message.shape[0...  9.86 us
    all_gather x1, blocking collectives, on_device(): row_parts = lax.all_gather(row_part, 'seq', axis=0, tiled=False)  9 us
    all_gather x1, blocking collectives, on_device(): lax.all_gather(jnp.stack([query_part, key_part, value_part], axis=0), 'se...  8.97 us
  transfers between devices with their start and end apart: 9, of which 9 were waited for; matrix products, arithmetic and copies ran while one was open for 8% of the time, Pallas kernels for 0%

profile of v9, /device:TPU:0, one launch (start us, length us, event | category | flops | bytes accessed | tf_op | source)
XLA Modules:
  0.0 172.1 jit_solution(7401705689351512854)
XLA Ops:
  2.4 5.1 %gather_fusion = bf16[128,2048]{1,0:T(8,128)(2,1)S(1)} fusion(bf16[1600,2048]{1,0:T(8,128)(2,1)} %param.26, s32[1024]{0:T(1024)S(1)} %pad_clamp_fusion.1), kind=kCustom, calls=%fused_computation | custom fusion | bytes 1049088 | tf_op jit(solution)/shard_map/jit(_take)/gather | solution.py:160
  9.1 6.3 %all-to-all-start = ((bf16[8,4,4,2048]{3,2,1,0:T(4,128)(2,1)}), bf16[8,4,4,2048]{3,2,1,0:T(4,128)(2,1)S(1)}, u32[]{:S(2)}, u32[]{:S(2)}) async-start(bf16[8,4,4,2048]{3,2,1,0:T(4,128)(2,1)} %select_select_fusion), calls=%async_computation | async-start | bytes 1048576 | tf_op jit(solution)/shard_map/all_to_all | solution.py:162
  16.5 4.0 %copy.169 = bf16[512,2048]{1,0:T(8,128)(2,1)} copy(bf16[512,2048]{0,1:T(8,128)(2,1)} %bitcast.134) | data formatting | bytes 4194304 | tf_op jit(solution)/shard_map/dot_general | solution.py:173
  20.5 4.0 %copy.167 = bf16[512,2048]{1,0:T(8,128)(2,1)} copy(bf16[512,2048]{0,1:T(8,128)(2,1)} %bitcast.135) | data formatting | bytes 4194304 | tf_op jit(solution)/shard_map/dot_general | solution.py:173
  24.5 3.9 %copy.168 = bf16[512,2048]{1,0:T(8,128)(2,1)} copy(bf16[512,2048]{0,1:T(8,128)(2,1)} %bitcast.136) | data formatting | bytes 4194304 | tf_op jit(solution)/shard_map/dot_general | solution.py:173
  28.7 2.1 %all-to-all-done = bf16[8,4,4,2048]{3,2,1,0:T(4,128)(2,1)S(1)} async-done(((bf16[8,4,4,2048]{3,2,1,0:T(4,128)(2,1)}), bf16[8,4,4,2048]{3,2,1,0:T(4,128)(2,1)S(1)}, u32[]{:S(2)}, u32[]{:S(2)}) %all-to-all-start) | async-done | bytes 524320 | tf_op jit(solution)/shard_map/all_to_all | solution.py:162
  31.1 9.0 %all-gather = bf16[16,4,2048]{2,1,0:T(4,128)(2,1)S(1)} all-gather(bf16[4,4,2048]{2,1,0:T(4,128)(2,1)S(1)} %reduce_sum.137), channel_id=2, replica_groups=mesh['seq'=4,'exp'=8] {'seq'}, dimensions={0}, use_global_device_ids=true | all-gather | bytes 327680 | tf_op jit(solution)/shard_map/all_gather | solution.py:164
  40.5 2.4 %convolution_convert_fusion.1 = bf16[16,4,128]{2,0,1:T(8,128)(2,1)S(1)} fusion(bf16[16,2048,1]{1,0,2:T(8,128)(2,1)S(1)} %reshape.676, bf16[4,128,2048]{2,1,0:T(8,128)(2,1)} %bitcast.132), kind=kOutput, calls=%fused_computation.24 | convolution fusion | flops 33562624 | bytes 2179072 | tf_op jit(solution)/shard_map/dot_general | solution.py:173
  42.9 2.3 %fusion.57 = f32[16,4,128]{2,0,1:T(8,128)S(1)} fusion(bf16[16,2048,1]{1,0,2:T(8,128)(2,1)S(1)} %reshape.676, bf16[4,128,2048]{2,1,0:T(8,128)(2,1)} %bitcast.131), kind=kOutput, calls=%fused_computation.131 | convolution fusion | flops 33554432 | bytes 2195456 | tf_op jit(solution)/shard_map/dot_general | solution.py:173
  46.1 9.0 %all-gather.1 = bf16[12,16,4,128]{3,1,2,0:T(8,128)(2,1)S(1)} all-gather(bf16[3,16,4,128]{3,1,2,0:T(8,128)(2,1)S(1)} %pad_maximum_fusion.5), channel_id=3, replica_groups=mesh['seq'=4,'exp'=8] {'seq'}, dimensions={0}, use_global_device_ids=true | all-gather | bytes 245760 | tf_op jit(solution)/shard_map/all_gather | solution.py:180
  59.1 3.3 %all-to-all-start.1 = ((f32[4,1,8320]{2,1,0:T(1,128)}), f32[4,1,8320]{2,1,0:T(1,128)S(1)}, u32[]{:S(2)}, u32[]{:S(2)}) async-start(f32[4,1,8320]{2,1,0:T(1,128)} %copy.150), calls=%async_computation.1 | async-start | bytes 266240 | tf_op jit(solution)/shard_map/all_to_all | solution.py:223
  63.0 4.4 %all-to-all-done.1 = f32[4,1,8320]{2,1,0:T(1,128)S(1)} async-done(((f32[4,1,8320]{2,1,0:T(1,128)}), f32[4,1,8320]{2,1,0:T(1,128)S(1)}, u32[]{:S(2)}, u32[]{:S(2)}) %all-to-all-start.1) | async-done | bytes 133152 | tf_op jit(solution)/shard_map/all_to_all | solution.py:223
  69.3 8.6 %all-gather.2 = bf16[64,2048]{1,0:T(8,128)(2,1)S(1)} all-gather(bf16[16,2048]{1,0:T(8,128)(2,1)S(1)} %convolution_convert_fusion), channel_id=4, replica_groups=mesh['seq'=4,'exp'=8] {'seq'}, dimensions={0}, use_global_device_ids=true | all-gather | bytes 327680 | tf_op jit(solution)/shard_map/all_gather | solution.py:257
  78.9 4.5 %collective-permute-done = bf16[16,2048]{1,0:T(8,128)(2,1)S(1)} collective-permute-done((bf16[16,2048]{1,0:T(8,128)(2,1)S(1)}, bf16[16,2048]{1,0:T(8,128)(2,1)S(1)}, u32[]{:S(2)}, u32[]{:S(2)}) %collective-permute-start) | collective-permute-done | bytes 65568 | tf_op jit(solution)/shard_map/ppermute | solution.py:267
  83.5 4.9 %collective-permute-done.1 = bf16[32,2048]{1,0:T(8,128)(2,1)S(1)} collective-permute-done((bf16[32,2048]{1,0:T(8,128)(2,1)S(1)}, bf16[32,2048]{1,0:T(8,128)(2,1)S(1)}, u32[]{:S(2)}, u32[]{:S(2)}) %collective-permute-start.1) | collective-permute-done | bytes 131104 | tf_op jit(solution)/shard_map/ppermute | solution.py:267
  92.0 21.3 %shard_map.221 = bf16[128,2048]{1,0:T(8,128)(2,1)} custom-call(bf16[128,2048]{1,0:T(8,128)(2,1)} %copy-done.3, f32[128,128]{1,0:T(8,128)} %pad.4.refs_1_, bf16[8,352,2048]{2,1,0:T(8,128)(2,1)} %bitcast.129, bf16[8,352,2048]{2,1,0:T(8,128)(2,1)} %bitcast.130, bf16[8,352,2048]{2,1,0:T(8,128)(2,1)} %refs_4_.1, bf16[352,2048]{1,0:T(8,128)(2,1)} %bitcast.138, ...), custom_call_target="tpu_custom_call" | custom-call | flops 4982833152 | bytes 39976960 | tf_op jit(solution)/shard_map/pallas_call | solution.py:84
  113.3 2.0 %reshape.640 = bf16[32,4,2048]{2,1,0:T(4,128)(2,1)} reshape(bf16[128,2048]{1,0:T(8,128)(2,1)} %shard_map.221) | data formatting | bytes 1048576 | tf_op jit(solution)/shard_map/reshape | solution.py:305
  115.4 3.6 %all-to-all-start.2 = ((bf16[32,4,2048]{2,1,0:T(4,128)(2,1)}), bf16[32,4,2048]{2,1,0:T(4,128)(2,1)S(1)}, u32[]{:S(2)}, u32[]{:S(2)}) async-start(bf16[32,4,2048]{2,1,0:T(4,128)(2,1)} %reshape.640), calls=%async_computation.2 | async-start | bytes 1048576 | tf_op jit(solution)/shard_map/all_to_all | solution.py:304
  118.9 16.2 %all-to-all-done.2 = bf16[32,4,2048]{2,1,0:T(4,128)(2,1)S(1)} async-done(((bf16[32,4,2048]{2,1,0:T(4,128)(2,1)}), bf16[32,4,2048]{2,1,0:T(4,128)(2,1)S(1)}, u32[]{:S(2)}, u32[]{:S(2)}) %all-to-all-start.2) | async-done | bytes 524320 | tf_op jit(solution)/shard_map/all_to_all | solution.py:304
  135.6 7.0 %all-gather.3 = bf16[4,4,2048]{2,1,0:T(4,128)(2,1)S(1)} all-gather(bf16[1,4,2048]{2,1,0:T(4,128)(2,1)S(1)} %fusion.38), channel_id=1, replica_groups=mesh['seq'=4,'exp'=8] {'seq'}, dimensions={0}, use_global_device_ids=true | all-gather | bytes 81920 | tf_op jit(solution)/shard_map/all_gather | solution.py:317
  143.6 4.9 %collective-permute-done.3 = bf16[16,2048]{1,0:T(8,128)(2,1)S(1)} collective-permute-done((bf16[16,2048]{1,0:T(8,128)(2,1)S(1)}, bf16[16,2048]{1,0:T(8,128)(2,1)S(1)}, u32[]{:S(2)}, u32[]{:S(2)}) %collective-permute-start.3) | collective-permute-done | bytes 65568 | tf_op jit(solution)/shard_map/ppermute | solution.py:320
  148.8 4.8 %collective-permute-done.4 = bf16[32,2048]{1,0:T(8,128)(2,1)S(1)} collective-permute-done((bf16[32,2048]{1,0:T(8,128)(2,1)S(1)}, bf16[32,2048]{1,0:T(8,128)(2,1)S(1)}, u32[]{:S(2)}, u32[]{:S(2)}) %collective-permute-start.4) | collective-permute-done | bytes 131104 | tf_op jit(solution)/shard_map/ppermute | solution.py:320
  155.2 4.7 %convolution_reduce_fusion = f32[128]{0:T(128)S(1)} fusion(bf16[2048,1600]{0,1:T(8,128)(2,1)} %param.43, bf16[64,2048]{1,0:T(8,128)(2,1)S(1)} %collective-permute-done.5, bf16[32,2048]{1,0:T(8,128)(2,1)S(1)} %collective-permute-done.4, bf16[16,2048]{1,0:T(8,128)(2,1)S(1)} %collective-permute-done.3, bf16[16,2048]{1,0:T(8,128)(2,1)S(1)} %reshape.675), kind=kOutput, calls=%fused_computation.10 | convolution fusion | flops 841162624 | bytes 7078400 | tf_op jit(solution)/shard_map/dot_general | solution.py:321
  160.9 9.9 %all_to_all.31 = f32[32,1,132]{2,1,0:T(1,128)S(1)} all-to-all(f32[32,1,132]{2,1,0:T(1,128)S(1)} %broadcast_in_dim.175), channel_id=1, replica_groups=mesh['seq'=4,'exp'=8] {'seq','exp'}, dimensions={0} | all-to-all | bytes 33792 | tf_op jit(solution)/shard_map/all_to_all | solution.py:328
  (150 shorter events, 22.6 us)
Async XLA Ops:
  0.6 68.2 %copy-start = (bf16[512,2048]{1,0:T(8,128)(2,1)S(1)}, bf16[512,2048]{1,0:T(8,128)(2,1)}, u32[]{:S(2)}) copy-start(bf16[512,2048]{1,0:T(8,128)(2,1)} %param.31) | copy-start | bytes 6291460
  0.6 15.8 %copy-start.11 = (s32[32]{0:T(128)S(1)}, s32[32]{0:T(128)}, u32[]{:S(2)}) copy-start(s32[32]{0:T(128)} %param.23) | copy-start | bytes 388
  9.1 21.7 %all-to-all-start = ((bf16[8,4,4,2048]{3,2,1,0:T(4,128)(2,1)}), bf16[8,4,4,2048]{3,2,1,0:T(4,128)(2,1)S(1)}, u32[]{:S(2)}, u32[]{:S(2)}) async-start(bf16[8,4,4,2048]{3,2,1,0:T(4,128)(2,1)} %select_select_fusion), calls=%async_computation | async-start | bytes 1048576 | tf_op jit(solution)/shard_map/all_to_all | solution.py:162
  20.5 19.9 %copy-start.6 = (f32[2048]{0:T(1024)S(1)}, f32[2048]{0:T(1024)}, u32[]{:S(2)}) copy-start(f32[2048]{0:T(1024)} %param.27) | copy-start | bytes 24580
  40.5 4.7 %copy-start.2 = (bf16[512,2048]{1,0:T(8,128)(2,1)S(1)}, bf16[512,2048]{1,0:T(8,128)(2,1)}, u32[]{:S(2)}) copy-start(bf16[512,2048]{1,0:T(8,128)(2,1)} %copy.168) | copy-start | bytes 6291460
  40.5 14.6 %copy-start.9 = (bf16[4,256,2048]{2,1,0:T(8,128)(2,1)S(1)}, bf16[4,256,2048]{2,1,0:T(8,128)(2,1)}, u32[]{:S(2)}) copy-start(bf16[4,256,2048]{2,1,0:T(8,128)(2,1)} %param.32) | copy-start | bytes 12582916
  45.2 11.5 %copy-start.10 = (bf16[4,256,2048]{2,1,0:T(8,128)(2,1)S(1)}, bf16[4,256,2048]{2,1,0:T(8,128)(2,1)}, u32[]{:S(2)}) copy-start(bf16[4,256,2048]{2,1,0:T(8,128)(2,1)} %param.33) | copy-start | bytes 12582916
  57.5 20.6 %copy-start.7 = (f32[2048]{0:T(1024)S(1)}, f32[2048]{0:T(1024)}, u32[]{:S(2)}) copy-start(f32[2048]{0:T(1024)} %param.34) | copy-start | bytes 24580
  57.5 31.2 %copy-start.5 = (s32[4,32,6]{1,0,2:T(4,128)S(1)}, s32[4,32,6]{1,0,2:T(4,128)}, u32[]{:S(2)}) copy-start(s32[4,32,6]{1,0,2:T(4,128)} %param.25) | copy-start | bytes 9220
  59.1 8.3 %all-to-all-start.1 = ((f32[4,1,8320]{2,1,0:T(1,128)}), f32[4,1,8320]{2,1,0:T(1,128)S(1)}, u32[]{:S(2)}, u32[]{:S(2)}) async-start(f32[4,1,8320]{2,1,0:T(1,128)} %copy.150), calls=%async_computation.1 | async-start | bytes 266240 | tf_op jit(solution)/shard_map/all_to_all | solution.py:223
  68.6 22.2 %copy-start.4 = (bf16[2048,64]{0,1:T(8,128)(2,1)S(1)}, bf16[2048,64]{0,1:T(8,128)(2,1)}, u32[]{:S(2)}) copy-start(bf16[2048,64]{0,1:T(8,128)(2,1)} %param.35) | copy-start | bytes 786436
  78.1 5.2 %collective-permute-start = (bf16[16,2048]{1,0:T(8,128)(2,1)S(1)}, bf16[16,2048]{1,0:T(8,128)(2,1)S(1)}, u32[]{:S(2)}, u32[]{:S(2)}) collective-permute-start(bf16[16,2048]{1,0:T(8,128)(2,1)S(1)} %multiply_convert_fusion), channel_id=1, source_target_pairs={{0,4},{1,5},{2,6},{3,7},{4,0},{5,1},{6,2},{7,3},{8,12},{9,13},{10,... | collective-permute-start | bytes 196616 | tf_op jit(solution)/shard_map/ppermute | solution.py:267
  83.4 5.0 %collective-permute-start.1 = (bf16[32,2048]{1,0:T(8,128)(2,1)S(1)}, bf16[32,2048]{1,0:T(8,128)(2,1)S(1)}, u32[]{:S(2)}, u32[]{:S(2)}) collective-permute-start(bf16[32,2048]{1,0:T(8,128)(2,1)S(1)} %pad_maximum_fusion.3), channel_id=1, source_target_pairs={{0,2},{1,3},{2,0},{3,1},{4,6},{5,7},{6,4},{7,5},{8,10},{9,11},{10,... | collective-permute-start | bytes 393224 | tf_op jit(solution)/shard_map/ppermute | solution.py:267
  88.4 1.6 collective-permute-start.2
  90.8 1.2 copy-start.3
  92.0 43.5 %copy-start.8 = (f32[2048]{0:T(1024)S(1)}, f32[2048]{0:T(1024)}, u32[]{:S(2)}) copy-start(f32[2048]{0:T(1024)} %param.42) | copy-start | bytes 24580
  115.4 19.8 %all-to-all-start.2 = ((bf16[32,4,2048]{2,1,0:T(4,128)(2,1)}), bf16[32,4,2048]{2,1,0:T(4,128)(2,1)S(1)}, u32[]{:S(2)}, u32[]{:S(2)}) async-start(bf16[32,4,2048]{2,1,0:T(4,128)(2,1)} %reshape.640), calls=%async_computation.2 | async-start | bytes 1048576 | tf_op jit(solution)/shard_map/all_to_all | solution.py:304
  142.6 5.9 %collective-permute-start.3 = (bf16[16,2048]{1,0:T(8,128)(2,1)S(1)}, bf16[16,2048]{1,0:T(8,128)(2,1)S(1)}, u32[]{:S(2)}, u32[]{:S(2)}) collective-permute-start(bf16[16,2048]{1,0:T(8,128)(2,1)S(1)} %reshape.675), channel_id=1, source_target_pairs={{0,4},{1,5},{2,6},{3,7},{4,0},{5,1},{6,2},{7,3},{8,12},{9,13},{10,... | collective-permute-start | bytes 196616 | tf_op jit(solution)/shard_map/ppermute | solution.py:320
  148.6 5.0 %collective-permute-start.4 = (bf16[32,2048]{1,0:T(8,128)(2,1)S(1)}, bf16[32,2048]{1,0:T(8,128)(2,1)S(1)}, u32[]{:S(2)}, u32[]{:S(2)}) collective-permute-start(bf16[32,2048]{1,0:T(8,128)(2,1)S(1)} %pad_maximum_fusion.4), channel_id=1, source_target_pairs={{0,2},{1,3},{2,0},{3,1},{4,6},{5,7},{6,4},{7,5},{8,10},{9,11},{10,... | collective-permute-start | bytes 393224 | tf_op jit(solution)/shard_map/ppermute | solution.py:320
  153.6 18.5 %copy-start.1 = (bf16[512,2048]{1,0:T(8,128)(2,1)S(1)}, bf16[512,2048]{1,0:T(8,128)(2,1)}, u32[]{:S(2)}) copy-start(bf16[512,2048]{1,0:T(8,128)(2,1)} %param.31) | copy-start | bytes 6291460
  153.6 1.6 collective-permute-start.5
